TPU v7x, 128 devices: a whole 4x4x4 slice. The times are simulated.
128 devices in a mesh: outer: 16 (over z, x), inner: 8 (over y, core).
Axes of the slice: x: 4, y: 4, z: 4, core: 2. Of those that a mesh axis runs over, the one named last changes fastest.
Arguments:
- features: bfloat16 [4194304, 64], P(('outer', 'inner')), may hold values from -6 to 6
- block_offset: int32 [32768], P(('outer', 'inner')), may hold values from 0 to 7
- parent_entry: int32 [4194304], P(('outer', 'inner')), may hold values from 0 to 8191, as said below
- owner_cell: int32 [128, 8192], P(('outer', 'inner')), may hold values from 0 to 4096, as said below
- w_down: bfloat16 [8, 64, 128], replicated, may hold values from -0.25 to 0.25
- b_down: float32 [128], replicated, may hold values from -3 to 3
- w_up: bfloat16 [8, 128, 64], replicated, may hold values from -0.5 to 0.5
Outputs:
- refined: bfloat16 [4194304, 64], P(('outer', 'inner'))
Inputs may be any that keep to these rules, and one draw needn't show every extreme that they name: `parent_entry`: In each group the first c slots are used (1 <= c <= 512), the rest empty; group 7 and one more group have all 512 slots used on every device. A voxel names a used entry of its own device; all voxels of one brick of 128 name entries of one aligned window of 128 entries (entries k * 128 to k * 128 + 127), lying in one group or among the device's own entries, and every neighbour group is named by some brick of every device. owner_cell[d, e] for e < 4096 is the cell of d's own entry e; for e >= 4096 it is the cell named by that entry of the device at d's position minus the step of group (e - 4096) // 512, or 4096 where that slot is empty. The used entries of one aligned window of 128 entries name cells of one aligned window of 128 cells.
All inputs are finite; a program needn't handle non-finite values.
Results may differ from a plain program's by a relative error of at most 0.017.
Values may be sent and summed in bfloat16 or wider, within the bound.
No kernel may reach another device: no remote copies, remote signals or barrier semaphores. Data moves between devices by JAX's collectives and lax.ppermute only.
A program may use at most 128 MiB of HBM per device.

v0:
```python
import jax
import jax.numpy as jnp
from jax import lax
from jax.experimental import pallas as pl
from jax.experimental.pallas import tpu as pltpu
from jax.sharding import PartitionSpec as P

BLK = 128
C_DEV = 4096
SELF_CAP = 4096
WIN = 128
BRICKS_PER_STEP = 32

step_table = ((-1, -1), (-1, 0), (-1, 1), (0, -1), (0, 1), (1, -1), (1, 0), (1, 1))

NT = (((1,), (1,)), ((), ()))
TN = (((0,), (0,)), ((), ()))


def split_parts(data):
    high = data.astype(jnp.bfloat16)
    low = (data - high.astype(jnp.float32)).astype(jnp.bfloat16)
    return high, low


def one_hot_rows(index_row):
    span = lax.broadcasted_iota(jnp.int32, (WIN, index_row.shape[1]), 0)
    return (span == index_row).astype(jnp.bfloat16)


def down_kernel(win_ref, off_ref, xt_ref, e_ref, w_ref, *refs):
    n_groups = len(step_table)
    outs = refs[: 1 + n_groups]
    acc = refs[1 + n_groups]
    step = pl.program_id(0)
    per_step = e_ref.shape[0]

    @pl.when(step == 0)
    def _():
        acc[...] = jnp.zeros_like(acc)

    def body(j, carry):
        brick = step * per_step + j
        window = win_ref[brick]
        offset = off_ref[brick]
        inside = jnp.bitwise_and(e_ref[pl.ds(j, 1), :], WIN - 1)
        pick = one_hot_rows(inside)
        cols = pl.ds(pl.multiple_of(j * BLK, BLK), BLK)
        summed = lax.dot_general(pick, xt_ref[:, cols], NT, preferred_element_type=jnp.float32)
        high, low = split_parts(summed)
        weights = w_ref[offset]
        part = jnp.dot(high, weights, preferred_element_type=jnp.float32) + jnp.dot(
            low, weights, preferred_element_type=jnp.float32
        )
        rows = pl.ds(pl.multiple_of(window * WIN, WIN), WIN)
        acc[rows, :] += part
        return carry

    lax.fori_loop(0, per_step, body, 0)

    @pl.when(step == pl.num_programs(0) - 1)
    def _():
        outs[0][...] = acc[0:SELF_CAP, :].astype(jnp.bfloat16)
        cap = outs[1].shape[0]
        for g in range(n_groups):
            start = SELF_CAP + g * cap
            outs[1 + g][...] = acc[start : start + cap, :].astype(jnp.bfloat16)


def coarse_kernel(cw_ref, cells_ref, bias_ref, *refs):
    n_groups = len(step_table)
    sources = refs[: 1 + n_groups]
    outs = refs[1 + n_groups : 2 + 2 * n_groups]
    acc, coarse = refs[2 + 2 * n_groups :]
    cell_windows = acc.shape[0] // WIN
    acc[...] = jnp.zeros_like(acc)

    def pick_of(w):
        window = jnp.minimum(cw_ref[w], cell_windows - 1)
        cells = cells_ref[pl.ds(w, 1), :]
        inside = jnp.where(cells < C_DEV, cells - window * WIN, -1)
        rows = pl.ds(pl.multiple_of(window * WIN, WIN), WIN)
        return one_hot_rows(inside), rows

    base = 0
    for src in sources:
        count = src.shape[0] // WIN

        def gather_body(j, carry, src=src, base=base):
            pick, rows = pick_of(base + j)
            entries = src[pl.ds(pl.multiple_of(j * WIN, WIN), WIN), :]
            acc[rows, :] += jnp.dot(pick, entries, preferred_element_type=jnp.float32)
            return carry

        lax.fori_loop(0, count, gather_body, 0)
        base += count

    coarse[...] = jnp.maximum(acc[...] + bias_ref[...], 0.0).astype(jnp.bfloat16)

    base = 0
    for out in outs:
        count = out.shape[0] // WIN

        def scatter_body(j, carry, out=out, base=base):
            pick, rows = pick_of(base + j)
            chosen = lax.dot_general(pick, coarse[rows, :], TN, preferred_element_type=jnp.float32)
            out[pl.ds(pl.multiple_of(j * WIN, WIN), WIN), :] = chosen.astype(jnp.bfloat16)
            return carry

        lax.fori_loop(0, count, scatter_body, 0)
        base += count


def up_kernel(win_ref, off_ref, xt_ref, e_ref, wt_ref, *refs):
    n_groups = len(step_table)
    sources = refs[: 1 + n_groups]
    out_ref = refs[1 + n_groups]
    stack, sems = refs[2 + n_groups :]
    step = pl.program_id(0)
    per_step = e_ref.shape[0]

    @pl.when(step == 0)
    def _():
        copies = []
        start = 0
        for index, src in enumerate(sources):
            size = src.shape[0]
            copy = pltpu.make_async_copy(src, stack.at[pl.ds(start, size)], sems.at[index])
            copy.start()
            copies.append(copy)
            start += size
        for copy in copies:
            copy.wait()

    def body(j, carry):
        brick = step * per_step + j
        window = win_ref[brick]
        offset = off_ref[brick]
        inside = jnp.bitwise_and(e_ref[pl.ds(j, 1), :], WIN - 1)
        pick = one_hot_rows(inside)
        parents = stack[pl.ds(pl.multiple_of(window * WIN, WIN), WIN), :]
        lifted_t = lax.dot_general(wt_ref[offset], parents, NT, preferred_element_type=jnp.float32)
        high, low = split_parts(lifted_t)
        lifted = jnp.dot(high, pick, preferred_element_type=jnp.float32) + jnp.dot(
            low, pick, preferred_element_type=jnp.float32
        )
        cols = pl.ds(pl.multiple_of(j * BLK, BLK), BLK)
        out_ref[:, cols] = (xt_ref[:, cols].astype(jnp.float32) + lifted).astype(out_ref.dtype)
        return carry

    lax.fori_loop(0, per_step, body, 0)


def group_route(g, sign):
    n_outer = lax.axis_size("outer")
    n_inner = lax.axis_size("inner")
    a, b = step_table[g]
    route = []
    for s in range(n_outer * n_inner):
        row, col = divmod(s, n_inner)
        owner = ((row + a) % n_outer) * n_inner + (col + b) % n_inner
        route.append((s, owner) if sign > 0 else (owner, s))
    return route


def local(features, block_offset, parent_entry, owner_cell, w_down, b_down, w_up):
    n_groups = len(step_table)
    fine_rows, in_width = features.shape
    out_width = w_down.shape[2]
    entries = owner_cell.shape[1]
    cap = (entries - SELF_CAP) // n_groups
    blocks = fine_rows // BLK
    steps = blocks // BRICKS_PER_STEP

    xt = features.T
    entry_rows = parent_entry.reshape(blocks, BLK)
    brick_window = entry_rows[:, 0] // WIN
    cells = owner_cell.reshape(entries // WIN, WIN)
    cell_window = jnp.min(cells, axis=1) // WIN
    w_up_t = jnp.swapaxes(w_up, 1, 2)

    part_shapes = [jax.ShapeDtypeStruct((SELF_CAP, out_width), jnp.bfloat16)] + [
        jax.ShapeDtypeStruct((cap, out_width), jnp.bfloat16)
    ] * n_groups
    whole = lambda shape: pl.BlockSpec(shape, lambda *idx: (0,) * len(shape))

    down = pl.pallas_call(
        down_kernel,
        out_shape=part_shapes,
        grid_spec=pltpu.PrefetchScalarGridSpec(
            num_scalar_prefetch=2,
            grid=(steps,),
            in_specs=[
                pl.BlockSpec((in_width, BRICKS_PER_STEP * BLK), lambda i, *_: (0, i)),
                pl.BlockSpec((BRICKS_PER_STEP, BLK), lambda i, *_: (i, 0)),
                whole(w_down.shape),
            ],
            out_specs=[whole(s.shape) for s in part_shapes],
            scratch_shapes=[pltpu.VMEM((entries, out_width), jnp.float32)],
        ),
        compiler_params=pltpu.CompilerParams(dimension_semantics=("arbitrary",)),
        cost_estimate=pl.CostEstimate(
            flops=6 * fine_rows * in_width * out_width,
            transcendentals=0,
            bytes_accessed=fine_rows * (in_width * 2 + 4) + entries * out_width * 2,
        ),
    )
    parts = down(brick_window, block_offset, xt, entry_rows, w_down)

    arrived = [
        lax.ppermute(parts[1 + g], ("outer", "inner"), group_route(g, 1)) for g in range(n_groups)
    ]

    coarse = pl.pallas_call(
        coarse_kernel,
        out_shape=part_shapes,
        grid_spec=pltpu.PrefetchScalarGridSpec(
            num_scalar_prefetch=1,
            grid=(1,),
            in_specs=[whole(cells.shape), whole((1, out_width))]
            + [whole(s.shape) for s in part_shapes],
            out_specs=[whole(s.shape) for s in part_shapes],
            scratch_shapes=[
                pltpu.VMEM((C_DEV, out_width), jnp.float32),
                pltpu.VMEM((C_DEV, out_width), jnp.bfloat16),
            ],
        ),
        cost_estimate=pl.CostEstimate(
            flops=4 * entries * WIN * out_width,
            transcendentals=0,
            bytes_accessed=4 * entries * out_width,
        ),
    )
    answers = coarse(cell_window, cells, b_down.reshape(1, out_width), parts[0], *arrived)

    returned = [
        lax.ppermute(answers[1 + g], ("outer", "inner"), group_route(g, -1)) for g in range(n_groups)
    ]

    up = pl.pallas_call(
        up_kernel,
        out_shape=jax.ShapeDtypeStruct((in_width, fine_rows), features.dtype),
        grid_spec=pltpu.PrefetchScalarGridSpec(
            num_scalar_prefetch=2,
            grid=(steps,),
            in_specs=[
                pl.BlockSpec((in_width, BRICKS_PER_STEP * BLK), lambda i, *_: (0, i)),
                pl.BlockSpec((BRICKS_PER_STEP, BLK), lambda i, *_: (i, 0)),
                whole(w_up_t.shape),
            ]
            + [pl.BlockSpec(memory_space=pl.ANY)] * (1 + n_groups),
            out_specs=pl.BlockSpec((in_width, BRICKS_PER_STEP * BLK), lambda i, *_: (0, i)),
            scratch_shapes=[
                pltpu.VMEM((entries, out_width), jnp.bfloat16),
                pltpu.SemaphoreType.DMA((1 + n_groups,)),
            ],
        ),
        compiler_params=pltpu.CompilerParams(dimension_semantics=("arbitrary",)),
        cost_estimate=pl.CostEstimate(
            flops=6 * fine_rows * in_width * out_width,
            transcendentals=0,
            bytes_accessed=fine_rows * (in_width * 4 + 4) + entries * out_width * 2,
        ),
    )
    out_t = up(brick_window, block_offset, xt, entry_rows, w_up_t, answers[0], *returned)
    return out_t.T


def solution(mesh):
    in_specs = (
        P(("outer", "inner"), None),
        P(("outer", "inner")),
        P(("outer", "inner")),
        P(("outer", "inner"), None),
        P(),
        P(),
        P(),
    )
    out_specs = P(("outer", "inner"), None)
    return jax.shard_map(local, mesh=mesh, in_specs=in_specs, out_specs=out_specs, check_vma=False)
```

profile of v0, /device:TPU:24, one launch (start us, length us, event | category | flops | bytes accessed | tf_op | source)
XLA Modules:
  0.0 237.2 jit_solution(17470055083679807385)
XLA Ops:
  0.0 0.0 copy-start.8
  0.0 1.0 slice_reduce_fusion
  1.0 0.6 and_select_fusion.1.win_ref
  1.6 77.9 %shard_map.73 = (bf16[4096,128]{1,0:T(8,128)(2,1)}, bf16[512,128]{1,0:T(8,128)(2,1)}, bf16[512,128]{1,0:T(8,128)(2,1)}, bf16[512,128]{1,0:T(8,128)(2,1)}, bf16[5...) custom-call(s32[256]{0:T(256)} %and_select_fusion.1.win_ref, ...), custom_call_target="tpu_custom_call" | custom-call | flops 1610612736 | bytes 6422528 | tf_op jit(solution)/shard_map/pallas_call | solution.py:208
  79.6 5.9 %collective-permute-start = (bf16[512,128]{1,0:T(8,128)(2,1)}, bf16[512,128]{1,0:T(8,128)(2,1)S(1)}, u32[]{:S(2)}, u32[]{:S(2)}) collective-permute-start(bf16[512,128]{1,0:T(8,128)(2,1)} %get-tuple-element.24), channel_id=1, source_target_pairs={{0,127},{1,120},{2,121},{3,122},{4,123},{5,124},{6,125},{7,126},{8... | collective-permute-start | bytes 393224 | tf_op jit(solution)/shard_map/ppermute | solution.py:211
  85.4 0.8 collective-permute-start.1
  86.3 0.4 collective-permute-start.2
  86.6 1.4 collective-permute-start.3
  88.0 0.9 collective-permute-start.4
  88.8 0.0 copy-done.8
  88.8 0.1 reduce_min.9
  89.0 0.7 collective-permute-done.refs_1_
  89.6 0.0 copy-start.9
  89.6 1.2 collective-permute-start.5
  90.9 1.7 collective-permute-done.1.refs_2_
  92.5 0.0 copy-start.10
  92.5 0.0 collective-permute-start.6
  92.5 2.6 %collective-permute-done.2.refs_3_ = bf16[512,128]{1,0:T(8,128)(2,1)S(1)} collective-permute-done((bf16[512,128]{1,0:T(8,128)(2,1)}, bf16[512,128]{1,0:T(8,128)(2,1)S(1)}, u32[]{:S(2)}, u32[]{:S(2)}) %collective-permute-start.2) | collective-permute-done | bytes 131104 | tf_op jit(solution)/shard_map/ppermute | solution.py:211
  95.1 0.0 copy-start.11
  95.1 0.0 collective-permute-start.7
  95.1 0.6 and_select_fusion.cw_ref
  95.8 0.0 collective-permute-done.3.refs_4_
  95.8 0.0 copy-start.12
  95.8 0.0 collective-permute-done.4.refs_5_
  95.8 0.0 copy-start.13
  95.8 4.8 %collective-permute-done.5.refs_6_ = bf16[512,128]{1,0:T(8,128)(2,1)S(1)} collective-permute-done((bf16[512,128]{1,0:T(8,128)(2,1)}, bf16[512,128]{1,0:T(8,128)(2,1)S(1)}, u32[]{:S(2)}, u32[]{:S(2)}) %collective-permute-start.5) | collective-permute-done | bytes 131104 | tf_op jit(solution)/shard_map/ppermute | solution.py:211
  100.6 4.6 %collective-permute-done.6.refs_7_ = bf16[512,128]{1,0:T(8,128)(2,1)S(1)} collective-permute-done((bf16[512,128]{1,0:T(8,128)(2,1)}, bf16[512,128]{1,0:T(8,128)(2,1)S(1)}, u32[]{:S(2)}, u32[]{:S(2)}) %collective-permute-start.6) | collective-permute-done | bytes 131104 | tf_op jit(solution)/shard_map/ppermute | solution.py:211
  105.2 2.2 collective-permute-done.7.refs_8_
  107.4 0.0 copy-done.9
  107.4 0.0 copy-done.10
  107.4 0.0 copy-done.11
  107.4 0.0 copy-done.12
  107.4 0.0 copy-done.13
  107.4 0.0 copy-done.14
  107.4 0.0 copy-done.15
  107.4 0.6 copy-done.16
  108.0 24.9 %shard_map.74 = (bf16[4096,128]{1,0:T(8,128)(2,1)}, bf16[512,128]{1,0:T(8,128)(2,1)}, bf16[512,128]{1,0:T(8,128)(2,1)}, bf16[512,128]{1,0:T(8,128)(2,1)}, bf16[5...) custom-call(s32[64]{0:T(128)} %and_select_fusion.cw_ref, ...), custom_call_target="tpu_custom_call" | custom-call | flops 536870912 | bytes 4194304 | tf_op jit(solution)/shard_map/pallas_call | solution.py:234
  133.0 0.0 collective-permute-start.8
  133.0 0.1 collective-permute-start.9
  133.1 0.1 collective-permute-start.10
  133.1 0.1 collective-permute-start.11
  133.2 1.7 collective-permute-start.12
  134.9 8.4 %collective-permute-done.8.refs_1_ = bf16[512,128]{1,0:T(8,128)(2,1)S(1)} collective-permute-done((bf16[512,128]{1,0:T(8,128)(2,1)}, bf16[512,128]{1,0:T(8,128)(2,1)S(1)}, u32[]{:S(2)}, u32[]{:S(2)}) %collective-permute-start.8) | collective-permute-done | bytes 131104 | tf_op jit(solution)/shard_map/ppermute | solution.py:237
  143.4 0.0 collective-permute-start.13
  143.4 1.6 collective-permute-done.9.refs_2_
  144.9 0.0 collective-permute-start.14
  144.9 3.5 %collective-permute-done.10.refs_3_ = bf16[512,128]{1,0:T(8,128)(2,1)S(1)} collective-permute-done((bf16[512,128]{1,0:T(8,128)(2,1)}, bf16[512,128]{1,0:T(8,128)(2,1)S(1)}, u32[]{:S(2)}, u32[]{:S(2)}) %collective-permute-start.10) | collective-permute-done | bytes 131104 | tf_op jit(solution)/shard_map/ppermute | solution.py:237
  148.4 0.0 collective-permute-start.15
  148.4 0.0 collective-permute-done.11.refs_4_
  148.4 0.0 copy-start.3
  148.5 0.0 collective-permute-done.12.refs_5_
  148.5 0.0 copy-start.4
  148.5 0.7 collective-permute-done.13.refs_6_
  149.2 1.0 collective-permute-done.14.refs_7_
  150.2 5.5 %collective-permute-done.15.refs_8_ = bf16[512,128]{1,0:T(8,128)(2,1)S(1)} collective-permute-done((bf16[512,128]{1,0:T(8,128)(2,1)}, bf16[512,128]{1,0:T(8,128)(2,1)S(1)}, u32[]{:S(2)}, u32[]{:S(2)}) %collective-permute-start.15) | collective-permute-done | bytes 131104 | tf_op jit(solution)/shard_map/ppermute | solution.py:237
  155.7 0.0 copy-done
  155.7 0.0 copy-done.1
  155.7 0.0 copy-done.2
  155.7 0.0 copy-done.3
  155.7 0.0 copy-done.4
  155.7 0.0 copy-done.5
  155.8 0.0 copy-done.6
  155.8 0.6 copy-done.7
  156.4 80.9 %shard_map.75 = bf16[64,32768]{1,0:T(8,128)(2,1)} custom-call(s32[256]{0:T(256)} %and_select_fusion.1.win_ref, s32[256]{0:T(256)} %off_ref.3, bf16[64,32768]{1,0:T(8,128)(2,1)} %bitcast.7, s32[256,128]{1,0:T(8,128)} %bitcast.10, bf16[8,64,128]{2,1,0:T(8,128)(2,1)} %bitcast.11, bf16[4096,128]{1,0:T(8,128)(2,1)} %get-tuple-element.32.refs_0_, ...), custom_call_target="tpu_custom_call" | custom-call | flops 1610612736 | bytes 10616832 | tf_op jit(solution)/shard_map/pallas_call | solution.py:265
  (9 shorter events, 0.0 us)
Async XLA Ops:
  0.0 88.8 %copy-start.8 = (s32[1,8192]{1,0:T(1,128)S(1)}, s32[1,8192]{1,0:T(1,128)}, u32[]{:S(2)}) copy-start(s32[1,8192]{1,0:T(1,128)} %param.10) | copy-start | bytes 98308
  79.6 10.1 %collective-permute-start = (bf16[512,128]{1,0:T(8,128)(2,1)}, bf16[512,128]{1,0:T(8,128)(2,1)S(1)}, u32[]{:S(2)}, u32[]{:S(2)}) collective-permute-start(bf16[512,128]{1,0:T(8,128)(2,1)} %get-tuple-element.24), channel_id=1, source_target_pairs={{0,127},{1,120},{2,121},{3,122},{4,123},{5,124},{6,125},{7,126},{8... | collective-permute-start | bytes 393224 | tf_op jit(solution)/shard_map/ppermute | solution.py:211
  85.4 7.1 %collective-permute-start.1 = (bf16[512,128]{1,0:T(8,128)(2,1)}, bf16[512,128]{1,0:T(8,128)(2,1)S(1)}, u32[]{:S(2)}, u32[]{:S(2)}) collective-permute-start(bf16[512,128]{1,0:T(8,128)(2,1)} %get-tuple-element.25), channel_id=1, source_target_pairs={{0,120},{1,121},{2,122},{3,123},{4,124},{5,125},{6,126},{7,127},{8... | collective-permute-start | bytes 393224 | tf_op jit(solution)/shard_map/ppermute | solution.py:211
  86.3 8.9 %collective-permute-start.2 = (bf16[512,128]{1,0:T(8,128)(2,1)}, bf16[512,128]{1,0:T(8,128)(2,1)S(1)}, u32[]{:S(2)}, u32[]{:S(2)}) collective-permute-start(bf16[512,128]{1,0:T(8,128)(2,1)} %get-tuple-element.26), channel_id=1, source_target_pairs={{0,121},{1,122},{2,123},{3,124},{4,125},{5,126},{6,127},{7,120},{8... | collective-permute-start | bytes 393224 | tf_op jit(solution)/shard_map/ppermute | solution.py:211
  86.6 9.2 %collective-permute-start.3 = (bf16[512,128]{1,0:T(8,128)(2,1)}, bf16[512,128]{1,0:T(8,128)(2,1)S(1)}, u32[]{:S(2)}, u32[]{:S(2)}) collective-permute-start(bf16[512,128]{1,0:T(8,128)(2,1)} %get-tuple-element.27), channel_id=1, source_target_pairs={{0,7},{1,0},{2,1},{3,2},{4,3},{5,4},{6,5},{7,6},{8,15},{9,8},{10,9... | collective-permute-start | bytes 393224 | tf_op jit(solution)/shard_map/ppermute | solution.py:211
  88.0 7.8 %collective-permute-start.4 = (bf16[512,128]{1,0:T(8,128)(2,1)}, bf16[512,128]{1,0:T(8,128)(2,1)S(1)}, u32[]{:S(2)}, u32[]{:S(2)}) collective-permute-start(bf16[512,128]{1,0:T(8,128)(2,1)} %get-tuple-element.28), channel_id=1, source_target_pairs={{0,1},{1,2},{2,3},{3,4},{4,5},{5,6},{6,7},{7,0},{8,9},{9,10},{10,1... | collective-permute-start | bytes 393224 | tf_op jit(solution)/shard_map/ppermute | solution.py:211
  89.6 17.8 %copy-start.9 = (bf16[512,128]{1,0:T(8,128)(2,1)}, bf16[512,128]{1,0:T(8,128)(2,1)S(1)}, u32[]{:S(2)}) copy-start(bf16[512,128]{1,0:T(8,128)(2,1)S(1)} %collective-permute-done.refs_1_) | copy-start | bytes 393220
  89.6 11.0 %collective-permute-start.5 = (bf16[512,128]{1,0:T(8,128)(2,1)}, bf16[512,128]{1,0:T(8,128)(2,1)S(1)}, u32[]{:S(2)}, u32[]{:S(2)}) collective-permute-start(bf16[512,128]{1,0:T(8,128)(2,1)} %get-tuple-element.29), channel_id=1, source_target_pairs={{0,15},{1,8},{2,9},{3,10},{4,11},{5,12},{6,13},{7,14},{8,23},{9,16... | collective-permute-start | bytes 393224 | tf_op jit(solution)/shard_map/ppermute | solution.py:211
  92.5 14.9 %copy-start.10 = (bf16[512,128]{1,0:T(8,128)(2,1)}, bf16[512,128]{1,0:T(8,128)(2,1)S(1)}, u32[]{:S(2)}) copy-start(bf16[512,128]{1,0:T(8,128)(2,1)S(1)} %collective-permute-done.1.refs_2_) | copy-start | bytes 393220
  92.5 12.7 %collective-permute-start.6 = (bf16[512,128]{1,0:T(8,128)(2,1)}, bf16[512,128]{1,0:T(8,128)(2,1)S(1)}, u32[]{:S(2)}, u32[]{:S(2)}) collective-permute-start(bf16[512,128]{1,0:T(8,128)(2,1)} %get-tuple-element.30), channel_id=1, source_target_pairs={{0,8},{1,9},{2,10},{3,11},{4,12},{5,13},{6,14},{7,15},{8,16},{9,17... | collective-permute-start | bytes 393224 | tf_op jit(solution)/shard_map/ppermute | solution.py:211
  95.1 12.3 %copy-start.11 = (bf16[512,128]{1,0:T(8,128)(2,1)}, bf16[512,128]{1,0:T(8,128)(2,1)S(1)}, u32[]{:S(2)}) copy-start(bf16[512,128]{1,0:T(8,128)(2,1)S(1)} %collective-permute-done.2.refs_3_) | copy-start | bytes 393220
  95.1 12.3 %collective-permute-start.7 = (bf16[512,128]{1,0:T(8,128)(2,1)}, bf16[512,128]{1,0:T(8,128)(2,1)S(1)}, u32[]{:S(2)}, u32[]{:S(2)}) collective-permute-start(bf16[512,128]{1,0:T(8,128)(2,1)} %get-tuple-element.31), channel_id=1, source_target_pairs={{0,9},{1,10},{2,11},{3,12},{4,13},{5,14},{6,15},{7,8},{8,17},{9,18... | collective-permute-start | bytes 393224 | tf_op jit(solution)/shard_map/ppermute | solution.py:211
  95.8 11.6 %copy-start.12 = (bf16[512,128]{1,0:T(8,128)(2,1)}, bf16[512,128]{1,0:T(8,128)(2,1)S(1)}, u32[]{:S(2)}) copy-start(bf16[512,128]{1,0:T(8,128)(2,1)S(1)} %collective-permute-done.3.refs_4_) | copy-start | bytes 393220
  95.8 11.6 %copy-start.13 = (bf16[512,128]{1,0:T(8,128)(2,1)}, bf16[512,128]{1,0:T(8,128)(2,1)S(1)}, u32[]{:S(2)}) copy-start(bf16[512,128]{1,0:T(8,128)(2,1)S(1)} %collective-permute-done.4.refs_5_) | copy-start | bytes 393220
  100.6 6.8 %copy-start.14 = (bf16[512,128]{1,0:T(8,128)(2,1)}, bf16[512,128]{1,0:T(8,128)(2,1)S(1)}, u32[]{:S(2)}) copy-start(bf16[512,128]{1,0:T(8,128)(2,1)S(1)} %collective-permute-done.5.refs_6_) | copy-start | bytes 393220
  105.2 2.2 copy-start.15
  107.4 0.6 copy-start.16
  133.0 10.4 %collective-permute-start.8 = (bf16[512,128]{1,0:T(8,128)(2,1)}, bf16[512,128]{1,0:T(8,128)(2,1)S(1)}, u32[]{:S(2)}, u32[]{:S(2)}) collective-permute-start(bf16[512,128]{1,0:T(8,128)(2,1)} %get-tuple-element.33), channel_id=1, source_target_pairs={{127,0},{120,1},{121,2},{122,3},{123,4},{124,5},{125,6},{126,7},{7... | collective-permute-start | bytes 393224 | tf_op jit(solution)/shard_map/ppermute | solution.py:237
  133.0 11.9 %collective-permute-start.9 = (bf16[512,128]{1,0:T(8,128)(2,1)}, bf16[512,128]{1,0:T(8,128)(2,1)S(1)}, u32[]{:S(2)}, u32[]{:S(2)}) collective-permute-start(bf16[512,128]{1,0:T(8,128)(2,1)} %get-tuple-element.34), channel_id=1, source_target_pairs={{120,0},{121,1},{122,2},{123,3},{124,4},{125,5},{126,6},{127,7},{0... | collective-permute-start | bytes 393224 | tf_op jit(solution)/shard_map/ppermute | solution.py:237
  133.1 15.4 %collective-permute-start.10 = (bf16[512,128]{1,0:T(8,128)(2,1)}, bf16[512,128]{1,0:T(8,128)(2,1)S(1)}, u32[]{:S(2)}, u32[]{:S(2)}) collective-permute-start(bf16[512,128]{1,0:T(8,128)(2,1)} %get-tuple-element.35), channel_id=1, source_target_pairs={{121,0},{122,1},{123,2},{124,3},{125,4},{126,5},{127,6},{120,7},{1... | collective-permute-start | bytes 393224 | tf_op jit(solution)/shard_map/ppermute | solution.py:237
  133.1 15.3 %collective-permute-start.11 = (bf16[512,128]{1,0:T(8,128)(2,1)}, bf16[512,128]{1,0:T(8,128)(2,1)S(1)}, u32[]{:S(2)}, u32[]{:S(2)}) collective-permute-start(bf16[512,128]{1,0:T(8,128)(2,1)} %get-tuple-element.36), channel_id=1, source_target_pairs={{7,0},{0,1},{1,2},{2,3},{3,4},{4,5},{5,6},{6,7},{15,8},{8,9},{9,10... | collective-permute-start | bytes 393224 | tf_op jit(solution)/shard_map/ppermute | solution.py:237
  133.2 15.2 %collective-permute-start.12 = (bf16[512,128]{1,0:T(8,128)(2,1)}, bf16[512,128]{1,0:T(8,128)(2,1)S(1)}, u32[]{:S(2)}, u32[]{:S(2)}) collective-permute-start(bf16[512,128]{1,0:T(8,128)(2,1)} %get-tuple-element.37), channel_id=1, source_target_pairs={{1,0},{2,1},{3,2},{4,3},{5,4},{6,5},{7,6},{0,7},{9,8},{10,9},{11,1... | collective-permute-start | bytes 393224 | tf_op jit(solution)/shard_map/ppermute | solution.py:237
  143.4 12.4 %copy-start = (bf16[512,128]{1,0:T(8,128)(2,1)}, bf16[512,128]{1,0:T(8,128)(2,1)S(1)}, u32[]{:S(2)}) copy-start(bf16[512,128]{1,0:T(8,128)(2,1)S(1)} %collective-permute-done.8.refs_1_) | copy-start | bytes 393220
  143.4 5.9 %collective-permute-start.13 = (bf16[512,128]{1,0:T(8,128)(2,1)}, bf16[512,128]{1,0:T(8,128)(2,1)S(1)}, u32[]{:S(2)}, u32[]{:S(2)}) collective-permute-start(bf16[512,128]{1,0:T(8,128)(2,1)} %get-tuple-element.38), channel_id=1, source_target_pairs={{15,0},{8,1},{9,2},{10,3},{11,4},{12,5},{13,6},{14,7},{23,8},{16,9... | collective-permute-start | bytes 393224 | tf_op jit(solution)/shard_map/ppermute | solution.py:237
  144.9 10.8 %copy-start.1 = (bf16[512,128]{1,0:T(8,128)(2,1)}, bf16[512,128]{1,0:T(8,128)(2,1)S(1)}, u32[]{:S(2)}) copy-start(bf16[512,128]{1,0:T(8,128)(2,1)S(1)} %collective-permute-done.9.refs_2_) | copy-start | bytes 393220
  144.9 5.3 %collective-permute-start.14 = (bf16[512,128]{1,0:T(8,128)(2,1)}, bf16[512,128]{1,0:T(8,128)(2,1)S(1)}, u32[]{:S(2)}, u32[]{:S(2)}) collective-permute-start(bf16[512,128]{1,0:T(8,128)(2,1)} %get-tuple-element.39), channel_id=1, source_target_pairs={{8,0},{9,1},{10,2},{11,3},{12,4},{13,5},{14,6},{15,7},{16,8},{17,9... | collective-permute-start | bytes 393224 | tf_op jit(solution)/shard_map/ppermute | solution.py:237
  148.4 7.3 %copy-start.2 = (bf16[512,128]{1,0:T(8,128)(2,1)}, bf16[512,128]{1,0:T(8,128)(2,1)S(1)}, u32[]{:S(2)}) copy-start(bf16[512,128]{1,0:T(8,128)(2,1)S(1)} %collective-permute-done.10.refs_3_) | copy-start | bytes 393220
  148.4 7.3 %collective-permute-start.15 = (bf16[512,128]{1,0:T(8,128)(2,1)}, bf16[512,128]{1,0:T(8,128)(2,1)S(1)}, u32[]{:S(2)}, u32[]{:S(2)}) collective-permute-start(bf16[512,128]{1,0:T(8,128)(2,1)} %get-tuple-element.40), channel_id=1, source_target_pairs={{9,0},{10,1},{11,2},{12,3},{13,4},{14,5},{15,6},{8,7},{17,8},{18,9... | collective-permute-start | bytes 393224 | tf_op jit(solution)/shard_map/ppermute | solution.py:237
  148.4 7.3 %copy-start.3 = (bf16[512,128]{1,0:T(8,128)(2,1)}, bf16[512,128]{1,0:T(8,128)(2,1)S(1)}, u32[]{:S(2)}) copy-start(bf16[512,128]{1,0:T(8,128)(2,1)S(1)} %collective-permute-done.11.refs_4_) | copy-start | bytes 393220
  148.5 7.3 %copy-start.4 = (bf16[512,128]{1,0:T(8,128)(2,1)}, bf16[512,128]{1,0:T(8,128)(2,1)S(1)}, u32[]{:S(2)}) copy-start(bf16[512,128]{1,0:T(8,128)(2,1)S(1)} %collective-permute-done.12.refs_5_) | copy-start | bytes 393220
  149.2 6.5 %copy-start.5 = (bf16[512,128]{1,0:T(8,128)(2,1)}, bf16[512,128]{1,0:T(8,128)(2,1)S(1)}, u32[]{:S(2)}) copy-start(bf16[512,128]{1,0:T(8,128)(2,1)S(1)} %collective-permute-done.13.refs_6_) | copy-start | bytes 393220
  150.2 5.6 %copy-start.6 = (bf16[512,128]{1,0:T(8,128)(2,1)}, bf16[512,128]{1,0:T(8,128)(2,1)S(1)}, u32[]{:S(2)}) copy-start(bf16[512,128]{1,0:T(8,128)(2,1)S(1)} %collective-permute-done.14.refs_7_) | copy-start | bytes 393220
  155.7 0.6 copy-start.7
where the time goes:
time: 238 us; the launch traced here: 237 us
  Pallas kernels  184 us (77%)
  waiting for transfers between devices  37.3 us (16%)
  starting transfers between devices  12.4 us (5%)
    pallas_call x1, Pallas kernels, local(): up(brick_window, block_offset, xt, entry_rows, w_up_t, answers[0], *retur...  80.9 us
    pallas_call x1, Pallas kernels, local(): parts = down(brick_window, block_offset, xt, entry_rows, w_down)  77.9 us
    pallas_call x1, Pallas kernels, local(): coarse(cell_window, cells, b_down.reshape(1, out_width), parts[0], *arrived)  24.9 us
    ppermute x8, waiting for transfers between devices, local(): lax.ppermute(answers[1 + g], ('outer', 'inner'), group_route(g, -1))  20.8 us
    ppermute x8, waiting for transfers between devices, local(): lax.ppermute(parts[1 + g], ('outer', 'inner'), group_route(g, 1))  16.5 us
    ppermute x8, starting transfers between devices, local(): lax.ppermute(parts[1 + g], ('outer', 'inner'), group_route(g, 1))  10.5 us
  transfers between devices with their start and end apart: 16, of which 12 were waited for; matrix products, arithmetic and copies ran while one was open for 0% of the time, Pallas kernels for 0%

commit v1 on v0

--- a/solution.py
+++ b/solution.py
@@ -10,6 +10,8 @@
 SELF_CAP = 4096
 WIN = 128
 BRICKS_PER_STEP = 32
+UNROLL = 8
+WIN_UNROLL = 4
 
 step_table = ((-1, -1), (-1, 0), (-1, 1), (0, -1), (0, 1), (1, -1), (1, 0), (1, 1))
 
@@ -39,24 +41,29 @@
     def _():
         acc[...] = jnp.zeros_like(acc)
 
-    def body(j, carry):
-        brick = step * per_step + j
-        window = win_ref[brick]
-        offset = off_ref[brick]
-        inside = jnp.bitwise_and(e_ref[pl.ds(j, 1), :], WIN - 1)
-        pick = one_hot_rows(inside)
-        cols = pl.ds(pl.multiple_of(j * BLK, BLK), BLK)
-        summed = lax.dot_general(pick, xt_ref[:, cols], NT, preferred_element_type=jnp.float32)
-        high, low = split_parts(summed)
-        weights = w_ref[offset]
-        part = jnp.dot(high, weights, preferred_element_type=jnp.float32) + jnp.dot(
-            low, weights, preferred_element_type=jnp.float32
-        )
-        rows = pl.ds(pl.multiple_of(window * WIN, WIN), WIN)
-        acc[rows, :] += part
+    def body(u, carry):
+        results = []
+        for t in range(UNROLL):
+            j = u * UNROLL + t
+            brick = step * per_step + j
+            window = win_ref[brick]
+            offset = off_ref[brick]
+            inside = jnp.bitwise_and(e_ref[pl.ds(j, 1), :], WIN - 1)
+            pick = one_hot_rows(inside)
+            cols = pl.ds(pl.multiple_of(j * BLK, BLK), BLK)
+            summed = lax.dot_general(pick, xt_ref[:, cols], NT, preferred_element_type=jnp.float32)
+            high, low = split_parts(summed)
+            weights = w_ref[offset]
+            part = jnp.dot(high, weights, preferred_element_type=jnp.float32) + jnp.dot(
+                low, weights, preferred_element_type=jnp.float32
+            )
+            results.append((window, part))
+        for window, part in results:
+            rows = pl.ds(pl.multiple_of(window * WIN, WIN), WIN)
+            acc[rows, :] += part
         return carry
 
-    lax.fori_loop(0, per_step, body, 0)
+    lax.fori_loop(0, per_step // UNROLL, body, 0)
 
     @pl.when(step == pl.num_programs(0) - 1)
     def _():
@@ -86,28 +93,35 @@
     for src in sources:
         count = src.shape[0] // WIN
 
-        def gather_body(j, carry, src=src, base=base):
-            pick, rows = pick_of(base + j)
-            entries = src[pl.ds(pl.multiple_of(j * WIN, WIN), WIN), :]
-            acc[rows, :] += jnp.dot(pick, entries, preferred_element_type=jnp.float32)
+        def gather_body(u, carry, src=src, base=base):
+            results = []
+            for t in range(WIN_UNROLL):
+                j = u * WIN_UNROLL + t
+                pick, rows = pick_of(base + j)
+                entries = src[pl.ds(pl.multiple_of(j * WIN, WIN), WIN), :]
+                results.append((rows, jnp.dot(pick, entries, preferred_element_type=jnp.float32)))
+            for rows, value in results:
+                acc[rows, :] += value
             return carry
 
-        lax.fori_loop(0, count, gather_body, 0)
+        lax.fori_loop(0, count // WIN_UNROLL, gather_body, 0)
         base += count
 
     coarse[...] = jnp.maximum(acc[...] + bias_ref[...], 0.0).astype(jnp.bfloat16)
 
     base = 0
     for out in outs:
-        count = out.shape[0] // WIN
-
-        def scatter_body(j, carry, out=out, base=base):
-            pick, rows = pick_of(base + j)
-            chosen = lax.dot_general(pick, coarse[rows, :], TN, preferred_element_type=jnp.float32)
-            out[pl.ds(pl.multiple_of(j * WIN, WIN), WIN), :] = chosen.astype(jnp.bfloat16)
+        count = out.shape[1] // WIN
+
+        def scatter_body(u, carry, out=out, base=base):
+            for t in range(WIN_UNROLL):
+                j = u * WIN_UNROLL + t
+                pick, rows = pick_of(base + j)
+                chosen = lax.dot_general(coarse[rows, :], pick, TN, preferred_element_type=jnp.float32)
+                out[:, pl.ds(pl.multiple_of(j * WIN, WIN), WIN)] = chosen.astype(jnp.bfloat16)
             return carry
 
-        lax.fori_loop(0, count, scatter_body, 0)
+        lax.fori_loop(0, count // WIN_UNROLL, scatter_body, 0)
         base += count
 
 
@@ -124,31 +138,30 @@
         copies = []
         start = 0
         for index, src in enumerate(sources):
-            size = src.shape[0]
-            copy = pltpu.make_async_copy(src, stack.at[pl.ds(start, size)], sems.at[index])
+            size = src.shape[1]
+            copy = pltpu.make_async_copy(src, stack.at[:, pl.ds(start, size)], sems.at[index])
             copy.start()
             copies.append(copy)
             start += size
         for copy in copies:
             copy.wait()
 
-    def body(j, carry):
-        brick = step * per_step + j
-        window = win_ref[brick]
-        offset = off_ref[brick]
-        inside = jnp.bitwise_and(e_ref[pl.ds(j, 1), :], WIN - 1)
-        pick = one_hot_rows(inside)
-        parents = stack[pl.ds(pl.multiple_of(window * WIN, WIN), WIN), :]
-        lifted_t = lax.dot_general(wt_ref[offset], parents, NT, preferred_element_type=jnp.float32)
-        high, low = split_parts(lifted_t)
-        lifted = jnp.dot(high, pick, preferred_element_type=jnp.float32) + jnp.dot(
-            low, pick, preferred_element_type=jnp.float32
-        )
-        cols = pl.ds(pl.multiple_of(j * BLK, BLK), BLK)
-        out_ref[:, cols] = (xt_ref[:, cols].astype(jnp.float32) + lifted).astype(out_ref.dtype)
+    def body(u, carry):
+        for t in range(UNROLL):
+            j = u * UNROLL + t
+            brick = step * per_step + j
+            window = win_ref[brick]
+            offset = off_ref[brick]
+            inside = jnp.bitwise_and(e_ref[pl.ds(j, 1), :], WIN - 1)
+            pick = one_hot_rows(inside)
+            parents = stack[:, pl.ds(pl.multiple_of(window * WIN, WIN), WIN)]
+            rows_t = jnp.dot(parents, pick, preferred_element_type=jnp.float32).astype(jnp.bfloat16)
+            lifted = jnp.dot(wt_ref[offset], rows_t, preferred_element_type=jnp.float32)
+            cols = pl.ds(pl.multiple_of(j * BLK, BLK), BLK)
+            out_ref[:, cols] = (xt_ref[:, cols].astype(jnp.float32) + lifted).astype(out_ref.dtype)
         return carry
 
-    lax.fori_loop(0, per_step, body, 0)
+    lax.fori_loop(0, per_step // UNROLL, body, 0)
 
 
 def group_route(g, sign):
@@ -182,6 +195,7 @@
     part_shapes = [jax.ShapeDtypeStruct((SELF_CAP, out_width), jnp.bfloat16)] + [
         jax.ShapeDtypeStruct((cap, out_width), jnp.bfloat16)
     ] * n_groups
+    answer_shapes = [jax.ShapeDtypeStruct((s.shape[1], s.shape[0]), s.dtype) for s in part_shapes]
     whole = lambda shape: pl.BlockSpec(shape, lambda *idx: (0,) * len(shape))
 
     down = pl.pallas_call(
@@ -213,13 +227,13 @@
 
     coarse = pl.pallas_call(
         coarse_kernel,
-        out_shape=part_shapes,
+        out_shape=answer_shapes,
         grid_spec=pltpu.PrefetchScalarGridSpec(
             num_scalar_prefetch=1,
             grid=(1,),
             in_specs=[whole(cells.shape), whole((1, out_width))]
             + [whole(s.shape) for s in part_shapes],
-            out_specs=[whole(s.shape) for s in part_shapes],
+            out_specs=[whole(s.shape) for s in answer_shapes],
             scratch_shapes=[
                 pltpu.VMEM((C_DEV, out_width), jnp.float32),
                 pltpu.VMEM((C_DEV, out_width), jnp.bfloat16),
@@ -251,7 +265,7 @@
             + [pl.BlockSpec(memory_space=pl.ANY)] * (1 + n_groups),
             out_specs=pl.BlockSpec((in_width, BRICKS_PER_STEP * BLK), lambda i, *_: (0, i)),
             scratch_shapes=[
-                pltpu.VMEM((entries, out_width), jnp.bfloat16),
+                pltpu.VMEM((out_width, entries), jnp.bfloat16),
                 pltpu.SemaphoreType.DMA((1 + n_groups,)),
             ],
         ),

time: 238 us -> 109 us (0.46)
  Pallas kernels: 184 us -> 55.6 us
    pallas_call x1, Pallas kernels: 80.9 us -> 17.3 us  [local(): up(brick_window, block_offset, xt, entry_rows, w_up_t, answers[0], *retur...]
    pallas_call x1, Pallas kernels: 77.9 us -> 30.3 us  [local(): parts = down(brick_window, block_offset, xt, entry_rows, w_down)]
    pallas_call x1, Pallas kernels: 24.9 us -> 8 us  [local(): coarse(cell_window, cells, b_down.reshape(1, out_width), parts[0], *arrived)]
  transfers between devices with their start and end apart: 16 -> 16, of which waited for: 12 -> 12; matrix products, arithmetic and copies ran while one was open for 0% -> 1% of each run, Pallas kernels for 0% -> 0%
where the time goes in v1:
time: 109 us
  Pallas kernels  55.6 us (51%)
  waiting for transfers between devices  37.3 us (34%)
  starting transfers between devices  12.4 us (11%)
  local copies, waits for them, and re-layouts  2.26 us (2%)
  other arithmetic  1.35 us (1%)
    pallas_call x1, Pallas kernels, local(): parts = down(brick_window, block_offset, xt, entry_rows, w_down)  30.3 us
    ppermute x8, waiting for transfers between devices, local(): lax.ppermute(answers[1 + g], ('outer', 'inner'), group_route(g, -1))  20.8 us
    pallas_call x1, Pallas kernels, local(): up(brick_window, block_offset, xt, entry_rows, w_up_t, answers[0], *retur...  17.3 us
    ppermute x8, waiting for transfers between devices, local(): lax.ppermute(parts[1 + g], ('outer', 'inner'), group_route(g, 1))  16.5 us
    ppermute x8, starting transfers between devices, local(): lax.ppermute(parts[1 + g], ('outer', 'inner'), group_route(g, 1))  10.5 us
    pallas_call x1, Pallas kernels, local(): coarse(cell_window, cells, b_down.reshape(1, out_width), parts[0], *arrived)  8 us
  transfers between devices with their start and end apart: 16, of which 12 were waited for; matrix products, arithmetic and copies ran while one was open for 1% of the time, Pallas kernels for 0%

profile of v1, /device:TPU:24, one launch (start us, length us, event | category | flops | bytes accessed | tf_op | source)
XLA Modules:
  0.0 109.1 jit_solution(14274285806908765377)
XLA Ops:
  0.0 0.0 copy-start.8
  0.0 1.0 slice_reduce_fusion
  1.0 0.6 and_select_fusion.1.win_ref
  1.6 30.3 %shard_map.73 = (bf16[4096,128]{1,0:T(8,128)(2,1)}, bf16[512,128]{1,0:T(8,128)(2,1)}, bf16[512,128]{1,0:T(8,128)(2,1)}, bf16[512,128]{1,0:T(8,128)(2,1)}, bf16[5...) custom-call(s32[256]{0:T(256)} %and_select_fusion.1.win_ref, ...), custom_call_target="tpu_custom_call" | custom-call | flops 1610612736 | bytes 6422528 | tf_op jit(solution)/shard_map/pallas_call | solution.py:222
  32.0 5.9 %collective-permute-start = (bf16[512,128]{1,0:T(8,128)(2,1)}, bf16[512,128]{1,0:T(8,128)(2,1)S(1)}, u32[]{:S(2)}, u32[]{:S(2)}) collective-permute-start(bf16[512,128]{1,0:T(8,128)(2,1)} %get-tuple-element.24), channel_id=1, source_target_pairs={{0,127},{1,120},{2,121},{3,122},{4,123},{5,124},{6,125},{7,126},{8... | collective-permute-start | bytes 393224 | tf_op jit(solution)/shard_map/ppermute | solution.py:225
  37.8 0.8 collective-permute-start.1
  38.7 0.3 collective-permute-start.2
  39.0 1.4 %collective-permute-start.3 = (bf16[512,128]{1,0:T(8,128)(2,1)}, bf16[512,128]{1,0:T(8,128)(2,1)S(1)}, u32[]{:S(2)}, u32[]{:S(2)}) collective-permute-start(bf16[512,128]{1,0:T(8,128)(2,1)} %get-tuple-element.27), channel_id=1, source_target_pairs={{0,7},{1,0},{2,1},{3,2},{4,3},{5,4},{6,5},{7,6},{8,15},{9,8},{10,9... | collective-permute-start | bytes 393224 | tf_op jit(solution)/shard_map/ppermute | solution.py:225
  40.4 0.9 collective-permute-start.4
  41.2 0.0 copy-done.8
  41.2 0.1 reduce_min.9
  41.3 0.7 collective-permute-done.refs_1_
  42.0 0.0 copy-start.9
  42.0 1.2 %collective-permute-start.5 = (bf16[512,128]{1,0:T(8,128)(2,1)}, bf16[512,128]{1,0:T(8,128)(2,1)S(1)}, u32[]{:S(2)}, u32[]{:S(2)}) collective-permute-start(bf16[512,128]{1,0:T(8,128)(2,1)} %get-tuple-element.29), channel_id=1, source_target_pairs={{0,15},{1,8},{2,9},{3,10},{4,11},{5,12},{6,13},{7,14},{8,23},{9,16... | collective-permute-start | bytes 393224 | tf_op jit(solution)/shard_map/ppermute | solution.py:225
  43.2 1.7 %collective-permute-done.1.refs_2_ = bf16[512,128]{1,0:T(8,128)(2,1)S(1)} collective-permute-done((bf16[512,128]{1,0:T(8,128)(2,1)}, bf16[512,128]{1,0:T(8,128)(2,1)S(1)}, u32[]{:S(2)}, u32[]{:S(2)}) %collective-permute-start.1) | collective-permute-done | bytes 131104 | tf_op jit(solution)/shard_map/ppermute | solution.py:225
  44.9 0.0 copy-start.10
  44.9 0.0 collective-permute-start.6
  44.9 2.6 %collective-permute-done.2.refs_3_ = bf16[512,128]{1,0:T(8,128)(2,1)S(1)} collective-permute-done((bf16[512,128]{1,0:T(8,128)(2,1)}, bf16[512,128]{1,0:T(8,128)(2,1)S(1)}, u32[]{:S(2)}, u32[]{:S(2)}) %collective-permute-start.2) | collective-permute-done | bytes 131104 | tf_op jit(solution)/shard_map/ppermute | solution.py:225
  47.5 0.0 collective-permute-start.7
  47.5 0.6 and_select_fusion.cw_ref
  48.2 0.0 collective-permute-done.3.refs_4_
  48.2 0.0 collective-permute-done.4.refs_5_
  48.2 0.0 copy-start.13
  48.2 4.8 %collective-permute-done.5.refs_6_ = bf16[512,128]{1,0:T(8,128)(2,1)S(1)} collective-permute-done((bf16[512,128]{1,0:T(8,128)(2,1)}, bf16[512,128]{1,0:T(8,128)(2,1)S(1)}, u32[]{:S(2)}, u32[]{:S(2)}) %collective-permute-start.5) | collective-permute-done | bytes 131104 | tf_op jit(solution)/shard_map/ppermute | solution.py:225
  53.0 0.0 copy-start.14
  53.0 4.6 %collective-permute-done.6.refs_7_ = bf16[512,128]{1,0:T(8,128)(2,1)S(1)} collective-permute-done((bf16[512,128]{1,0:T(8,128)(2,1)}, bf16[512,128]{1,0:T(8,128)(2,1)S(1)}, u32[]{:S(2)}, u32[]{:S(2)}) %collective-permute-start.6) | collective-permute-done | bytes 131104 | tf_op jit(solution)/shard_map/ppermute | solution.py:225
  57.6 0.0 copy-start.15
  57.6 2.2 %collective-permute-done.7.refs_8_ = bf16[512,128]{1,0:T(8,128)(2,1)S(1)} collective-permute-done((bf16[512,128]{1,0:T(8,128)(2,1)}, bf16[512,128]{1,0:T(8,128)(2,1)S(1)}, u32[]{:S(2)}, u32[]{:S(2)}) %collective-permute-start.7) | collective-permute-done | bytes 131104 | tf_op jit(solution)/shard_map/ppermute | solution.py:225
  59.8 0.0 copy-done.9
  59.8 0.0 copy-done.10
  59.8 0.0 copy-done.11
  59.8 0.0 copy-done.12
  59.8 0.0 copy-done.13
  59.8 0.0 copy-done.14
  59.8 0.0 copy-done.15
  59.8 0.6 copy-done.16
  60.4 8.0 %shard_map.74 = (bf16[128,4096]{1,0:T(8,128)(2,1)}, bf16[128,512]{1,0:T(8,128)(2,1)}, bf16[128,512]{1,0:T(8,128)(2,1)}, bf16[128,512]{1,0:T(8,128)(2,1)}, bf16[1...) custom-call(s32[64]{0:T(128)} %and_select_fusion.cw_ref, ...), custom_call_target="tpu_custom_call" | custom-call | flops 536870912 | bytes 4194304 | tf_op jit(solution)/shard_map/pallas_call | solution.py:248
  68.4 0.0 collective-permute-start.8
  68.4 0.1 collective-permute-start.9
  68.5 0.1 collective-permute-start.10
  68.6 0.1 collective-permute-start.11
  68.7 1.7 %collective-permute-start.12 = (bf16[128,512]{1,0:T(8,128)(2,1)}, bf16[128,512]{1,0:T(8,128)(2,1)S(1)}, u32[]{:S(2)}, u32[]{:S(2)}) collective-permute-start(bf16[128,512]{1,0:T(8,128)(2,1)} %get-tuple-element.37), channel_id=1, source_target_pairs={{1,0},{2,1},{3,2},{4,3},{5,4},{6,5},{7,6},{0,7},{9,8},{10,9},{11,1... | collective-permute-start | bytes 393224 | tf_op jit(solution)/shard_map/ppermute | solution.py:251
  70.3 8.5 %collective-permute-done.8.refs_1_ = bf16[128,512]{1,0:T(8,128)(2,1)S(1)} collective-permute-done((bf16[128,512]{1,0:T(8,128)(2,1)}, bf16[128,512]{1,0:T(8,128)(2,1)S(1)}, u32[]{:S(2)}, u32[]{:S(2)}) %collective-permute-start.8) | collective-permute-done | bytes 131104 | tf_op jit(solution)/shard_map/ppermute | solution.py:251
  78.8 0.0 collective-permute-start.13
  78.8 1.6 %collective-permute-done.9.refs_2_ = bf16[128,512]{1,0:T(8,128)(2,1)S(1)} collective-permute-done((bf16[128,512]{1,0:T(8,128)(2,1)}, bf16[128,512]{1,0:T(8,128)(2,1)S(1)}, u32[]{:S(2)}, u32[]{:S(2)}) %collective-permute-start.9) | collective-permute-done | bytes 131104 | tf_op jit(solution)/shard_map/ppermute | solution.py:251
  80.4 0.0 collective-permute-start.14
  80.4 3.5 %collective-permute-done.10.refs_3_ = bf16[128,512]{1,0:T(8,128)(2,1)S(1)} collective-permute-done((bf16[128,512]{1,0:T(8,128)(2,1)}, bf16[128,512]{1,0:T(8,128)(2,1)S(1)}, u32[]{:S(2)}, u32[]{:S(2)}) %collective-permute-start.10) | collective-permute-done | bytes 131104 | tf_op jit(solution)/shard_map/ppermute | solution.py:251
  83.9 0.0 collective-permute-start.15
  83.9 0.0 collective-permute-done.11.refs_4_
  83.9 0.0 copy-start.3
  83.9 0.0 collective-permute-done.12.refs_5_
  83.9 0.0 copy-start.4
  83.9 0.8 collective-permute-done.13.refs_6_
  84.7 1.1 collective-permute-done.14.refs_7_
  85.7 5.5 %collective-permute-done.15.refs_8_ = bf16[128,512]{1,0:T(8,128)(2,1)S(1)} collective-permute-done((bf16[128,512]{1,0:T(8,128)(2,1)}, bf16[128,512]{1,0:T(8,128)(2,1)S(1)}, u32[]{:S(2)}, u32[]{:S(2)}) %collective-permute-start.15) | collective-permute-done | bytes 131104 | tf_op jit(solution)/shard_map/ppermute | solution.py:251
  91.2 0.0 copy-done
  91.2 0.0 copy-done.1
  91.2 0.0 copy-done.2
  91.2 0.0 copy-done.3
  91.2 0.0 copy-done.4
  91.2 0.0 copy-done.5
  91.2 0.0 copy-done.6
  91.2 0.6 copy-done.7
  91.8 17.3 %shard_map.75 = bf16[64,32768]{1,0:T(8,128)(2,1)} custom-call(s32[256]{0:T(256)} %and_select_fusion.1.win_ref, s32[256]{0:T(256)} %off_ref.3, bf16[64,32768]{1,0:T(8,128)(2,1)} %bitcast.7, s32[256,128]{1,0:T(8,128)} %bitcast.10, bf16[8,64,128]{2,1,0:T(8,128)(2,1)} %bitcast.11, bf16[128,4096]{1,0:T(8,128)(2,1)} %get-tuple-element.32.refs_0_, ...), custom_call_target="tpu_custom_call" | custom-call | flops 1610612736 | bytes 10616832 | tf_op jit(solution)/shard_map/pallas_call | solution.py:279
  (9 shorter events, 0.0 us)
Async XLA Ops:
  0.0 41.2 %copy-start.8 = (s32[1,8192]{1,0:T(1,128)S(1)}, s32[1,8192]{1,0:T(1,128)}, u32[]{:S(2)}) copy-start(s32[1,8192]{1,0:T(1,128)} %param.10) | copy-start | bytes 98308
  32.0 10.1 %collective-permute-start = (bf16[512,128]{1,0:T(8,128)(2,1)}, bf16[512,128]{1,0:T(8,128)(2,1)S(1)}, u32[]{:S(2)}, u32[]{:S(2)}) collective-permute-start(bf16[512,128]{1,0:T(8,128)(2,1)} %get-tuple-element.24), channel_id=1, source_target_pairs={{0,127},{1,120},{2,121},{3,122},{4,123},{5,124},{6,125},{7,126},{8... | collective-permute-start | bytes 393224 | tf_op jit(solution)/shard_map/ppermute | solution.py:225
  37.8 7.1 %collective-permute-start.1 = (bf16[512,128]{1,0:T(8,128)(2,1)}, bf16[512,128]{1,0:T(8,128)(2,1)S(1)}, u32[]{:S(2)}, u32[]{:S(2)}) collective-permute-start(bf16[512,128]{1,0:T(8,128)(2,1)} %get-tuple-element.25), channel_id=1, source_target_pairs={{0,120},{1,121},{2,122},{3,123},{4,124},{5,125},{6,126},{7,127},{8... | collective-permute-start | bytes 393224 | tf_op jit(solution)/shard_map/ppermute | solution.py:225
  38.7 8.9 %collective-permute-start.2 = (bf16[512,128]{1,0:T(8,128)(2,1)}, bf16[512,128]{1,0:T(8,128)(2,1)S(1)}, u32[]{:S(2)}, u32[]{:S(2)}) collective-permute-start(bf16[512,128]{1,0:T(8,128)(2,1)} %get-tuple-element.26), channel_id=1, source_target_pairs={{0,121},{1,122},{2,123},{3,124},{4,125},{5,126},{6,127},{7,120},{8... | collective-permute-start | bytes 393224 | tf_op jit(solution)/shard_map/ppermute | solution.py:225
  39.0 9.2 %collective-permute-start.3 = (bf16[512,128]{1,0:T(8,128)(2,1)}, bf16[512,128]{1,0:T(8,128)(2,1)S(1)}, u32[]{:S(2)}, u32[]{:S(2)}) collective-permute-start(bf16[512,128]{1,0:T(8,128)(2,1)} %get-tuple-element.27), channel_id=1, source_target_pairs={{0,7},{1,0},{2,1},{3,2},{4,3},{5,4},{6,5},{7,6},{8,15},{9,8},{10,9... | collective-permute-start | bytes 393224 | tf_op jit(solution)/shard_map/ppermute | solution.py:225
  40.4 7.8 %collective-permute-start.4 = (bf16[512,128]{1,0:T(8,128)(2,1)}, bf16[512,128]{1,0:T(8,128)(2,1)S(1)}, u32[]{:S(2)}, u32[]{:S(2)}) collective-permute-start(bf16[512,128]{1,0:T(8,128)(2,1)} %get-tuple-element.28), channel_id=1, source_target_pairs={{0,1},{1,2},{2,3},{3,4},{4,5},{5,6},{6,7},{7,0},{8,9},{9,10},{10,1... | collective-permute-start | bytes 393224 | tf_op jit(solution)/shard_map/ppermute | solution.py:225
  42.0 17.8 %copy-start.9 = (bf16[512,128]{1,0:T(8,128)(2,1)}, bf16[512,128]{1,0:T(8,128)(2,1)S(1)}, u32[]{:S(2)}) copy-start(bf16[512,128]{1,0:T(8,128)(2,1)S(1)} %collective-permute-done.refs_1_) | copy-start | bytes 393220
  42.0 11.0 %collective-permute-start.5 = (bf16[512,128]{1,0:T(8,128)(2,1)}, bf16[512,128]{1,0:T(8,128)(2,1)S(1)}, u32[]{:S(2)}, u32[]{:S(2)}) collective-permute-start(bf16[512,128]{1,0:T(8,128)(2,1)} %get-tuple-element.29), channel_id=1, source_target_pairs={{0,15},{1,8},{2,9},{3,10},{4,11},{5,12},{6,13},{7,14},{8,23},{9,16... | collective-permute-start | bytes 393224 | tf_op jit(solution)/shard_map/ppermute | solution.py:225
  44.9 14.9 %copy-start.10 = (bf16[512,128]{1,0:T(8,128)(2,1)}, bf16[512,128]{1,0:T(8,128)(2,1)S(1)}, u32[]{:S(2)}) copy-start(bf16[512,128]{1,0:T(8,128)(2,1)S(1)} %collective-permute-done.1.refs_2_) | copy-start | bytes 393220
  44.9 12.7 %collective-permute-start.6 = (bf16[512,128]{1,0:T(8,128)(2,1)}, bf16[512,128]{1,0:T(8,128)(2,1)S(1)}, u32[]{:S(2)}, u32[]{:S(2)}) collective-permute-start(bf16[512,128]{1,0:T(8,128)(2,1)} %get-tuple-element.30), channel_id=1, source_target_pairs={{0,8},{1,9},{2,10},{3,11},{4,12},{5,13},{6,14},{7,15},{8,16},{9,17... | collective-permute-start | bytes 393224 | tf_op jit(solution)/shard_map/ppermute | solution.py:225
  47.5 12.3 %copy-start.11 = (bf16[512,128]{1,0:T(8,128)(2,1)}, bf16[512,128]{1,0:T(8,128)(2,1)S(1)}, u32[]{:S(2)}) copy-start(bf16[512,128]{1,0:T(8,128)(2,1)S(1)} %collective-permute-done.2.refs_3_) | copy-start | bytes 393220
  47.5 12.2 %collective-permute-start.7 = (bf16[512,128]{1,0:T(8,128)(2,1)}, bf16[512,128]{1,0:T(8,128)(2,1)S(1)}, u32[]{:S(2)}, u32[]{:S(2)}) collective-permute-start(bf16[512,128]{1,0:T(8,128)(2,1)} %get-tuple-element.31), channel_id=1, source_target_pairs={{0,9},{1,10},{2,11},{3,12},{4,13},{5,14},{6,15},{7,8},{8,17},{9,18... | collective-permute-start | bytes 393224 | tf_op jit(solution)/shard_map/ppermute | solution.py:225
  48.2 11.6 %copy-start.12 = (bf16[512,128]{1,0:T(8,128)(2,1)}, bf16[512,128]{1,0:T(8,128)(2,1)S(1)}, u32[]{:S(2)}) copy-start(bf16[512,128]{1,0:T(8,128)(2,1)S(1)} %collective-permute-done.3.refs_4_) | copy-start | bytes 393220
  48.2 11.6 %copy-start.13 = (bf16[512,128]{1,0:T(8,128)(2,1)}, bf16[512,128]{1,0:T(8,128)(2,1)S(1)}, u32[]{:S(2)}) copy-start(bf16[512,128]{1,0:T(8,128)(2,1)S(1)} %collective-permute-done.4.refs_5_) | copy-start | bytes 393220
  53.0 6.8 %copy-start.14 = (bf16[512,128]{1,0:T(8,128)(2,1)}, bf16[512,128]{1,0:T(8,128)(2,1)S(1)}, u32[]{:S(2)}) copy-start(bf16[512,128]{1,0:T(8,128)(2,1)S(1)} %collective-permute-done.5.refs_6_) | copy-start | bytes 393220
  57.6 2.2 %copy-start.15 = (bf16[512,128]{1,0:T(8,128)(2,1)}, bf16[512,128]{1,0:T(8,128)(2,1)S(1)}, u32[]{:S(2)}) copy-start(bf16[512,128]{1,0:T(8,128)(2,1)S(1)} %collective-permute-done.6.refs_7_) | copy-start | bytes 393220
  59.8 0.6 copy-start.16
  68.4 10.4 %collective-permute-start.8 = (bf16[128,512]{1,0:T(8,128)(2,1)}, bf16[128,512]{1,0:T(8,128)(2,1)S(1)}, u32[]{:S(2)}, u32[]{:S(2)}) collective-permute-start(bf16[128,512]{1,0:T(8,128)(2,1)} %get-tuple-element.33), channel_id=1, source_target_pairs={{127,0},{120,1},{121,2},{122,3},{123,4},{124,5},{125,6},{126,7},{7... | collective-permute-start | bytes 393224 | tf_op jit(solution)/shard_map/ppermute | solution.py:251
  68.4 12.0 %collective-permute-start.9 = (bf16[128,512]{1,0:T(8,128)(2,1)}, bf16[128,512]{1,0:T(8,128)(2,1)S(1)}, u32[]{:S(2)}, u32[]{:S(2)}) collective-permute-start(bf16[128,512]{1,0:T(8,128)(2,1)} %get-tuple-element.34), channel_id=1, source_target_pairs={{120,0},{121,1},{122,2},{123,3},{124,4},{125,5},{126,6},{127,7},{0... | collective-permute-start | bytes 393224 | tf_op jit(solution)/shard_map/ppermute | solution.py:251
  68.5 15.4 %collective-permute-start.10 = (bf16[128,512]{1,0:T(8,128)(2,1)}, bf16[128,512]{1,0:T(8,128)(2,1)S(1)}, u32[]{:S(2)}, u32[]{:S(2)}) collective-permute-start(bf16[128,512]{1,0:T(8,128)(2,1)} %get-tuple-element.35), channel_id=1, source_target_pairs={{121,0},{122,1},{123,2},{124,3},{125,4},{126,5},{127,6},{120,7},{1... | collective-permute-start | bytes 393224 | tf_op jit(solution)/shard_map/ppermute | solution.py:251
  68.6 15.3 %collective-permute-start.11 = (bf16[128,512]{1,0:T(8,128)(2,1)}, bf16[128,512]{1,0:T(8,128)(2,1)S(1)}, u32[]{:S(2)}, u32[]{:S(2)}) collective-permute-start(bf16[128,512]{1,0:T(8,128)(2,1)} %get-tuple-element.36), channel_id=1, source_target_pairs={{7,0},{0,1},{1,2},{2,3},{3,4},{4,5},{5,6},{6,7},{15,8},{8,9},{9,10... | collective-permute-start | bytes 393224 | tf_op jit(solution)/shard_map/ppermute | solution.py:251
  68.7 15.2 %collective-permute-start.12 = (bf16[128,512]{1,0:T(8,128)(2,1)}, bf16[128,512]{1,0:T(8,128)(2,1)S(1)}, u32[]{:S(2)}, u32[]{:S(2)}) collective-permute-start(bf16[128,512]{1,0:T(8,128)(2,1)} %get-tuple-element.37), channel_id=1, source_target_pairs={{1,0},{2,1},{3,2},{4,3},{5,4},{6,5},{7,6},{0,7},{9,8},{10,9},{11,1... | collective-permute-start | bytes 393224 | tf_op jit(solution)/shard_map/ppermute | solution.py:251
  78.8 12.4 %copy-start = (bf16[128,512]{1,0:T(8,128)(2,1)}, bf16[128,512]{1,0:T(8,128)(2,1)S(1)}, u32[]{:S(2)}) copy-start(bf16[128,512]{1,0:T(8,128)(2,1)S(1)} %collective-permute-done.8.refs_1_) | copy-start | bytes 393220
  78.8 5.9 %collective-permute-start.13 = (bf16[128,512]{1,0:T(8,128)(2,1)}, bf16[128,512]{1,0:T(8,128)(2,1)S(1)}, u32[]{:S(2)}, u32[]{:S(2)}) collective-permute-start(bf16[128,512]{1,0:T(8,128)(2,1)} %get-tuple-element.38), channel_id=1, source_target_pairs={{15,0},{8,1},{9,2},{10,3},{11,4},{12,5},{13,6},{14,7},{23,8},{16,9... | collective-permute-start | bytes 393224 | tf_op jit(solution)/shard_map/ppermute | solution.py:251
  80.4 10.8 %copy-start.1 = (bf16[128,512]{1,0:T(8,128)(2,1)}, bf16[128,512]{1,0:T(8,128)(2,1)S(1)}, u32[]{:S(2)}) copy-start(bf16[128,512]{1,0:T(8,128)(2,1)S(1)} %collective-permute-done.9.refs_2_) | copy-start | bytes 393220
  80.4 5.3 %collective-permute-start.14 = (bf16[128,512]{1,0:T(8,128)(2,1)}, bf16[128,512]{1,0:T(8,128)(2,1)S(1)}, u32[]{:S(2)}, u32[]{:S(2)}) collective-permute-start(bf16[128,512]{1,0:T(8,128)(2,1)} %get-tuple-element.39), channel_id=1, source_target_pairs={{8,0},{9,1},{10,2},{11,3},{12,4},{13,5},{14,6},{15,7},{16,8},{17,9... | collective-permute-start | bytes 393224 | tf_op jit(solution)/shard_map/ppermute | solution.py:251
  83.9 7.3 %copy-start.2 = (bf16[128,512]{1,0:T(8,128)(2,1)}, bf16[128,512]{1,0:T(8,128)(2,1)S(1)}, u32[]{:S(2)}) copy-start(bf16[128,512]{1,0:T(8,128)(2,1)S(1)} %collective-permute-done.10.refs_3_) | copy-start | bytes 393220
  83.9 7.3 %collective-permute-start.15 = (bf16[128,512]{1,0:T(8,128)(2,1)}, bf16[128,512]{1,0:T(8,128)(2,1)S(1)}, u32[]{:S(2)}, u32[]{:S(2)}) collective-permute-start(bf16[128,512]{1,0:T(8,128)(2,1)} %get-tuple-element.40), channel_id=1, source_target_pairs={{9,0},{10,1},{11,2},{12,3},{13,4},{14,5},{15,6},{8,7},{17,8},{18,9... | collective-permute-start | bytes 393224 | tf_op jit(solution)/shard_map/ppermute | solution.py:251
  83.9 7.3 %copy-start.3 = (bf16[128,512]{1,0:T(8,128)(2,1)}, bf16[128,512]{1,0:T(8,128)(2,1)S(1)}, u32[]{:S(2)}) copy-start(bf16[128,512]{1,0:T(8,128)(2,1)S(1)} %collective-permute-done.11.refs_4_) | copy-start | bytes 393220
  83.9 7.3 %copy-start.4 = (bf16[128,512]{1,0:T(8,128)(2,1)}, bf16[128,512]{1,0:T(8,128)(2,1)S(1)}, u32[]{:S(2)}) copy-start(bf16[128,512]{1,0:T(8,128)(2,1)S(1)} %collective-permute-done.12.refs_5_) | copy-start | bytes 393220
  84.7 6.5 %copy-start.5 = (bf16[128,512]{1,0:T(8,128)(2,1)}, bf16[128,512]{1,0:T(8,128)(2,1)S(1)}, u32[]{:S(2)}) copy-start(bf16[128,512]{1,0:T(8,128)(2,1)S(1)} %collective-permute-done.13.refs_6_) | copy-start | bytes 393220
  85.7 5.5 %copy-start.6 = (bf16[128,512]{1,0:T(8,128)(2,1)}, bf16[128,512]{1,0:T(8,128)(2,1)S(1)}, u32[]{:S(2)}) copy-start(bf16[128,512]{1,0:T(8,128)(2,1)S(1)} %collective-permute-done.14.refs_7_) | copy-start | bytes 393220
  91.2 0.6 copy-start.7

commit v2 on v1

--- a/solution.py
+++ b/solution.py
@@ -1,3 +1,5 @@
+import functools
+
 import jax
 import jax.numpy as jnp
 from jax import lax
@@ -30,27 +32,28 @@
     return (span == index_row).astype(jnp.bfloat16)
 
 
-def down_kernel(win_ref, off_ref, xt_ref, e_ref, w_ref, *refs):
-    n_groups = len(step_table)
-    outs = refs[: 1 + n_groups]
-    acc = refs[1 + n_groups]
-    step = pl.program_id(0)
-    per_step = e_ref.shape[0]
-
-    @pl.when(step == 0)
-    def _():
-        acc[...] = jnp.zeros_like(acc)
+def down_kernel(first_window, count_ref, order_ref, win_ref, off_ref, xt_ref, e_ref, w_ref, *refs):
+    outs = refs[:-1]
+    acc = refs[-1]
+    bricks = e_ref.shape[0]
+    trash = acc.shape[0] // WIN - 1
+    acc[...] = jnp.zeros_like(acc)
+    neighbours = count_ref[0]
+    if first_window == 0:
+        start, stop = neighbours, bricks
+    else:
+        start, stop = 0, neighbours
 
     def body(u, carry):
         results = []
         for t in range(UNROLL):
-            j = u * UNROLL + t
-            brick = step * per_step + j
-            window = win_ref[brick]
+            position = start + u * UNROLL + t
+            brick = order_ref[jnp.minimum(position, bricks - 1)]
+            window = jnp.where(position < stop, win_ref[brick] - first_window, trash)
             offset = off_ref[brick]
-            inside = jnp.bitwise_and(e_ref[pl.ds(j, 1), :], WIN - 1)
+            inside = jnp.bitwise_and(e_ref[pl.ds(brick, 1), :], WIN - 1)
             pick = one_hot_rows(inside)
-            cols = pl.ds(pl.multiple_of(j * BLK, BLK), BLK)
+            cols = pl.ds(pl.multiple_of(brick * BLK, BLK), BLK)
             summed = lax.dot_general(pick, xt_ref[:, cols], NT, preferred_element_type=jnp.float32)
             high, low = split_parts(summed)
             weights = w_ref[offset]
@@ -63,15 +66,10 @@
             acc[rows, :] += part
         return carry
 
-    lax.fori_loop(0, per_step // UNROLL, body, 0)
-
-    @pl.when(step == pl.num_programs(0) - 1)
-    def _():
-        outs[0][...] = acc[0:SELF_CAP, :].astype(jnp.bfloat16)
-        cap = outs[1].shape[0]
-        for g in range(n_groups):
-            start = SELF_CAP + g * cap
-            outs[1 + g][...] = acc[start : start + cap, :].astype(jnp.bfloat16)
+    lax.fori_loop(0, (stop - start + UNROLL - 1) // UNROLL, body, 0)
+    size = outs[0].shape[0]
+    for g, out in enumerate(outs):
+        out[...] = acc[g * size : (g + 1) * size, :].astype(out.dtype)
 
 
 def coarse_kernel(cw_ref, cells_ref, bias_ref, *refs):
@@ -198,28 +196,39 @@
     answer_shapes = [jax.ShapeDtypeStruct((s.shape[1], s.shape[0]), s.dtype) for s in part_shapes]
     whole = lambda shape: pl.BlockSpec(shape, lambda *idx: (0,) * len(shape))
 
-    down = pl.pallas_call(
-        down_kernel,
-        out_shape=part_shapes,
-        grid_spec=pltpu.PrefetchScalarGridSpec(
-            num_scalar_prefetch=2,
-            grid=(steps,),
-            in_specs=[
-                pl.BlockSpec((in_width, BRICKS_PER_STEP * BLK), lambda i, *_: (0, i)),
-                pl.BlockSpec((BRICKS_PER_STEP, BLK), lambda i, *_: (i, 0)),
-                whole(w_down.shape),
-            ],
-            out_specs=[whole(s.shape) for s in part_shapes],
-            scratch_shapes=[pltpu.VMEM((entries, out_width), jnp.float32)],
-        ),
-        compiler_params=pltpu.CompilerParams(dimension_semantics=("arbitrary",)),
-        cost_estimate=pl.CostEstimate(
-            flops=6 * fine_rows * in_width * out_width,
-            transcendentals=0,
-            bytes_accessed=fine_rows * (in_width * 2 + 4) + entries * out_width * 2,
-        ),
-    )
-    parts = down(brick_window, block_offset, xt, entry_rows, w_down)
+    is_far = (brick_window >= SELF_CAP // WIN).astype(jnp.int32)
+    far_count = jnp.sum(is_far)
+    far_rank = jnp.cumsum(is_far) - is_far
+    own_rank = jnp.cumsum(1 - is_far) - (1 - is_far)
+    position = jnp.where(is_far == 1, far_rank, far_count + own_rank)
+    brick_ids = jnp.arange(blocks, dtype=jnp.int32)
+    order = jnp.sum(
+        jnp.where(position[None, :] == brick_ids[:, None], brick_ids[None, :], 0), axis=1
+    ).astype(jnp.int32)
+    counts = far_count.reshape(1).astype(jnp.int32)
+
+    def down_call(first_window, shapes):
+        rows = sum(s.shape[0] for s in shapes)
+        return pl.pallas_call(
+            functools.partial(down_kernel, first_window),
+            out_shape=shapes,
+            grid_spec=pltpu.PrefetchScalarGridSpec(
+                num_scalar_prefetch=4,
+                grid=(1,),
+                in_specs=[whole(xt.shape), whole(entry_rows.shape), whole(w_down.shape)],
+                out_specs=[whole(s.shape) for s in shapes],
+                scratch_shapes=[pltpu.VMEM((rows + WIN, out_width), jnp.float32)],
+            ),
+            compiler_params=pltpu.CompilerParams(vmem_limit_bytes=48 * 1024 * 1024),
+            cost_estimate=pl.CostEstimate(
+                flops=3 * fine_rows * in_width * out_width,
+                transcendentals=0,
+                bytes_accessed=fine_rows * (in_width * 2 + 4) + rows * out_width * 2,
+            ),
+        )(counts, order, brick_window, block_offset, xt, entry_rows, w_down)
+
+    parts = [None] + list(down_call(SELF_CAP // WIN, part_shapes[1:]))
+    parts[0] = down_call(0, part_shapes[:1])[0]
 
     arrived = [
         lax.ppermute(parts[1 + g], ("outer", "inner"), group_route(g, 1)) for g in range(n_groups)

time: 109 us -> 111 us (1.018); the launches traced: 109 us -> 109 us
  waiting for transfers between devices: 37.3 us -> 11.3 us
  starting transfers between devices: 12.4 us -> 28.7 us
  local copies, waits for them, and re-layouts: 2.26 us -> 10.6 us
  other arithmetic: 1.35 us -> 2.92 us
    ppermute x8, starting transfers between devices: 1.92 us -> 17.1 us  [local(): lax.ppermute(answers[1 + g], ('outer', 'inner'), group_route(g, -1))]
    ppermute x8, waiting for transfers between devices: 16.5 us -> 2.09 us  [local(): lax.ppermute(parts[1 + g], ('outer', 'inner'), group_route(g, 1))]
    ppermute x8, waiting for transfers between devices: 20.8 us -> 9.17 us  [local(): lax.ppermute(answers[1 + g], ('outer', 'inner'), group_route(g, -1))]
    unnamed x34 -> x54, local copies, waits for them, and re-layouts: 1.25 us -> 9.21 us
    pallas_call x1 -> x2, Pallas kernels: 30.3 us -> 29.6 us  [down_call(): pl.pallas_call(functools.partial(down_kernel, first_window), out_shape=sh...]
  transfers between devices with their start and end apart: 16 -> 16, of which waited for: 12 -> 5; matrix products, arithmetic and copies ran while one was open for 1% -> 1% of each run, Pallas kernels for 0% -> 12%
where the time goes in v2:
time: 111 us; the launch traced here: 109 us
  Pallas kernels  54.9 us (49%)
  starting transfers between devices  28.7 us (26%)
  waiting for transfers between devices  11.3 us (10%)
  local copies, waits for them, and re-layouts  10.6 us (10%)
  other arithmetic  2.92 us (3%)
    pallas_call x2, Pallas kernels, down_call(): pl.pallas_call(functools.partial(down_kernel, first_window), out_shape=sh...  29.6 us
    pallas_call x1, Pallas kernels, local(): up(brick_window, block_offset, xt, entry_rows, w_up_t, answers[0], *retur...  17.3 us
    ppermute x8, starting transfers between devices, local(): lax.ppermute(answers[1 + g], ('outer', 'inner'), group_route(g, -1))  17.1 us
    ppermute x8, starting transfers between devices, local(): lax.ppermute(parts[1 + g], ('outer', 'inner'), group_route(g, 1))  11.6 us
    unnamed x54, local copies, waits for them, and re-layouts  9.21 us
    ppermute x8, waiting for transfers between devices, local(): lax.ppermute(answers[1 + g], ('outer', 'inner'), group_route(g, -1))  9.17 us
    pallas_call x1, Pallas kernels, local(): coarse(cell_window, cells, b_down.reshape(1, out_width), parts[0], *arrived)  8 us
  transfers between devices with their start and end apart: 16, of which 5 were waited for; matrix products, arithmetic and copies ran while one was open for 1% of the time, Pallas kernels for 12%

profile of v2, /device:TPU:24, one launch (start us, length us, event | category | flops | bytes accessed | tf_op | source)
XLA Modules:
  0.0 108.7 jit_solution(2029297881257368636)
XLA Ops:
  0.0 1.1 slice_reduce_fusion
  1.1 0.6 fusion.1
  1.8 0.3 reduce-window.24
  2.1 0.1 slice.20
  2.2 0.3 reduce-window.16
  2.5 0.1 slice.18
  2.6 0.1 slice_reduce_fusion.1
  2.8 0.7 compare_select_fusion
  3.5 0.1 select_reduce_fusion.order_ref
  3.6 0.0 copy-start
  3.6 2.2 %copy-done = bf16[32768,64]{0,1:T(8,128)(2,1)S(1)} copy-done((bf16[32768,64]{0,1:T(8,128)(2,1)S(1)}, bf16[32768,64]{0,1:T(8,128)(2,1)}, u32[]{:S(2)}) %copy-start) | copy-done | bytes 4194328
  5.8 0.9 copy-done.3
  6.7 0.9 copy-done.5
  7.6 0.7 copy-done.8
  8.3 16.5 %shard_map.74 = (bf16[512,128]{1,0:T(8,128)(2,1)S(1)}, bf16[512,128]{1,0:T(8,128)(2,1)S(1)}, bf16[512,128]{1,0:T(8,128)(2,1)S(1)}, bf16[512,128]{1,0:T(8,128)(2,...) custom-call(s32[1]{0:T(128)} %bitcast.5.count_ref, ...), custom_call_target="tpu_custom_call" | custom-call | flops 805306368 | bytes 5373952 | tf_op jit(solution)/shard_map/pallas_call | solution.py:212
  24.8 5.1 %collective-permute-start = (bf16[512,128]{1,0:T(8,128)(2,1)S(1)}, bf16[512,128]{1,0:T(8,128)(2,1)S(1)}, u32[]{:S(2)}, u32[]{:S(2)}) collective-permute-start(bf16[512,128]{1,0:T(8,128)(2,1)S(1)} %get-tuple-element.22), channel_id=1, source_target_pairs={{0,127},{1,120},{2,121},{3,122},{4,123},{5,124},{6,125},{7,126},{8... | collective-permute-start | bytes 393224 | tf_op jit(solution)/shard_map/ppermute | solution.py:234
  29.9 1.7 %collective-permute-start.1 = (bf16[512,128]{1,0:T(8,128)(2,1)S(1)}, bf16[512,128]{1,0:T(8,128)(2,1)S(1)}, u32[]{:S(2)}, u32[]{:S(2)}) collective-permute-start(bf16[512,128]{1,0:T(8,128)(2,1)S(1)} %get-tuple-element.23), channel_id=1, source_target_pairs={{0,120},{1,121},{2,122},{3,123},{4,124},{5,125},{6,126},{7,127},{8... | collective-permute-start | bytes 393224 | tf_op jit(solution)/shard_map/ppermute | solution.py:234
  31.5 0.0 collective-permute-start.2
  31.5 1.7 %collective-permute-start.3 = (bf16[512,128]{1,0:T(8,128)(2,1)S(1)}, bf16[512,128]{1,0:T(8,128)(2,1)S(1)}, u32[]{:S(2)}, u32[]{:S(2)}) collective-permute-start(bf16[512,128]{1,0:T(8,128)(2,1)S(1)} %get-tuple-element.25), channel_id=1, source_target_pairs={{0,7},{1,0},{2,1},{3,2},{4,3},{5,4},{6,5},{7,6},{8,15},{9,8},{10,9... | collective-permute-start | bytes 393224 | tf_op jit(solution)/shard_map/ppermute | solution.py:234
  33.3 1.7 %collective-permute-start.4 = (bf16[512,128]{1,0:T(8,128)(2,1)S(1)}, bf16[512,128]{1,0:T(8,128)(2,1)S(1)}, u32[]{:S(2)}, u32[]{:S(2)}) collective-permute-start(bf16[512,128]{1,0:T(8,128)(2,1)S(1)} %get-tuple-element.26), channel_id=1, source_target_pairs={{0,1},{1,2},{2,3},{3,4},{4,5},{5,6},{6,7},{7,0},{8,9},{9,10},{10,1... | collective-permute-start | bytes 393224 | tf_op jit(solution)/shard_map/ppermute | solution.py:234
  35.0 0.1 reduce_min.9
  35.1 0.0 collective-permute-done.refs_1_
  35.1 1.0 collective-permute-start.5
  36.1 0.0 collective-permute-done.1.refs_2_
  36.1 0.4 collective-permute-start.6
  36.5 2.1 %collective-permute-done.2.refs_3_ = bf16[512,128]{1,0:T(8,128)(2,1)S(1)} collective-permute-done((bf16[512,128]{1,0:T(8,128)(2,1)S(1)}, bf16[512,128]{1,0:T(8,128)(2,1)S(1)}, u32[]{:S(2)}, u32[]{:S(2)}) %collective-permute-start.2) | collective-permute-done | bytes 131104 | tf_op jit(solution)/shard_map/ppermute | solution.py:234
  38.6 0.0 collective-permute-start.7
  38.6 0.6 and_select_fusion.1.cw_ref
  39.2 0.0 copy-done.6
  39.2 2.2 %copy-done.1 = bf16[32768,64]{0,1:T(8,128)(2,1)S(1)} copy-done((bf16[32768,64]{0,1:T(8,128)(2,1)S(1)}, bf16[32768,64]{0,1:T(8,128)(2,1)}, u32[]{:S(2)}) %copy-start.1) | copy-done | bytes 4194328
  41.4 13.1 %shard_map.73.refs_0_ = bf16[4096,128]{1,0:T(8,128)(2,1)S(1)} custom-call(s32[1]{0:T(128)} %bitcast.5.count_ref, s32[256]{0:T(256)S(1)} %select_reduce_fusion.order_ref, s32[256]{0:T(256)S(1)} %get-tuple-element.40.win_ref, s32[256]{0:T(256)S(1)} %copy-done.9, bf16[64,32768]{1,0:T(8,128)(2,1)S(1)} %bitcast.31, s32[256,128]{1,0:T(8,128)S(1)} %bitcast.35, ...), custom_call_target="tpu_custom_call" | custom-call | flops 805306368 | bytes 5373952 | tf_op jit(solution)/shard_map/pallas_call | solution.py:212
  54.6 0.0 copy-start.2
  54.6 1.0 copy-done.2
  55.5 0.0 collective-permute-done.3.refs_4_
  55.5 0.0 collective-permute-done.4.refs_5_
  55.6 0.0 copy-start.23
  55.6 0.0 collective-permute-done.5.refs_6_
  55.6 0.0 collective-permute-done.6.refs_7_
  55.6 0.0 collective-permute-done.7.refs_8_
  55.6 0.0 copy-start.26
  55.7 0.5 copy-done.22
  56.2 0.1 copy-done.23
  56.3 0.0 copy-done.24
  56.3 0.1 copy-done.25
  56.4 0.0 copy-done.26
  56.4 8.0 %shard_map.75 = (bf16[128,4096]{1,0:T(8,128)(2,1)}, bf16[128,512]{1,0:T(8,128)(2,1)}, bf16[128,512]{1,0:T(8,128)(2,1)}, bf16[128,512]{1,0:T(8,128)(2,1)}, bf16[1...) custom-call(s32[64]{0:T(128)} %and_select_fusion.1.cw_ref, ...), custom_call_target="tpu_custom_call" | custom-call | flops 536870912 | bytes 4194304 | tf_op jit(solution)/shard_map/pallas_call | solution.py:257
  64.4 3.5 %collective-permute-start.8 = (bf16[128,512]{1,0:T(8,128)(2,1)}, bf16[128,512]{1,0:T(8,128)(2,1)S(1)}, u32[]{:S(2)}, u32[]{:S(2)}) collective-permute-start(bf16[128,512]{1,0:T(8,128)(2,1)} %get-tuple-element.31), channel_id=1, source_target_pairs={{127,0},{120,1},{121,2},{122,3},{123,4},{124,5},{125,6},{126,7},{7... | collective-permute-start | bytes 393224 | tf_op jit(solution)/shard_map/ppermute | solution.py:260
  67.9 2.3 %collective-permute-start.9 = (bf16[128,512]{1,0:T(8,128)(2,1)}, bf16[128,512]{1,0:T(8,128)(2,1)S(1)}, u32[]{:S(2)}, u32[]{:S(2)}) collective-permute-start(bf16[128,512]{1,0:T(8,128)(2,1)} %get-tuple-element.32), channel_id=1, source_target_pairs={{120,0},{121,1},{122,2},{123,3},{124,4},{125,5},{126,6},{127,7},{0... | collective-permute-start | bytes 393224 | tf_op jit(solution)/shard_map/ppermute | solution.py:260
  70.2 0.0 collective-permute-start.10
  70.2 1.3 %collective-permute-start.11 = (bf16[128,512]{1,0:T(8,128)(2,1)}, bf16[128,512]{1,0:T(8,128)(2,1)S(1)}, u32[]{:S(2)}, u32[]{:S(2)}) collective-permute-start(bf16[128,512]{1,0:T(8,128)(2,1)} %get-tuple-element.34), channel_id=1, source_target_pairs={{7,0},{0,1},{1,2},{2,3},{3,4},{4,5},{5,6},{6,7},{15,8},{8,9},{9,10... | collective-permute-start | bytes 393224 | tf_op jit(solution)/shard_map/ppermute | solution.py:260
  71.5 0.5 collective-permute-start.12
  71.9 2.6 %collective-permute-done.8.refs_1_ = bf16[128,512]{1,0:T(8,128)(2,1)S(1)} collective-permute-done((bf16[128,512]{1,0:T(8,128)(2,1)}, bf16[128,512]{1,0:T(8,128)(2,1)S(1)}, u32[]{:S(2)}, u32[]{:S(2)}) %collective-permute-start.8) | collective-permute-done | bytes 131104 | tf_op jit(solution)/shard_map/ppermute | solution.py:260
  74.6 5.1 %collective-permute-start.13 = (bf16[128,512]{1,0:T(8,128)(2,1)}, bf16[128,512]{1,0:T(8,128)(2,1)S(1)}, u32[]{:S(2)}, u32[]{:S(2)}) collective-permute-start(bf16[128,512]{1,0:T(8,128)(2,1)} %get-tuple-element.36), channel_id=1, source_target_pairs={{15,0},{8,1},{9,2},{10,3},{11,4},{12,5},{13,6},{14,7},{23,8},{16,9... | collective-permute-start | bytes 393224 | tf_op jit(solution)/shard_map/ppermute | solution.py:260
  79.6 1.4 %collective-permute-done.9.refs_2_ = bf16[128,512]{1,0:T(8,128)(2,1)S(1)} collective-permute-done((bf16[128,512]{1,0:T(8,128)(2,1)}, bf16[128,512]{1,0:T(8,128)(2,1)S(1)}, u32[]{:S(2)}, u32[]{:S(2)}) %collective-permute-start.9) | collective-permute-done | bytes 131104 | tf_op jit(solution)/shard_map/ppermute | solution.py:260
  81.0 1.7 %collective-permute-start.14 = (bf16[128,512]{1,0:T(8,128)(2,1)}, bf16[128,512]{1,0:T(8,128)(2,1)S(1)}, u32[]{:S(2)}, u32[]{:S(2)}) collective-permute-start(bf16[128,512]{1,0:T(8,128)(2,1)} %get-tuple-element.37), channel_id=1, source_target_pairs={{8,0},{9,1},{10,2},{11,3},{12,4},{13,5},{14,6},{15,7},{16,8},{17,9... | collective-permute-start | bytes 393224 | tf_op jit(solution)/shard_map/ppermute | solution.py:260
  82.7 0.0 collective-permute-done.10.refs_3_
  82.7 2.8 %collective-permute-start.15 = (bf16[128,512]{1,0:T(8,128)(2,1)}, bf16[128,512]{1,0:T(8,128)(2,1)S(1)}, u32[]{:S(2)}, u32[]{:S(2)}) collective-permute-start(bf16[128,512]{1,0:T(8,128)(2,1)} %get-tuple-element.38), channel_id=1, source_target_pairs={{9,0},{10,1},{11,2},{12,3},{13,4},{14,5},{15,6},{8,7},{17,8},{18,9... | collective-permute-start | bytes 393224 | tf_op jit(solution)/shard_map/ppermute | solution.py:260
  85.5 0.0 collective-permute-done.11.refs_4_
  85.6 0.0 collective-permute-done.12.refs_5_
  85.6 0.0 collective-permute-done.13.refs_6_
  85.6 2.0 %collective-permute-done.14.refs_7_ = bf16[128,512]{1,0:T(8,128)(2,1)S(1)} collective-permute-done((bf16[128,512]{1,0:T(8,128)(2,1)}, bf16[128,512]{1,0:T(8,128)(2,1)S(1)}, u32[]{:S(2)}, u32[]{:S(2)}) %collective-permute-start.14) | collective-permute-done | bytes 131104 | tf_op jit(solution)/shard_map/ppermute | solution.py:260
  87.6 3.1 %collective-permute-done.15.refs_8_ = bf16[128,512]{1,0:T(8,128)(2,1)S(1)} collective-permute-done((bf16[128,512]{1,0:T(8,128)(2,1)}, bf16[128,512]{1,0:T(8,128)(2,1)S(1)}, u32[]{:S(2)}, u32[]{:S(2)}) %collective-permute-start.15) | collective-permute-done | bytes 131104 | tf_op jit(solution)/shard_map/ppermute | solution.py:260
  90.8 0.6 copy-done.17
  91.4 17.3 %shard_map.76 = bf16[64,32768]{1,0:T(8,128)(2,1)} custom-call(s32[256]{0:T(256)} %copy-done.7, s32[256]{0:T(256)} %off_ref.5, bf16[64,32768]{1,0:T(8,128)(2,1)} %bitcast.29, s32[256,128]{1,0:T(8,128)} %bitcast.33, bf16[8,64,128]{2,1,0:T(8,128)(2,1)} %bitcast.36, bf16[128,4096]{1,0:T(8,128)(2,1)} %get-tuple-element.30.refs_0_, bf16[128,512]{1,0:T(8,128)(2,1)} %copy-done.10, ...), custom_call_target="tpu_custom_call" | custom-call | flops 1610612736 | bytes 10616832 | tf_op jit(solution)/shard_map/pallas_call | solution.py:288
  (41 shorter events, 0.2 us)
Async XLA Ops:
  0.0 39.2 %copy-start.4 = (s32[32768]{0:T(1024)S(1)}, s32[32768]{0:T(1024)}, u32[]{:S(2)}) copy-start(s32[32768]{0:T(1024)} %param.9) | copy-start | bytes 393220
  0.0 39.2 %copy-start.9 = (s32[256]{0:T(256)S(1)}, s32[256]{0:T(256)}, u32[]{:S(2)}) copy-start(s32[256]{0:T(256)} %off_ref.5) | copy-start | bytes 3076
  0.0 35.0 %copy-start.18 = (s32[1,8192]{1,0:T(1,128)S(1)}, s32[1,8192]{1,0:T(1,128)}, u32[]{:S(2)}) copy-start(s32[1,8192]{1,0:T(1,128)} %param.10) | copy-start | bytes 98308
  1.8 52.8 %copy-start.7 = (s32[256]{0:T(256)}, s32[256]{0:T(256)S(1)}, u32[]{:S(2)}) copy-start(s32[256]{0:T(256)S(1)} %get-tuple-element.40.win_ref) | copy-start | bytes 3076
  3.6 2.2 %copy-start = (bf16[32768,64]{0,1:T(8,128)(2,1)S(1)}, bf16[32768,64]{0,1:T(8,128)(2,1)}, u32[]{:S(2)}) copy-start(bf16[32768,64]{0,1:T(8,128)(2,1)} %param.7) | copy-start | bytes 12582916
  5.8 0.9 copy-start.3
  6.7 0.9 copy-start.5
  7.6 0.7 copy-start.8
  8.3 30.9 %copy-start.6 = (bf16[8,64,128]{2,1,0:T(8,128)(2,1)S(1)}, bf16[8,64,128]{2,1,0:T(8,128)(2,1)}, u32[]{:S(2)}) copy-start(bf16[8,64,128]{2,1,0:T(8,128)(2,1)} %w_ref.3) | copy-start | bytes 393220
  24.8 10.3 %collective-permute-start = (bf16[512,128]{1,0:T(8,128)(2,1)S(1)}, bf16[512,128]{1,0:T(8,128)(2,1)S(1)}, u32[]{:S(2)}, u32[]{:S(2)}) collective-permute-start(bf16[512,128]{1,0:T(8,128)(2,1)S(1)} %get-tuple-element.22), channel_id=1, source_target_pairs={{0,127},{1,120},{2,121},{3,122},{4,123},{5,124},{6,125},{7,126},{8... | collective-permute-start | bytes 393224 | tf_op jit(solution)/shard_map/ppermute | solution.py:234
  29.9 6.3 %collective-permute-start.1 = (bf16[512,128]{1,0:T(8,128)(2,1)S(1)}, bf16[512,128]{1,0:T(8,128)(2,1)S(1)}, u32[]{:S(2)}, u32[]{:S(2)}) collective-permute-start(bf16[512,128]{1,0:T(8,128)(2,1)S(1)} %get-tuple-element.23), channel_id=1, source_target_pairs={{0,120},{1,121},{2,122},{3,123},{4,124},{5,125},{6,126},{7,127},{8... | collective-permute-start | bytes 393224 | tf_op jit(solution)/shard_map/ppermute | solution.py:234
  31.5 7.0 %collective-permute-start.2 = (bf16[512,128]{1,0:T(8,128)(2,1)S(1)}, bf16[512,128]{1,0:T(8,128)(2,1)S(1)}, u32[]{:S(2)}, u32[]{:S(2)}) collective-permute-start(bf16[512,128]{1,0:T(8,128)(2,1)S(1)} %get-tuple-element.24), channel_id=1, source_target_pairs={{0,121},{1,122},{2,123},{3,124},{4,125},{5,126},{6,127},{7,120},{8... | collective-permute-start | bytes 393224 | tf_op jit(solution)/shard_map/ppermute | solution.py:234
  31.5 24.0 %collective-permute-start.3 = (bf16[512,128]{1,0:T(8,128)(2,1)S(1)}, bf16[512,128]{1,0:T(8,128)(2,1)S(1)}, u32[]{:S(2)}, u32[]{:S(2)}) collective-permute-start(bf16[512,128]{1,0:T(8,128)(2,1)S(1)} %get-tuple-element.25), channel_id=1, source_target_pairs={{0,7},{1,0},{2,1},{3,2},{4,3},{5,4},{6,5},{7,6},{8,15},{9,8},{10,9... | collective-permute-start | bytes 393224 | tf_op jit(solution)/shard_map/ppermute | solution.py:234
  33.3 22.3 %collective-permute-start.4 = (bf16[512,128]{1,0:T(8,128)(2,1)S(1)}, bf16[512,128]{1,0:T(8,128)(2,1)S(1)}, u32[]{:S(2)}, u32[]{:S(2)}) collective-permute-start(bf16[512,128]{1,0:T(8,128)(2,1)S(1)} %get-tuple-element.26), channel_id=1, source_target_pairs={{0,1},{1,2},{2,3},{3,4},{4,5},{5,6},{6,7},{7,0},{8,9},{9,10},{10,1... | collective-permute-start | bytes 393224 | tf_op jit(solution)/shard_map/ppermute | solution.py:234
  35.1 20.5 %copy-start.19 = (bf16[512,128]{1,0:T(8,128)(2,1)}, bf16[512,128]{1,0:T(8,128)(2,1)S(1)}, u32[]{:S(2)}) copy-start(bf16[512,128]{1,0:T(8,128)(2,1)S(1)} %collective-permute-done.refs_1_) | copy-start | bytes 393220
  35.1 20.5 %collective-permute-start.5 = (bf16[512,128]{1,0:T(8,128)(2,1)S(1)}, bf16[512,128]{1,0:T(8,128)(2,1)S(1)}, u32[]{:S(2)}, u32[]{:S(2)}) collective-permute-start(bf16[512,128]{1,0:T(8,128)(2,1)S(1)} %get-tuple-element.27), channel_id=1, source_target_pairs={{0,15},{1,8},{2,9},{3,10},{4,11},{5,12},{6,13},{7,14},{8,23},{9,16... | collective-permute-start | bytes 393224 | tf_op jit(solution)/shard_map/ppermute | solution.py:234
  36.1 19.5 %copy-start.20 = (bf16[512,128]{1,0:T(8,128)(2,1)}, bf16[512,128]{1,0:T(8,128)(2,1)S(1)}, u32[]{:S(2)}) copy-start(bf16[512,128]{1,0:T(8,128)(2,1)S(1)} %collective-permute-done.1.refs_2_) | copy-start | bytes 393220
  36.1 19.4 %collective-permute-start.6 = (bf16[512,128]{1,0:T(8,128)(2,1)S(1)}, bf16[512,128]{1,0:T(8,128)(2,1)S(1)}, u32[]{:S(2)}, u32[]{:S(2)}) collective-permute-start(bf16[512,128]{1,0:T(8,128)(2,1)S(1)} %get-tuple-element.28), channel_id=1, source_target_pairs={{0,8},{1,9},{2,10},{3,11},{4,12},{5,13},{6,14},{7,15},{8,16},{9,17... | collective-permute-start | bytes 393224 | tf_op jit(solution)/shard_map/ppermute | solution.py:234
  38.6 17.1 %copy-start.21 = (bf16[512,128]{1,0:T(8,128)(2,1)}, bf16[512,128]{1,0:T(8,128)(2,1)S(1)}, u32[]{:S(2)}) copy-start(bf16[512,128]{1,0:T(8,128)(2,1)S(1)} %collective-permute-done.2.refs_3_) | copy-start | bytes 393220
  38.6 17.0 %collective-permute-start.7 = (bf16[512,128]{1,0:T(8,128)(2,1)S(1)}, bf16[512,128]{1,0:T(8,128)(2,1)S(1)}, u32[]{:S(2)}, u32[]{:S(2)}) collective-permute-start(bf16[512,128]{1,0:T(8,128)(2,1)S(1)} %get-tuple-element.29), channel_id=1, source_target_pairs={{0,9},{1,10},{2,11},{3,12},{4,13},{5,14},{6,15},{7,8},{8,17},{9,18... | collective-permute-start | bytes 393224 | tf_op jit(solution)/shard_map/ppermute | solution.py:234
  39.2 2.2 %copy-start.1 = (bf16[32768,64]{0,1:T(8,128)(2,1)S(1)}, bf16[32768,64]{0,1:T(8,128)(2,1)}, u32[]{:S(2)}) copy-start(bf16[32768,64]{0,1:T(8,128)(2,1)} %param.7) | copy-start | bytes 12582916
  54.6 1.0 copy-start.2
  55.5 0.6 copy-start.22
  55.6 0.7 copy-start.23
  55.6 0.7 copy-start.24
  55.6 0.8 copy-start.25
  55.6 0.8 copy-start.26
  64.4 10.2 %collective-permute-start.8 = (bf16[128,512]{1,0:T(8,128)(2,1)}, bf16[128,512]{1,0:T(8,128)(2,1)S(1)}, u32[]{:S(2)}, u32[]{:S(2)}) collective-permute-start(bf16[128,512]{1,0:T(8,128)(2,1)} %get-tuple-element.31), channel_id=1, source_target_pairs={{127,0},{120,1},{121,2},{122,3},{123,4},{124,5},{125,6},{126,7},{7... | collective-permute-start | bytes 393224 | tf_op jit(solution)/shard_map/ppermute | solution.py:260
  67.9 13.2 %collective-permute-start.9 = (bf16[128,512]{1,0:T(8,128)(2,1)}, bf16[128,512]{1,0:T(8,128)(2,1)S(1)}, u32[]{:S(2)}, u32[]{:S(2)}) collective-permute-start(bf16[128,512]{1,0:T(8,128)(2,1)} %get-tuple-element.32), channel_id=1, source_target_pairs={{120,0},{121,1},{122,2},{123,3},{124,4},{125,5},{126,6},{127,7},{0... | collective-permute-start | bytes 393224 | tf_op jit(solution)/shard_map/ppermute | solution.py:260
  70.2 12.6 %collective-permute-start.10 = (bf16[128,512]{1,0:T(8,128)(2,1)}, bf16[128,512]{1,0:T(8,128)(2,1)S(1)}, u32[]{:S(2)}, u32[]{:S(2)}) collective-permute-start(bf16[128,512]{1,0:T(8,128)(2,1)} %get-tuple-element.33), channel_id=1, source_target_pairs={{121,0},{122,1},{123,2},{124,3},{125,4},{126,5},{127,6},{120,7},{1... | collective-permute-start | bytes 393224 | tf_op jit(solution)/shard_map/ppermute | solution.py:260
  70.2 15.4 %collective-permute-start.11 = (bf16[128,512]{1,0:T(8,128)(2,1)}, bf16[128,512]{1,0:T(8,128)(2,1)S(1)}, u32[]{:S(2)}, u32[]{:S(2)}) collective-permute-start(bf16[128,512]{1,0:T(8,128)(2,1)} %get-tuple-element.34), channel_id=1, source_target_pairs={{7,0},{0,1},{1,2},{2,3},{3,4},{4,5},{5,6},{6,7},{15,8},{8,9},{9,10... | collective-permute-start | bytes 393224 | tf_op jit(solution)/shard_map/ppermute | solution.py:260
  71.5 14.1 %collective-permute-start.12 = (bf16[128,512]{1,0:T(8,128)(2,1)}, bf16[128,512]{1,0:T(8,128)(2,1)S(1)}, u32[]{:S(2)}, u32[]{:S(2)}) collective-permute-start(bf16[128,512]{1,0:T(8,128)(2,1)} %get-tuple-element.35), channel_id=1, source_target_pairs={{1,0},{2,1},{3,2},{4,3},{5,4},{6,5},{7,6},{0,7},{9,8},{10,9},{11,1... | collective-permute-start | bytes 393224 | tf_op jit(solution)/shard_map/ppermute | solution.py:260
  74.6 16.2 %copy-start.10 = (bf16[128,512]{1,0:T(8,128)(2,1)}, bf16[128,512]{1,0:T(8,128)(2,1)S(1)}, u32[]{:S(2)}) copy-start(bf16[128,512]{1,0:T(8,128)(2,1)S(1)} %collective-permute-done.8.refs_1_) | copy-start | bytes 393220
  74.6 11.0 %collective-permute-start.13 = (bf16[128,512]{1,0:T(8,128)(2,1)}, bf16[128,512]{1,0:T(8,128)(2,1)S(1)}, u32[]{:S(2)}, u32[]{:S(2)}) collective-permute-start(bf16[128,512]{1,0:T(8,128)(2,1)} %get-tuple-element.36), channel_id=1, source_target_pairs={{15,0},{8,1},{9,2},{10,3},{11,4},{12,5},{13,6},{14,7},{23,8},{16,9... | collective-permute-start | bytes 393224 | tf_op jit(solution)/shard_map/ppermute | solution.py:260
  81.0 9.7 %copy-start.11 = (bf16[128,512]{1,0:T(8,128)(2,1)}, bf16[128,512]{1,0:T(8,128)(2,1)S(1)}, u32[]{:S(2)}) copy-start(bf16[128,512]{1,0:T(8,128)(2,1)S(1)} %collective-permute-done.9.refs_2_) | copy-start | bytes 393220
  81.0 6.6 %collective-permute-start.14 = (bf16[128,512]{1,0:T(8,128)(2,1)}, bf16[128,512]{1,0:T(8,128)(2,1)S(1)}, u32[]{:S(2)}, u32[]{:S(2)}) collective-permute-start(bf16[128,512]{1,0:T(8,128)(2,1)} %get-tuple-element.37), channel_id=1, source_target_pairs={{8,0},{9,1},{10,2},{11,3},{12,4},{13,5},{14,6},{15,7},{16,8},{17,9... | collective-permute-start | bytes 393224 | tf_op jit(solution)/shard_map/ppermute | solution.py:260
  82.7 8.0 %copy-start.12 = (bf16[128,512]{1,0:T(8,128)(2,1)}, bf16[128,512]{1,0:T(8,128)(2,1)S(1)}, u32[]{:S(2)}) copy-start(bf16[128,512]{1,0:T(8,128)(2,1)S(1)} %collective-permute-done.10.refs_3_) | copy-start | bytes 393220
  82.7 8.0 %collective-permute-start.15 = (bf16[128,512]{1,0:T(8,128)(2,1)}, bf16[128,512]{1,0:T(8,128)(2,1)S(1)}, u32[]{:S(2)}, u32[]{:S(2)}) collective-permute-start(bf16[128,512]{1,0:T(8,128)(2,1)} %get-tuple-element.38), channel_id=1, source_target_pairs={{9,0},{10,1},{11,2},{12,3},{13,4},{14,5},{15,6},{8,7},{17,8},{18,9... | collective-permute-start | bytes 393224 | tf_op jit(solution)/shard_map/ppermute | solution.py:260
  85.6 5.2 %copy-start.13 = (bf16[128,512]{1,0:T(8,128)(2,1)}, bf16[128,512]{1,0:T(8,128)(2,1)S(1)}, u32[]{:S(2)}) copy-start(bf16[128,512]{1,0:T(8,128)(2,1)S(1)} %collective-permute-done.11.refs_4_) | copy-start | bytes 393220
  85.6 5.2 %copy-start.14 = (bf16[128,512]{1,0:T(8,128)(2,1)}, bf16[128,512]{1,0:T(8,128)(2,1)S(1)}, u32[]{:S(2)}) copy-start(bf16[128,512]{1,0:T(8,128)(2,1)S(1)} %collective-permute-done.12.refs_5_) | copy-start | bytes 393220
  85.6 5.2 %copy-start.15 = (bf16[128,512]{1,0:T(8,128)(2,1)}, bf16[128,512]{1,0:T(8,128)(2,1)S(1)}, u32[]{:S(2)}) copy-start(bf16[128,512]{1,0:T(8,128)(2,1)S(1)} %collective-permute-done.13.refs_6_) | copy-start | bytes 393220
  87.6 3.1 %copy-start.16 = (bf16[128,512]{1,0:T(8,128)(2,1)}, bf16[128,512]{1,0:T(8,128)(2,1)S(1)}, u32[]{:S(2)}) copy-start(bf16[128,512]{1,0:T(8,128)(2,1)S(1)} %collective-permute-done.14.refs_7_) | copy-start | bytes 393220
  90.7 0.7 copy-start.17

commit v3 on v2

--- a/solution.py
+++ b/solution.py
@@ -35,12 +35,17 @@
 def down_kernel(first_window, count_ref, order_ref, win_ref, off_ref, xt_ref, e_ref, w_ref, *refs):
     outs = refs[:-1]
     acc = refs[-1]
-    bricks = e_ref.shape[0]
+    step = pl.program_id(0)
+    per_step = e_ref.shape[0]
     trash = acc.shape[0] // WIN - 1
-    acc[...] = jnp.zeros_like(acc)
-    neighbours = count_ref[0]
+
+    @pl.when(step == 0)
+    def _():
+        acc[...] = jnp.zeros_like(acc)
+
+    neighbours = count_ref[step]
     if first_window == 0:
-        start, stop = neighbours, bricks
+        start, stop = neighbours, per_step
     else:
         start, stop = 0, neighbours
 
@@ -48,18 +53,15 @@
         results = []
         for t in range(UNROLL):
             position = start + u * UNROLL + t
-            brick = order_ref[jnp.minimum(position, bricks - 1)]
+            j = order_ref[step * per_step + jnp.minimum(position, per_step - 1)]
+            brick = step * per_step + j
             window = jnp.where(position < stop, win_ref[brick] - first_window, trash)
             offset = off_ref[brick]
-            inside = jnp.bitwise_and(e_ref[pl.ds(brick, 1), :], WIN - 1)
+            inside = jnp.bitwise_and(e_ref[pl.ds(j, 1), :], WIN - 1)
             pick = one_hot_rows(inside)
-            cols = pl.ds(pl.multiple_of(brick * BLK, BLK), BLK)
+            cols = pl.ds(pl.multiple_of(j * BLK, BLK), BLK)
             summed = lax.dot_general(pick, xt_ref[:, cols], NT, preferred_element_type=jnp.float32)
-            high, low = split_parts(summed)
-            weights = w_ref[offset]
-            part = jnp.dot(high, weights, preferred_element_type=jnp.float32) + jnp.dot(
-                low, weights, preferred_element_type=jnp.float32
-            )
+            part = jnp.dot(summed.astype(jnp.bfloat16), w_ref[offset], preferred_element_type=jnp.float32)
             results.append((window, part))
         for window, part in results:
             rows = pl.ds(pl.multiple_of(window * WIN, WIN), WIN)
@@ -67,9 +69,12 @@
         return carry
 
     lax.fori_loop(0, (stop - start + UNROLL - 1) // UNROLL, body, 0)
-    size = outs[0].shape[0]
-    for g, out in enumerate(outs):
-        out[...] = acc[g * size : (g + 1) * size, :].astype(out.dtype)
+
+    @pl.when(step == pl.num_programs(0) - 1)
+    def _():
+        size = outs[0].shape[0]
+        for g, out in enumerate(outs):
+            out[...] = acc[g * size : (g + 1) * size, :].astype(out.dtype)
 
 
 def coarse_kernel(cw_ref, cells_ref, bias_ref, *refs):
@@ -196,16 +201,17 @@
     answer_shapes = [jax.ShapeDtypeStruct((s.shape[1], s.shape[0]), s.dtype) for s in part_shapes]
     whole = lambda shape: pl.BlockSpec(shape, lambda *idx: (0,) * len(shape))
 
-    is_far = (brick_window >= SELF_CAP // WIN).astype(jnp.int32)
-    far_count = jnp.sum(is_far)
-    far_rank = jnp.cumsum(is_far) - is_far
-    own_rank = jnp.cumsum(1 - is_far) - (1 - is_far)
-    position = jnp.where(is_far == 1, far_rank, far_count + own_rank)
-    brick_ids = jnp.arange(blocks, dtype=jnp.int32)
+    is_far = (brick_window >= SELF_CAP // WIN).astype(jnp.int32).reshape(steps, BRICKS_PER_STEP)
+    far_count = jnp.sum(is_far, axis=1)
+    far_rank = jnp.cumsum(is_far, axis=1) - is_far
+    own_rank = jnp.cumsum(1 - is_far, axis=1) - (1 - is_far)
+    position = jnp.where(is_far == 1, far_rank, far_count[:, None] + own_rank)
+    local_ids = jnp.arange(BRICKS_PER_STEP, dtype=jnp.int32)
     order = jnp.sum(
-        jnp.where(position[None, :] == brick_ids[:, None], brick_ids[None, :], 0), axis=1
-    ).astype(jnp.int32)
-    counts = far_count.reshape(1).astype(jnp.int32)
+        jnp.where(position[:, None, :] == local_ids[None, :, None], local_ids[None, None, :], 0), axis=2
+    )
+    order = order.reshape(blocks).astype(jnp.int32)
+    counts = far_count.astype(jnp.int32)
 
     def down_call(first_window, shapes):
         rows = sum(s.shape[0] for s in shapes)
@@ -214,14 +220,18 @@
             out_shape=shapes,
             grid_spec=pltpu.PrefetchScalarGridSpec(
                 num_scalar_prefetch=4,
-                grid=(1,),
-                in_specs=[whole(xt.shape), whole(entry_rows.shape), whole(w_down.shape)],
+                grid=(steps,),
+                in_specs=[
+                    pl.BlockSpec((in_width, BRICKS_PER_STEP * BLK), lambda i, *_: (0, i)),
+                    pl.BlockSpec((BRICKS_PER_STEP, BLK), lambda i, *_: (i, 0)),
+                    whole(w_down.shape),
+                ],
                 out_specs=[whole(s.shape) for s in shapes],
                 scratch_shapes=[pltpu.VMEM((rows + WIN, out_width), jnp.float32)],
             ),
-            compiler_params=pltpu.CompilerParams(vmem_limit_bytes=48 * 1024 * 1024),
+            compiler_params=pltpu.CompilerParams(dimension_semantics=("arbitrary",)),
             cost_estimate=pl.CostEstimate(
-                flops=3 * fine_rows * in_width * out_width,
+                flops=2 * fine_rows * in_width * out_width,
                 transcendentals=0,
                 bytes_accessed=fine_rows * (in_width * 2 + 4) + rows * out_width * 2,
             ),

time: 111 us -> 98.9 us (0.89); the launches traced: 109 us -> 97.7 us
  local copies, waits for them, and re-layouts: 10.6 us -> 3.15 us
  waiting for transfers between devices: 11.3 us -> 16.2 us
  starting transfers between devices: 28.7 us -> 24.1 us
  Pallas kernels: 54.9 us -> 51.9 us
    unnamed x54 -> x36, local copies, waits for them, and re-layouts: 9.21 us -> 1.41 us
    ppermute x8, starting transfers between devices: 17.1 us -> 10.6 us  [local(): lax.ppermute(answers[1 + g], ('outer', 'inner'), group_route(g, -1))]
    ppermute x8, waiting for transfers between devices: 9.17 us -> 13.8 us  [local(): lax.ppermute(answers[1 + g], ('outer', 'inner'), group_route(g, -1))]
    pallas_call x2, Pallas kernels: 29.6 us -> 26.7 us  [down_call(): pl.pallas_call(functools.partial(down_kernel, first_window), out_shape=sh...]
    ppermute x8, starting transfers between devices: 11.6 us -> 13.5 us  [local(): lax.ppermute(parts[1 + g], ('outer', 'inner'), group_route(g, 1))]
  transfers between devices with their start and end apart: 16 -> 16, of which waited for: 5 -> 6; matrix products, arithmetic and copies ran while one was open for 1% -> 1% of each run, Pallas kernels for 12% -> 14%
where the time goes in v3:
time: 98.9 us; the launch traced here: 97.7 us
  Pallas kernels  51.9 us (52%)
  starting transfers between devices  24.1 us (24%)
  waiting for transfers between devices  16.2 us (16%)
  local copies, waits for them, and re-layouts  3.15 us (3%)
  other arithmetic  2.1 us (2%)
    pallas_call x2, Pallas kernels, down_call(): pl.pallas_call(functools.partial(down_kernel, first_window), out_shape=sh...  26.7 us
    pallas_call x1, Pallas kernels, local(): up(brick_window, block_offset, xt, entry_rows, w_up_t, answers[0], *retur...  17.3 us
    ppermute x8, waiting for transfers between devices, local(): lax.ppermute(answers[1 + g], ('outer', 'inner'), group_route(g, -1))  13.8 us
    ppermute x8, starting transfers between devices, local(): lax.ppermute(parts[1 + g], ('outer', 'inner'), group_route(g, 1))  13.5 us
    ppermute x8, starting transfers between devices, local(): lax.ppermute(answers[1 + g], ('outer', 'inner'), group_route(g, -1))  10.6 us
    pallas_call x1, Pallas kernels, local(): coarse(cell_window, cells, b_down.reshape(1, out_width), parts[0], *arrived)  7.98 us
    ppermute x8, waiting for transfers between devices, local(): lax.ppermute(parts[1 + g], ('outer', 'inner'), group_route(g, 1))  2.45 us
  transfers between devices with their start and end apart: 16, of which 6 were waited for; matrix products, arithmetic and copies ran while one was open for 1% of the time, Pallas kernels for 14%

profile of v3, /device:TPU:24, one launch (start us, length us, event | category | flops | bytes accessed | tf_op | source)
XLA Modules:
  0.0 97.7 jit_solution(16505194390550597005)
XLA Ops:
  0.0 1.0 %slice_reduce_fusion = s32[256]{0:T(256)S(1)} fusion(s32[256,128]{1,0:T(8,128)} %bitcast.9), kind=kLoop, calls=%fused_computation | loop fusion | bytes 2048 | tf_op jit(solution)/shard_map/slice | solution.py:193
  1.0 0.6 and_select_fusion.1.win_ref
  1.6 0.1 squeeze.6
  1.7 0.1 convert_reduce_fusion.count_ref
  1.9 0.2 reduce_window_sum.18
  2.0 0.2 reduce_window_sum.17
  2.2 0.1 fusion.2
  2.3 0.2 select_reduce_fusion
  2.5 0.7 reshape.114.order_ref
  3.2 0.0 copy-done.17
  3.2 13.1 %shard_map.74 = (bf16[512,128]{1,0:T(8,128)(2,1)}, bf16[512,128]{1,0:T(8,128)(2,1)}, bf16[512,128]{1,0:T(8,128)(2,1)}, bf16[512,128]{1,0:T(8,128)(2,1)}, bf16[51...) custom-call(s32[8]{0:T(128)} %copy-done.17, ...), custom_call_target="tpu_custom_call" | custom-call | flops 536870912 | bytes 5373952 | tf_op jit(solution)/shard_map/pallas_call | solution.py:218
  16.3 5.3 %collective-permute-start = (bf16[512,128]{1,0:T(8,128)(2,1)}, bf16[512,128]{1,0:T(8,128)(2,1)S(1)}, u32[]{:S(2)}, u32[]{:S(2)}) collective-permute-start(bf16[512,128]{1,0:T(8,128)(2,1)} %get-tuple-element.22), channel_id=1, source_target_pairs={{0,127},{1,120},{2,121},{3,122},{4,123},{5,124},{6,125},{7,126},{8... | collective-permute-start | bytes 393224 | tf_op jit(solution)/shard_map/ppermute | solution.py:244
  21.6 2.4 %collective-permute-start.1 = (bf16[512,128]{1,0:T(8,128)(2,1)}, bf16[512,128]{1,0:T(8,128)(2,1)S(1)}, u32[]{:S(2)}, u32[]{:S(2)}) collective-permute-start(bf16[512,128]{1,0:T(8,128)(2,1)} %get-tuple-element.23), channel_id=1, source_target_pairs={{0,120},{1,121},{2,122},{3,123},{4,124},{5,125},{6,126},{7,127},{8... | collective-permute-start | bytes 393224 | tf_op jit(solution)/shard_map/ppermute | solution.py:244
  24.0 0.0 collective-permute-start.2
  24.0 1.2 %collective-permute-start.3 = (bf16[512,128]{1,0:T(8,128)(2,1)}, bf16[512,128]{1,0:T(8,128)(2,1)S(1)}, u32[]{:S(2)}, u32[]{:S(2)}) collective-permute-start(bf16[512,128]{1,0:T(8,128)(2,1)} %get-tuple-element.25), channel_id=1, source_target_pairs={{0,7},{1,0},{2,1},{3,2},{4,3},{5,4},{6,5},{7,6},{8,15},{9,8},{10,9... | collective-permute-start | bytes 393224 | tf_op jit(solution)/shard_map/ppermute | solution.py:244
  25.2 0.9 collective-permute-start.4
  26.1 0.0 copy-done.8
  26.1 0.1 reduce_min.9
  26.2 0.0 collective-permute-done.refs_1_
  26.2 0.0 copy-start.9
  26.2 2.4 %collective-permute-start.5 = (bf16[512,128]{1,0:T(8,128)(2,1)}, bf16[512,128]{1,0:T(8,128)(2,1)S(1)}, u32[]{:S(2)}, u32[]{:S(2)}) collective-permute-start(bf16[512,128]{1,0:T(8,128)(2,1)} %get-tuple-element.27), channel_id=1, source_target_pairs={{0,15},{1,8},{2,9},{3,10},{4,11},{5,12},{6,13},{7,14},{8,23},{9,16... | collective-permute-start | bytes 393224 | tf_op jit(solution)/shard_map/ppermute | solution.py:244
  28.6 0.0 collective-permute-done.1.refs_2_
  28.6 0.0 collective-permute-start.6
  28.6 2.4 %collective-permute-done.2.refs_3_ = bf16[512,128]{1,0:T(8,128)(2,1)S(1)} collective-permute-done((bf16[512,128]{1,0:T(8,128)(2,1)}, bf16[512,128]{1,0:T(8,128)(2,1)S(1)}, u32[]{:S(2)}, u32[]{:S(2)}) %collective-permute-start.2) | collective-permute-done | bytes 131104 | tf_op jit(solution)/shard_map/ppermute | solution.py:244
  31.0 1.3 %collective-permute-start.7 = (bf16[512,128]{1,0:T(8,128)(2,1)}, bf16[512,128]{1,0:T(8,128)(2,1)S(1)}, u32[]{:S(2)}, u32[]{:S(2)}) collective-permute-start(bf16[512,128]{1,0:T(8,128)(2,1)} %get-tuple-element.29), channel_id=1, source_target_pairs={{0,9},{1,10},{2,11},{3,12},{4,13},{5,14},{6,15},{7,8},{8,17},{9,18... | collective-permute-start | bytes 393224 | tf_op jit(solution)/shard_map/ppermute | solution.py:244
  32.3 0.6 and_select_fusion.cw_ref
  32.9 13.6 %shard_map.73.refs_0_ = bf16[4096,128]{1,0:T(8,128)(2,1)} custom-call(s32[8]{0:T(128)} %copy-done.17, s32[256]{0:T(256)} %reshape.114.order_ref, s32[256]{0:T(256)} %and_select_fusion.1.win_ref, s32[256]{0:T(256)} %off_ref.5, bf16[64,32768]{1,0:T(8,128)(2,1)} %bitcast.7, s32[256,128]{1,0:T(8,128)} %bitcast.11, bf16[8,64,128]{2,1,0:T(8,128)(2,1)} %w_ref.3), custom_call_target="tpu_custom_call" | custom-call | flops 536870912 | bytes 5373952 | tf_op jit(solution)/shard_map/pallas_call | solution.py:218
  46.5 0.0 collective-permute-done.3.refs_4_
  46.5 0.0 collective-permute-done.4.refs_5_
  46.5 0.0 copy-start.13
  46.5 0.0 collective-permute-done.5.refs_6_
  46.5 0.0 copy-start.14
  46.5 0.0 collective-permute-done.6.refs_7_
  46.5 0.0 copy-start.15
  46.6 0.0 collective-permute-done.7.refs_8_
  46.6 0.0 copy-start.16
  46.6 0.0 copy-done.9
  46.6 0.5 copy-done.12
  47.1 0.1 copy-done.13
  47.2 0.1 copy-done.14
  47.3 0.0 copy-done.15
  47.3 0.0 copy-done.16
  47.4 8.0 %shard_map.75 = (bf16[128,4096]{1,0:T(8,128)(2,1)}, bf16[128,512]{1,0:T(8,128)(2,1)}, bf16[128,512]{1,0:T(8,128)(2,1)}, bf16[128,512]{1,0:T(8,128)(2,1)}, bf16[1...) custom-call(s32[64]{0:T(128)} %and_select_fusion.cw_ref, ...), custom_call_target="tpu_custom_call" | custom-call | flops 536870912 | bytes 4194304 | tf_op jit(solution)/shard_map/pallas_call | solution.py:267
  55.3 2.1 %collective-permute-start.8 = (bf16[128,512]{1,0:T(8,128)(2,1)}, bf16[128,512]{1,0:T(8,128)(2,1)S(1)}, u32[]{:S(2)}, u32[]{:S(2)}) collective-permute-start(bf16[128,512]{1,0:T(8,128)(2,1)} %get-tuple-element.31), channel_id=1, source_target_pairs={{127,0},{120,1},{121,2},{122,3},{123,4},{124,5},{125,6},{126,7},{7... | collective-permute-start | bytes 393224 | tf_op jit(solution)/shard_map/ppermute | solution.py:270
  57.5 2.6 %collective-permute-start.9 = (bf16[128,512]{1,0:T(8,128)(2,1)}, bf16[128,512]{1,0:T(8,128)(2,1)S(1)}, u32[]{:S(2)}, u32[]{:S(2)}) collective-permute-start(bf16[128,512]{1,0:T(8,128)(2,1)} %get-tuple-element.32), channel_id=1, source_target_pairs={{120,0},{121,1},{122,2},{123,3},{124,4},{125,5},{126,6},{127,7},{0... | collective-permute-start | bytes 393224 | tf_op jit(solution)/shard_map/ppermute | solution.py:270
  60.1 0.0 collective-permute-start.10
  60.1 0.1 collective-permute-start.11
  60.3 1.6 %collective-permute-start.12 = (bf16[128,512]{1,0:T(8,128)(2,1)}, bf16[128,512]{1,0:T(8,128)(2,1)S(1)}, u32[]{:S(2)}, u32[]{:S(2)}) collective-permute-start(bf16[128,512]{1,0:T(8,128)(2,1)} %get-tuple-element.35), channel_id=1, source_target_pairs={{1,0},{2,1},{3,2},{4,3},{5,4},{6,5},{7,6},{0,7},{9,8},{10,9},{11,1... | collective-permute-start | bytes 393224 | tf_op jit(solution)/shard_map/ppermute | solution.py:270
  61.9 3.3 %collective-permute-done.8.refs_1_ = bf16[128,512]{1,0:T(8,128)(2,1)S(1)} collective-permute-done((bf16[128,512]{1,0:T(8,128)(2,1)}, bf16[128,512]{1,0:T(8,128)(2,1)S(1)}, u32[]{:S(2)}, u32[]{:S(2)}) %collective-permute-start.8) | collective-permute-done | bytes 131104 | tf_op jit(solution)/shard_map/ppermute | solution.py:270
  65.2 2.8 %collective-permute-start.13 = (bf16[128,512]{1,0:T(8,128)(2,1)}, bf16[128,512]{1,0:T(8,128)(2,1)S(1)}, u32[]{:S(2)}, u32[]{:S(2)}) collective-permute-start(bf16[128,512]{1,0:T(8,128)(2,1)} %get-tuple-element.36), channel_id=1, source_target_pairs={{15,0},{8,1},{9,2},{10,3},{11,4},{12,5},{13,6},{14,7},{23,8},{16,9... | collective-permute-start | bytes 393224 | tf_op jit(solution)/shard_map/ppermute | solution.py:270
  68.0 3.4 %collective-permute-done.9.refs_2_ = bf16[128,512]{1,0:T(8,128)(2,1)S(1)} collective-permute-done((bf16[128,512]{1,0:T(8,128)(2,1)}, bf16[128,512]{1,0:T(8,128)(2,1)S(1)}, u32[]{:S(2)}, u32[]{:S(2)}) %collective-permute-start.9) | collective-permute-done | bytes 131104 | tf_op jit(solution)/shard_map/ppermute | solution.py:270
  71.3 0.0 collective-permute-start.14
  71.3 1.3 %collective-permute-done.10.refs_3_ = bf16[128,512]{1,0:T(8,128)(2,1)S(1)} collective-permute-done((bf16[128,512]{1,0:T(8,128)(2,1)}, bf16[128,512]{1,0:T(8,128)(2,1)S(1)}, u32[]{:S(2)}, u32[]{:S(2)}) %collective-permute-start.10) | collective-permute-done | bytes 131104 | tf_op jit(solution)/shard_map/ppermute | solution.py:270
  72.6 1.3 %collective-permute-start.15 = (bf16[128,512]{1,0:T(8,128)(2,1)}, bf16[128,512]{1,0:T(8,128)(2,1)S(1)}, u32[]{:S(2)}, u32[]{:S(2)}) collective-permute-start(bf16[128,512]{1,0:T(8,128)(2,1)} %get-tuple-element.38), channel_id=1, source_target_pairs={{9,0},{10,1},{11,2},{12,3},{13,4},{14,5},{15,6},{8,7},{17,8},{18,9... | collective-permute-start | bytes 393224 | tf_op jit(solution)/shard_map/ppermute | solution.py:270
  73.9 0.0 collective-permute-done.11.refs_4_
  73.9 0.0 collective-permute-done.12.refs_5_
  73.9 0.0 copy-start.4
  74.0 0.0 collective-permute-done.13.refs_6_
  74.0 4.0 %collective-permute-done.14.refs_7_ = bf16[128,512]{1,0:T(8,128)(2,1)S(1)} collective-permute-done((bf16[128,512]{1,0:T(8,128)(2,1)}, bf16[128,512]{1,0:T(8,128)(2,1)S(1)}, u32[]{:S(2)}, u32[]{:S(2)}) %collective-permute-start.14) | collective-permute-done | bytes 131104 | tf_op jit(solution)/shard_map/ppermute | solution.py:270
  78.0 1.8 %collective-permute-done.15.refs_8_ = bf16[128,512]{1,0:T(8,128)(2,1)S(1)} collective-permute-done((bf16[128,512]{1,0:T(8,128)(2,1)}, bf16[128,512]{1,0:T(8,128)(2,1)S(1)}, u32[]{:S(2)}, u32[]{:S(2)}) %collective-permute-start.15) | collective-permute-done | bytes 131104 | tf_op jit(solution)/shard_map/ppermute | solution.py:270
  79.8 0.0 copy-done
  79.8 0.0 copy-done.2
  79.8 0.6 copy-done.7
  80.4 17.3 %shard_map.76 = bf16[64,32768]{1,0:T(8,128)(2,1)} custom-call(s32[256]{0:T(256)} %and_select_fusion.1.win_ref, s32[256]{0:T(256)} %off_ref.5, bf16[64,32768]{1,0:T(8,128)(2,1)} %bitcast.8, s32[256,128]{1,0:T(8,128)} %bitcast.12, bf16[8,64,128]{2,1,0:T(8,128)(2,1)} %bitcast.13, bf16[128,4096]{1,0:T(8,128)(2,1)} %get-tuple-element.30.refs_0_, ...), custom_call_target="tpu_custom_call" | custom-call | flops 1610612736 | bytes 10616832 | tf_op jit(solution)/shard_map/pallas_call | solution.py:298
  (21 shorter events, 0.1 us)
Async XLA Ops:
  0.0 26.1 %copy-start.8 = (s32[1,8192]{1,0:T(1,128)S(1)}, s32[1,8192]{1,0:T(1,128)}, u32[]{:S(2)}) copy-start(s32[1,8192]{1,0:T(1,128)} %param.10) | copy-start | bytes 98308
  1.8 1.3 %copy-start.17 = (s32[8]{0:T(128)}, s32[8]{0:T(128)S(1)}, u32[]{:S(2)}) copy-start(s32[8]{0:T(128)S(1)} %convert_reduce_fusion.count_ref) | copy-start | bytes 100
  16.3 9.9 %collective-permute-start = (bf16[512,128]{1,0:T(8,128)(2,1)}, bf16[512,128]{1,0:T(8,128)(2,1)S(1)}, u32[]{:S(2)}, u32[]{:S(2)}) collective-permute-start(bf16[512,128]{1,0:T(8,128)(2,1)} %get-tuple-element.22), channel_id=1, source_target_pairs={{0,127},{1,120},{2,121},{3,122},{4,123},{5,124},{6,125},{7,126},{8... | collective-permute-start | bytes 393224 | tf_op jit(solution)/shard_map/ppermute | solution.py:244
  21.6 6.9 %collective-permute-start.1 = (bf16[512,128]{1,0:T(8,128)(2,1)}, bf16[512,128]{1,0:T(8,128)(2,1)S(1)}, u32[]{:S(2)}, u32[]{:S(2)}) collective-permute-start(bf16[512,128]{1,0:T(8,128)(2,1)} %get-tuple-element.23), channel_id=1, source_target_pairs={{0,120},{1,121},{2,122},{3,123},{4,124},{5,125},{6,126},{7,127},{8... | collective-permute-start | bytes 393224 | tf_op jit(solution)/shard_map/ppermute | solution.py:244
  24.0 7.0 %collective-permute-start.2 = (bf16[512,128]{1,0:T(8,128)(2,1)}, bf16[512,128]{1,0:T(8,128)(2,1)S(1)}, u32[]{:S(2)}, u32[]{:S(2)}) collective-permute-start(bf16[512,128]{1,0:T(8,128)(2,1)} %get-tuple-element.24), channel_id=1, source_target_pairs={{0,121},{1,122},{2,123},{3,124},{4,125},{5,126},{6,127},{7,120},{8... | collective-permute-start | bytes 393224 | tf_op jit(solution)/shard_map/ppermute | solution.py:244
  24.0 22.5 %collective-permute-start.3 = (bf16[512,128]{1,0:T(8,128)(2,1)}, bf16[512,128]{1,0:T(8,128)(2,1)S(1)}, u32[]{:S(2)}, u32[]{:S(2)}) collective-permute-start(bf16[512,128]{1,0:T(8,128)(2,1)} %get-tuple-element.25), channel_id=1, source_target_pairs={{0,7},{1,0},{2,1},{3,2},{4,3},{5,4},{6,5},{7,6},{8,15},{9,8},{10,9... | collective-permute-start | bytes 393224 | tf_op jit(solution)/shard_map/ppermute | solution.py:244
  25.2 21.3 %collective-permute-start.4 = (bf16[512,128]{1,0:T(8,128)(2,1)}, bf16[512,128]{1,0:T(8,128)(2,1)S(1)}, u32[]{:S(2)}, u32[]{:S(2)}) collective-permute-start(bf16[512,128]{1,0:T(8,128)(2,1)} %get-tuple-element.26), channel_id=1, source_target_pairs={{0,1},{1,2},{2,3},{3,4},{4,5},{5,6},{6,7},{7,0},{8,9},{9,10},{10,1... | collective-permute-start | bytes 393224 | tf_op jit(solution)/shard_map/ppermute | solution.py:244
  26.2 20.4 %copy-start.9 = (bf16[512,128]{1,0:T(8,128)(2,1)}, bf16[512,128]{1,0:T(8,128)(2,1)S(1)}, u32[]{:S(2)}) copy-start(bf16[512,128]{1,0:T(8,128)(2,1)S(1)} %collective-permute-done.refs_1_) | copy-start | bytes 393220
  26.2 20.3 %collective-permute-start.5 = (bf16[512,128]{1,0:T(8,128)(2,1)}, bf16[512,128]{1,0:T(8,128)(2,1)S(1)}, u32[]{:S(2)}, u32[]{:S(2)}) collective-permute-start(bf16[512,128]{1,0:T(8,128)(2,1)} %get-tuple-element.27), channel_id=1, source_target_pairs={{0,15},{1,8},{2,9},{3,10},{4,11},{5,12},{6,13},{7,14},{8,23},{9,16... | collective-permute-start | bytes 393224 | tf_op jit(solution)/shard_map/ppermute | solution.py:244
  28.6 18.0 %copy-start.10 = (bf16[512,128]{1,0:T(8,128)(2,1)}, bf16[512,128]{1,0:T(8,128)(2,1)S(1)}, u32[]{:S(2)}) copy-start(bf16[512,128]{1,0:T(8,128)(2,1)S(1)} %collective-permute-done.1.refs_2_) | copy-start | bytes 393220
  28.6 18.0 %collective-permute-start.6 = (bf16[512,128]{1,0:T(8,128)(2,1)}, bf16[512,128]{1,0:T(8,128)(2,1)S(1)}, u32[]{:S(2)}, u32[]{:S(2)}) collective-permute-start(bf16[512,128]{1,0:T(8,128)(2,1)} %get-tuple-element.28), channel_id=1, source_target_pairs={{0,8},{1,9},{2,10},{3,11},{4,12},{5,13},{6,14},{7,15},{8,16},{9,17... | collective-permute-start | bytes 393224 | tf_op jit(solution)/shard_map/ppermute | solution.py:244
  31.0 15.6 %copy-start.11 = (bf16[512,128]{1,0:T(8,128)(2,1)}, bf16[512,128]{1,0:T(8,128)(2,1)S(1)}, u32[]{:S(2)}) copy-start(bf16[512,128]{1,0:T(8,128)(2,1)S(1)} %collective-permute-done.2.refs_3_) | copy-start | bytes 393220
  31.0 15.5 %collective-permute-start.7 = (bf16[512,128]{1,0:T(8,128)(2,1)}, bf16[512,128]{1,0:T(8,128)(2,1)S(1)}, u32[]{:S(2)}, u32[]{:S(2)}) collective-permute-start(bf16[512,128]{1,0:T(8,128)(2,1)} %get-tuple-element.29), channel_id=1, source_target_pairs={{0,9},{1,10},{2,11},{3,12},{4,13},{5,14},{6,15},{7,8},{8,17},{9,18... | collective-permute-start | bytes 393224 | tf_op jit(solution)/shard_map/ppermute | solution.py:244
  46.5 0.6 copy-start.12
  46.5 0.7 copy-start.13
  46.5 0.7 copy-start.14
  46.5 0.8 copy-start.15
  46.6 0.8 copy-start.16
  55.3 9.8 %collective-permute-start.8 = (bf16[128,512]{1,0:T(8,128)(2,1)}, bf16[128,512]{1,0:T(8,128)(2,1)S(1)}, u32[]{:S(2)}, u32[]{:S(2)}) collective-permute-start(bf16[128,512]{1,0:T(8,128)(2,1)} %get-tuple-element.31), channel_id=1, source_target_pairs={{127,0},{120,1},{121,2},{122,3},{123,4},{124,5},{125,6},{126,7},{7... | collective-permute-start | bytes 393224 | tf_op jit(solution)/shard_map/ppermute | solution.py:270
  57.5 13.9 %collective-permute-start.9 = (bf16[128,512]{1,0:T(8,128)(2,1)}, bf16[128,512]{1,0:T(8,128)(2,1)S(1)}, u32[]{:S(2)}, u32[]{:S(2)}) collective-permute-start(bf16[128,512]{1,0:T(8,128)(2,1)} %get-tuple-element.32), channel_id=1, source_target_pairs={{120,0},{121,1},{122,2},{123,3},{124,4},{125,5},{126,6},{127,7},{0... | collective-permute-start | bytes 393224 | tf_op jit(solution)/shard_map/ppermute | solution.py:270
  60.1 12.5 %collective-permute-start.10 = (bf16[128,512]{1,0:T(8,128)(2,1)}, bf16[128,512]{1,0:T(8,128)(2,1)S(1)}, u32[]{:S(2)}, u32[]{:S(2)}) collective-permute-start(bf16[128,512]{1,0:T(8,128)(2,1)} %get-tuple-element.33), channel_id=1, source_target_pairs={{121,0},{122,1},{123,2},{124,3},{125,4},{126,5},{127,6},{120,7},{1... | collective-permute-start | bytes 393224 | tf_op jit(solution)/shard_map/ppermute | solution.py:270
  60.1 13.8 %collective-permute-start.11 = (bf16[128,512]{1,0:T(8,128)(2,1)}, bf16[128,512]{1,0:T(8,128)(2,1)S(1)}, u32[]{:S(2)}, u32[]{:S(2)}) collective-permute-start(bf16[128,512]{1,0:T(8,128)(2,1)} %get-tuple-element.34), channel_id=1, source_target_pairs={{7,0},{0,1},{1,2},{2,3},{3,4},{4,5},{5,6},{6,7},{15,8},{8,9},{9,10... | collective-permute-start | bytes 393224 | tf_op jit(solution)/shard_map/ppermute | solution.py:270
  60.3 13.7 %collective-permute-start.12 = (bf16[128,512]{1,0:T(8,128)(2,1)}, bf16[128,512]{1,0:T(8,128)(2,1)S(1)}, u32[]{:S(2)}, u32[]{:S(2)}) collective-permute-start(bf16[128,512]{1,0:T(8,128)(2,1)} %get-tuple-element.35), channel_id=1, source_target_pairs={{1,0},{2,1},{3,2},{4,3},{5,4},{6,5},{7,6},{0,7},{9,8},{10,9},{11,1... | collective-permute-start | bytes 393224 | tf_op jit(solution)/shard_map/ppermute | solution.py:270
  65.2 14.6 %copy-start = (bf16[128,512]{1,0:T(8,128)(2,1)}, bf16[128,512]{1,0:T(8,128)(2,1)S(1)}, u32[]{:S(2)}) copy-start(bf16[128,512]{1,0:T(8,128)(2,1)S(1)} %collective-permute-done.8.refs_1_) | copy-start | bytes 393220
  65.2 8.8 %collective-permute-start.13 = (bf16[128,512]{1,0:T(8,128)(2,1)}, bf16[128,512]{1,0:T(8,128)(2,1)S(1)}, u32[]{:S(2)}, u32[]{:S(2)}) collective-permute-start(bf16[128,512]{1,0:T(8,128)(2,1)} %get-tuple-element.36), channel_id=1, source_target_pairs={{15,0},{8,1},{9,2},{10,3},{11,4},{12,5},{13,6},{14,7},{23,8},{16,9... | collective-permute-start | bytes 393224 | tf_op jit(solution)/shard_map/ppermute | solution.py:270
  71.3 8.4 %copy-start.1 = (bf16[128,512]{1,0:T(8,128)(2,1)}, bf16[128,512]{1,0:T(8,128)(2,1)S(1)}, u32[]{:S(2)}) copy-start(bf16[128,512]{1,0:T(8,128)(2,1)S(1)} %collective-permute-done.9.refs_2_) | copy-start | bytes 393220
  71.3 6.6 %collective-permute-start.14 = (bf16[128,512]{1,0:T(8,128)(2,1)}, bf16[128,512]{1,0:T(8,128)(2,1)S(1)}, u32[]{:S(2)}, u32[]{:S(2)}) collective-permute-start(bf16[128,512]{1,0:T(8,128)(2,1)} %get-tuple-element.37), channel_id=1, source_target_pairs={{8,0},{9,1},{10,2},{11,3},{12,4},{13,5},{14,6},{15,7},{16,8},{17,9... | collective-permute-start | bytes 393224 | tf_op jit(solution)/shard_map/ppermute | solution.py:270
  72.6 7.1 %copy-start.2 = (bf16[128,512]{1,0:T(8,128)(2,1)}, bf16[128,512]{1,0:T(8,128)(2,1)S(1)}, u32[]{:S(2)}) copy-start(bf16[128,512]{1,0:T(8,128)(2,1)S(1)} %collective-permute-done.10.refs_3_) | copy-start | bytes 393220
  72.6 7.1 %collective-permute-start.15 = (bf16[128,512]{1,0:T(8,128)(2,1)}, bf16[128,512]{1,0:T(8,128)(2,1)S(1)}, u32[]{:S(2)}, u32[]{:S(2)}) collective-permute-start(bf16[128,512]{1,0:T(8,128)(2,1)} %get-tuple-element.38), channel_id=1, source_target_pairs={{9,0},{10,1},{11,2},{12,3},{13,4},{14,5},{15,6},{8,7},{17,8},{18,9... | collective-permute-start | bytes 393224 | tf_op jit(solution)/shard_map/ppermute | solution.py:270
  73.9 5.8 %copy-start.3 = (bf16[128,512]{1,0:T(8,128)(2,1)}, bf16[128,512]{1,0:T(8,128)(2,1)S(1)}, u32[]{:S(2)}) copy-start(bf16[128,512]{1,0:T(8,128)(2,1)S(1)} %collective-permute-done.11.refs_4_) | copy-start | bytes 393220
  73.9 5.9 %copy-start.4 = (bf16[128,512]{1,0:T(8,128)(2,1)}, bf16[128,512]{1,0:T(8,128)(2,1)S(1)}, u32[]{:S(2)}) copy-start(bf16[128,512]{1,0:T(8,128)(2,1)S(1)} %collective-permute-done.12.refs_5_) | copy-start | bytes 393220
  74.0 5.8 %copy-start.5 = (bf16[128,512]{1,0:T(8,128)(2,1)}, bf16[128,512]{1,0:T(8,128)(2,1)S(1)}, u32[]{:S(2)}) copy-start(bf16[128,512]{1,0:T(8,128)(2,1)S(1)} %collective-permute-done.13.refs_6_) | copy-start | bytes 393220
  78.0 1.8 %copy-start.6 = (bf16[128,512]{1,0:T(8,128)(2,1)}, bf16[128,512]{1,0:T(8,128)(2,1)S(1)}, u32[]{:S(2)}) copy-start(bf16[128,512]{1,0:T(8,128)(2,1)S(1)} %collective-permute-done.14.refs_7_) | copy-start | bytes 393220
  79.8 0.7 copy-start.7

commit v4 on v3

--- a/solution.py
+++ b/solution.py
@@ -11,7 +11,7 @@
 C_DEV = 4096
 SELF_CAP = 4096
 WIN = 128
-BRICKS_PER_STEP = 32
+BRICKS_PER_STEP = 64
 UNROLL = 8
 WIN_UNROLL = 4
 

time: 98.9 us -> 96.7 us (0.978)
  starting transfers between devices: 24.1 us -> 19.4 us
  waiting for transfers between devices: 16.2 us -> 20.9 us
  Pallas kernels: 51.9 us -> 49.5 us
    ppermute x8, waiting for transfers between devices: 2.45 us -> 5.86 us  [local(): lax.ppermute(parts[1 + g], ('outer', 'inner'), group_route(g, 1))]
    pallas_call x2, Pallas kernels: 26.7 us -> 24 us  [down_call(): pl.pallas_call(functools.partial(down_kernel, first_window), out_shape=sh...]
    ppermute x8, starting transfers between devices: 13.5 us -> 11 us  [local(): lax.ppermute(parts[1 + g], ('outer', 'inner'), group_route(g, 1))]
    ppermute x8, starting transfers between devices: 10.6 us -> 8.32 us  [local(): lax.ppermute(answers[1 + g], ('outer', 'inner'), group_route(g, -1))]
    ppermute x8, waiting for transfers between devices: 13.8 us -> 15 us  [local(): lax.ppermute(answers[1 + g], ('outer', 'inner'), group_route(g, -1))]
  transfers between devices with their start and end apart: 16 -> 16, of which waited for: 6 -> 7; matrix products, arithmetic and copies ran while one was open for 1% -> 1% of each run, Pallas kernels for 14% -> 13%
where the time goes in v4:
time: 96.7 us; the launch traced here: 95.3 us
  Pallas kernels  49.5 us (51%)
  waiting for transfers between devices  20.9 us (22%)
  starting transfers between devices  19.4 us (20%)
  local copies, waits for them, and re-layouts  3.16 us (3%)
  other arithmetic  2.2 us (2%)
    pallas_call x2, Pallas kernels, down_call(): pl.pallas_call(functools.partial(down_kernel, first_window), out_shape=sh...  24 us
    pallas_call x1, Pallas kernels, local(): up(brick_window, block_offset, xt, entry_rows, w_up_t, answers[0], *retur...  17.5 us
    ppermute x8, waiting for transfers between devices, local(): lax.ppermute(answers[1 + g], ('outer', 'inner'), group_route(g, -1))  15 us
    ppermute x8, starting transfers between devices, local(): lax.ppermute(parts[1 + g], ('outer', 'inner'), group_route(g, 1))  11 us
    ppermute x8, starting transfers between devices, local(): lax.ppermute(answers[1 + g], ('outer', 'inner'), group_route(g, -1))  8.32 us
    pallas_call x1, Pallas kernels, local(): coarse(cell_window, cells, b_down.reshape(1, out_width), parts[0], *arrived)  7.99 us
    ppermute x8, waiting for transfers between devices, local(): lax.ppermute(parts[1 + g], ('outer', 'inner'), group_route(g, 1))  5.86 us
  transfers between devices with their start and end apart: 16, of which 7 were waited for; matrix products, arithmetic and copies ran while one was open for 1% of the time, Pallas kernels for 13%

profile of v4, /device:TPU:24, one launch (start us, length us, event | category | flops | bytes accessed | tf_op | source)
XLA Modules:
  0.0 95.3 jit_solution(17525168545908209554)
XLA Ops:
  0.0 1.0 %slice_reduce_fusion = s32[256]{0:T(256)S(1)} fusion(s32[256,128]{1,0:T(8,128)} %bitcast.9), kind=kLoop, calls=%fused_computation | loop fusion | bytes 2048 | tf_op jit(solution)/shard_map/slice | solution.py:193
  1.0 0.6 and_select_fusion.1.win_ref
  1.6 0.1 squeeze.6
  1.7 0.1 convert_reduce_fusion.count_ref
  1.9 0.2 reduce_window_sum.18
  2.1 0.2 reduce_window_sum.17
  2.3 0.1 fusion.2
  2.4 0.1 select_reduce_fusion
  2.6 0.7 reshape.114.order_ref
  3.2 0.0 copy-done.17
  3.2 11.5 %shard_map.74 = (bf16[512,128]{1,0:T(8,128)(2,1)}, bf16[512,128]{1,0:T(8,128)(2,1)}, bf16[512,128]{1,0:T(8,128)(2,1)}, bf16[512,128]{1,0:T(8,128)(2,1)}, bf16[51...) custom-call(s32[4]{0:T(128)} %copy-done.17, ...), custom_call_target="tpu_custom_call" | custom-call | flops 536870912 | bytes 5373952 | tf_op jit(solution)/shard_map/pallas_call | solution.py:218
  14.7 7.9 %collective-permute-start = (bf16[512,128]{1,0:T(8,128)(2,1)}, bf16[512,128]{1,0:T(8,128)(2,1)S(1)}, u32[]{:S(2)}, u32[]{:S(2)}) collective-permute-start(bf16[512,128]{1,0:T(8,128)(2,1)} %get-tuple-element.22), channel_id=1, source_target_pairs={{0,127},{1,120},{2,121},{3,122},{4,123},{5,124},{6,125},{7,126},{8... | collective-permute-start | bytes 393224 | tf_op jit(solution)/shard_map/ppermute | solution.py:244
  22.6 0.3 collective-permute-start.1
  22.9 0.1 collective-permute-start.2
  23.1 1.5 %collective-permute-start.3 = (bf16[512,128]{1,0:T(8,128)(2,1)}, bf16[512,128]{1,0:T(8,128)(2,1)S(1)}, u32[]{:S(2)}, u32[]{:S(2)}) collective-permute-start(bf16[512,128]{1,0:T(8,128)(2,1)} %get-tuple-element.25), channel_id=1, source_target_pairs={{0,7},{1,0},{2,1},{3,2},{4,3},{5,4},{6,5},{7,6},{8,15},{9,8},{10,9... | collective-permute-start | bytes 393224 | tf_op jit(solution)/shard_map/ppermute | solution.py:244
  24.6 0.4 collective-permute-start.4
  25.0 0.0 copy-done.8
  25.0 0.1 reduce_min.9
  25.1 1.6 %collective-permute-done.refs_1_ = bf16[512,128]{1,0:T(8,128)(2,1)S(1)} collective-permute-done((bf16[512,128]{1,0:T(8,128)(2,1)}, bf16[512,128]{1,0:T(8,128)(2,1)S(1)}, u32[]{:S(2)}, u32[]{:S(2)}) %collective-permute-start) | collective-permute-done | bytes 131104 | tf_op jit(solution)/shard_map/ppermute | solution.py:244
  26.8 0.8 collective-permute-start.5
  27.5 2.1 %collective-permute-done.1.refs_2_ = bf16[512,128]{1,0:T(8,128)(2,1)S(1)} collective-permute-done((bf16[512,128]{1,0:T(8,128)(2,1)}, bf16[512,128]{1,0:T(8,128)(2,1)S(1)}, u32[]{:S(2)}, u32[]{:S(2)}) %collective-permute-start.1) | collective-permute-done | bytes 131104 | tf_op jit(solution)/shard_map/ppermute | solution.py:244
  29.6 0.0 collective-permute-start.6
  29.6 2.1 %collective-permute-done.2.refs_3_ = bf16[512,128]{1,0:T(8,128)(2,1)S(1)} collective-permute-done((bf16[512,128]{1,0:T(8,128)(2,1)}, bf16[512,128]{1,0:T(8,128)(2,1)S(1)}, u32[]{:S(2)}, u32[]{:S(2)}) %collective-permute-start.2) | collective-permute-done | bytes 131104 | tf_op jit(solution)/shard_map/ppermute | solution.py:244
  31.7 0.0 collective-permute-start.7
  31.7 0.6 and_select_fusion.cw_ref
  32.4 12.5 %shard_map.73.refs_0_ = bf16[4096,128]{1,0:T(8,128)(2,1)} custom-call(s32[4]{0:T(128)} %copy-done.17, s32[256]{0:T(256)} %reshape.114.order_ref, s32[256]{0:T(256)} %and_select_fusion.1.win_ref, s32[256]{0:T(256)} %off_ref.5, bf16[64,32768]{1,0:T(8,128)(2,1)} %bitcast.7, s32[256,128]{1,0:T(8,128)} %bitcast.11, bf16[8,64,128]{2,1,0:T(8,128)(2,1)} %w_ref.3), custom_call_target="tpu_custom_call" | custom-call | flops 536870912 | bytes 5373952 | tf_op jit(solution)/shard_map/pallas_call | solution.py:218
  44.9 0.0 collective-permute-done.3.refs_4_
  44.9 0.0 collective-permute-done.4.refs_5_
  44.9 0.0 copy-start.13
  44.9 0.0 collective-permute-done.5.refs_6_
  44.9 0.0 copy-start.14
  44.9 0.0 collective-permute-done.6.refs_7_
  44.9 0.0 copy-start.15
  44.9 0.0 collective-permute-done.7.refs_8_
  45.0 0.5 copy-done.12
  45.5 0.1 copy-done.13
  45.6 0.1 copy-done.14
  45.6 0.0 copy-done.15
  45.7 0.0 copy-done.16
  45.7 8.0 %shard_map.75 = (bf16[128,4096]{1,0:T(8,128)(2,1)}, bf16[128,512]{1,0:T(8,128)(2,1)}, bf16[128,512]{1,0:T(8,128)(2,1)}, bf16[128,512]{1,0:T(8,128)(2,1)}, bf16[1...) custom-call(s32[64]{0:T(128)} %and_select_fusion.cw_ref, ...), custom_call_target="tpu_custom_call" | custom-call | flops 536870912 | bytes 4194304 | tf_op jit(solution)/shard_map/pallas_call | solution.py:267
  53.7 0.0 collective-permute-start.8
  53.7 3.1 %collective-permute-start.9 = (bf16[128,512]{1,0:T(8,128)(2,1)}, bf16[128,512]{1,0:T(8,128)(2,1)S(1)}, u32[]{:S(2)}, u32[]{:S(2)}) collective-permute-start(bf16[128,512]{1,0:T(8,128)(2,1)} %get-tuple-element.32), channel_id=1, source_target_pairs={{120,0},{121,1},{122,2},{123,3},{124,4},{125,5},{126,6},{127,7},{0... | collective-permute-start | bytes 393224 | tf_op jit(solution)/shard_map/ppermute | solution.py:270
  56.8 1.0 %collective-permute-start.10 = (bf16[128,512]{1,0:T(8,128)(2,1)}, bf16[128,512]{1,0:T(8,128)(2,1)S(1)}, u32[]{:S(2)}, u32[]{:S(2)}) collective-permute-start(bf16[128,512]{1,0:T(8,128)(2,1)} %get-tuple-element.33), channel_id=1, source_target_pairs={{121,0},{122,1},{123,2},{124,3},{125,4},{126,5},{127,6},{120,7},{1... | collective-permute-start | bytes 393224 | tf_op jit(solution)/shard_map/ppermute | solution.py:270
  57.8 0.0 collective-permute-start.11
  57.8 1.7 %collective-permute-start.12 = (bf16[128,512]{1,0:T(8,128)(2,1)}, bf16[128,512]{1,0:T(8,128)(2,1)S(1)}, u32[]{:S(2)}, u32[]{:S(2)}) collective-permute-start(bf16[128,512]{1,0:T(8,128)(2,1)} %get-tuple-element.35), channel_id=1, source_target_pairs={{1,0},{2,1},{3,2},{4,3},{5,4},{6,5},{7,6},{0,7},{9,8},{10,9},{11,1... | collective-permute-start | bytes 393224 | tf_op jit(solution)/shard_map/ppermute | solution.py:270
  59.5 4.8 %collective-permute-done.8.refs_1_ = bf16[128,512]{1,0:T(8,128)(2,1)S(1)} collective-permute-done((bf16[128,512]{1,0:T(8,128)(2,1)}, bf16[128,512]{1,0:T(8,128)(2,1)S(1)}, u32[]{:S(2)}, u32[]{:S(2)}) %collective-permute-start.8) | collective-permute-done | bytes 131104 | tf_op jit(solution)/shard_map/ppermute | solution.py:270
  64.3 0.0 collective-permute-start.13
  64.3 3.4 %collective-permute-done.9.refs_2_ = bf16[128,512]{1,0:T(8,128)(2,1)S(1)} collective-permute-done((bf16[128,512]{1,0:T(8,128)(2,1)}, bf16[128,512]{1,0:T(8,128)(2,1)S(1)}, u32[]{:S(2)}, u32[]{:S(2)}) %collective-permute-start.9) | collective-permute-done | bytes 131104 | tf_op jit(solution)/shard_map/ppermute | solution.py:270
  67.7 1.3 %collective-permute-start.14 = (bf16[128,512]{1,0:T(8,128)(2,1)}, bf16[128,512]{1,0:T(8,128)(2,1)S(1)}, u32[]{:S(2)}, u32[]{:S(2)}) collective-permute-start(bf16[128,512]{1,0:T(8,128)(2,1)} %get-tuple-element.37), channel_id=1, source_target_pairs={{8,0},{9,1},{10,2},{11,3},{12,4},{13,5},{14,6},{15,7},{16,8},{17,9... | collective-permute-start | bytes 393224 | tf_op jit(solution)/shard_map/ppermute | solution.py:270
  69.0 0.0 collective-permute-done.10.refs_3_
  69.1 1.2 %collective-permute-start.15 = (bf16[128,512]{1,0:T(8,128)(2,1)}, bf16[128,512]{1,0:T(8,128)(2,1)S(1)}, u32[]{:S(2)}, u32[]{:S(2)}) collective-permute-start(bf16[128,512]{1,0:T(8,128)(2,1)} %get-tuple-element.38), channel_id=1, source_target_pairs={{9,0},{10,1},{11,2},{12,3},{13,4},{14,5},{15,6},{8,7},{17,8},{18,9... | collective-permute-start | bytes 393224 | tf_op jit(solution)/shard_map/ppermute | solution.py:270
  70.3 0.0 collective-permute-done.11.refs_4_
  70.3 0.0 collective-permute-done.12.refs_5_
  70.3 0.0 collective-permute-done.13.refs_6_
  70.3 0.0 copy-start.5
  70.3 3.6 %collective-permute-done.14.refs_7_ = bf16[128,512]{1,0:T(8,128)(2,1)S(1)} collective-permute-done((bf16[128,512]{1,0:T(8,128)(2,1)}, bf16[128,512]{1,0:T(8,128)(2,1)S(1)}, u32[]{:S(2)}, u32[]{:S(2)}) %collective-permute-start.14) | collective-permute-done | bytes 131104 | tf_op jit(solution)/shard_map/ppermute | solution.py:270
  73.9 3.2 %collective-permute-done.15.refs_8_ = bf16[128,512]{1,0:T(8,128)(2,1)S(1)} collective-permute-done((bf16[128,512]{1,0:T(8,128)(2,1)}, bf16[128,512]{1,0:T(8,128)(2,1)S(1)}, u32[]{:S(2)}, u32[]{:S(2)}) %collective-permute-start.15) | collective-permute-done | bytes 131104 | tf_op jit(solution)/shard_map/ppermute | solution.py:270
  77.1 0.0 copy-done.1
  77.1 0.0 copy-done.3
  77.2 0.0 copy-done.4
  77.2 0.0 copy-done.5
  77.2 0.0 copy-done.6
  77.2 0.6 copy-done.7
  77.8 17.5 %shard_map.76 = bf16[64,32768]{1,0:T(8,128)(2,1)} custom-call(s32[256]{0:T(256)} %and_select_fusion.1.win_ref, s32[256]{0:T(256)} %off_ref.5, bf16[64,32768]{1,0:T(8,128)(2,1)} %bitcast.8, s32[256,128]{1,0:T(8,128)} %bitcast.12, bf16[8,64,128]{2,1,0:T(8,128)(2,1)} %bitcast.13, bf16[128,4096]{1,0:T(8,128)(2,1)} %get-tuple-element.30.refs_0_, ...), custom_call_target="tpu_custom_call" | custom-call | flops 1610612736 | bytes 10616832 | tf_op jit(solution)/shard_map/pallas_call | solution.py:298
  (21 shorter events, 0.1 us)
Async XLA Ops:
  0.0 25.0 %copy-start.8 = (s32[1,8192]{1,0:T(1,128)S(1)}, s32[1,8192]{1,0:T(1,128)}, u32[]{:S(2)}) copy-start(s32[1,8192]{1,0:T(1,128)} %param.10) | copy-start | bytes 98308
  1.8 1.4 %copy-start.17 = (s32[4]{0:T(128)}, s32[4]{0:T(128)S(1)}, u32[]{:S(2)}) copy-start(s32[4]{0:T(128)S(1)} %convert_reduce_fusion.count_ref) | copy-start | bytes 52
  14.7 12.0 %collective-permute-start = (bf16[512,128]{1,0:T(8,128)(2,1)}, bf16[512,128]{1,0:T(8,128)(2,1)S(1)}, u32[]{:S(2)}, u32[]{:S(2)}) collective-permute-start(bf16[512,128]{1,0:T(8,128)(2,1)} %get-tuple-element.22), channel_id=1, source_target_pairs={{0,127},{1,120},{2,121},{3,122},{4,123},{5,124},{6,125},{7,126},{8... | collective-permute-start | bytes 393224 | tf_op jit(solution)/shard_map/ppermute | solution.py:244
  22.6 7.0 %collective-permute-start.1 = (bf16[512,128]{1,0:T(8,128)(2,1)}, bf16[512,128]{1,0:T(8,128)(2,1)S(1)}, u32[]{:S(2)}, u32[]{:S(2)}) collective-permute-start(bf16[512,128]{1,0:T(8,128)(2,1)} %get-tuple-element.23), channel_id=1, source_target_pairs={{0,120},{1,121},{2,122},{3,123},{4,124},{5,125},{6,126},{7,127},{8... | collective-permute-start | bytes 393224 | tf_op jit(solution)/shard_map/ppermute | solution.py:244
  22.9 8.8 %collective-permute-start.2 = (bf16[512,128]{1,0:T(8,128)(2,1)}, bf16[512,128]{1,0:T(8,128)(2,1)S(1)}, u32[]{:S(2)}, u32[]{:S(2)}) collective-permute-start(bf16[512,128]{1,0:T(8,128)(2,1)} %get-tuple-element.24), channel_id=1, source_target_pairs={{0,121},{1,122},{2,123},{3,124},{4,125},{5,126},{6,127},{7,120},{8... | collective-permute-start | bytes 393224 | tf_op jit(solution)/shard_map/ppermute | solution.py:244
  23.1 21.8 %collective-permute-start.3 = (bf16[512,128]{1,0:T(8,128)(2,1)}, bf16[512,128]{1,0:T(8,128)(2,1)S(1)}, u32[]{:S(2)}, u32[]{:S(2)}) collective-permute-start(bf16[512,128]{1,0:T(8,128)(2,1)} %get-tuple-element.25), channel_id=1, source_target_pairs={{0,7},{1,0},{2,1},{3,2},{4,3},{5,4},{6,5},{7,6},{8,15},{9,8},{10,9... | collective-permute-start | bytes 393224 | tf_op jit(solution)/shard_map/ppermute | solution.py:244
  24.6 20.3 %collective-permute-start.4 = (bf16[512,128]{1,0:T(8,128)(2,1)}, bf16[512,128]{1,0:T(8,128)(2,1)S(1)}, u32[]{:S(2)}, u32[]{:S(2)}) collective-permute-start(bf16[512,128]{1,0:T(8,128)(2,1)} %get-tuple-element.26), channel_id=1, source_target_pairs={{0,1},{1,2},{2,3},{3,4},{4,5},{5,6},{6,7},{7,0},{8,9},{9,10},{10,1... | collective-permute-start | bytes 393224 | tf_op jit(solution)/shard_map/ppermute | solution.py:244
  26.8 18.2 %copy-start.9 = (bf16[512,128]{1,0:T(8,128)(2,1)}, bf16[512,128]{1,0:T(8,128)(2,1)S(1)}, u32[]{:S(2)}) copy-start(bf16[512,128]{1,0:T(8,128)(2,1)S(1)} %collective-permute-done.refs_1_) | copy-start | bytes 393220
  26.8 18.1 %collective-permute-start.5 = (bf16[512,128]{1,0:T(8,128)(2,1)}, bf16[512,128]{1,0:T(8,128)(2,1)S(1)}, u32[]{:S(2)}, u32[]{:S(2)}) collective-permute-start(bf16[512,128]{1,0:T(8,128)(2,1)} %get-tuple-element.27), channel_id=1, source_target_pairs={{0,15},{1,8},{2,9},{3,10},{4,11},{5,12},{6,13},{7,14},{8,23},{9,16... | collective-permute-start | bytes 393224 | tf_op jit(solution)/shard_map/ppermute | solution.py:244
  29.6 15.4 %copy-start.10 = (bf16[512,128]{1,0:T(8,128)(2,1)}, bf16[512,128]{1,0:T(8,128)(2,1)S(1)}, u32[]{:S(2)}) copy-start(bf16[512,128]{1,0:T(8,128)(2,1)S(1)} %collective-permute-done.1.refs_2_) | copy-start | bytes 393220
  29.6 15.3 %collective-permute-start.6 = (bf16[512,128]{1,0:T(8,128)(2,1)}, bf16[512,128]{1,0:T(8,128)(2,1)S(1)}, u32[]{:S(2)}, u32[]{:S(2)}) collective-permute-start(bf16[512,128]{1,0:T(8,128)(2,1)} %get-tuple-element.28), channel_id=1, source_target_pairs={{0,8},{1,9},{2,10},{3,11},{4,12},{5,13},{6,14},{7,15},{8,16},{9,17... | collective-permute-start | bytes 393224 | tf_op jit(solution)/shard_map/ppermute | solution.py:244
  31.7 13.3 %copy-start.11 = (bf16[512,128]{1,0:T(8,128)(2,1)}, bf16[512,128]{1,0:T(8,128)(2,1)S(1)}, u32[]{:S(2)}) copy-start(bf16[512,128]{1,0:T(8,128)(2,1)S(1)} %collective-permute-done.2.refs_3_) | copy-start | bytes 393220
  31.7 13.2 %collective-permute-start.7 = (bf16[512,128]{1,0:T(8,128)(2,1)}, bf16[512,128]{1,0:T(8,128)(2,1)S(1)}, u32[]{:S(2)}, u32[]{:S(2)}) collective-permute-start(bf16[512,128]{1,0:T(8,128)(2,1)} %get-tuple-element.29), channel_id=1, source_target_pairs={{0,9},{1,10},{2,11},{3,12},{4,13},{5,14},{6,15},{7,8},{8,17},{9,18... | collective-permute-start | bytes 393224 | tf_op jit(solution)/shard_map/ppermute | solution.py:244
  44.9 0.6 copy-start.12
  44.9 0.7 copy-start.13
  44.9 0.7 copy-start.14
  44.9 0.8 copy-start.15
  44.9 0.8 copy-start.16
  53.7 10.6 %collective-permute-start.8 = (bf16[128,512]{1,0:T(8,128)(2,1)}, bf16[128,512]{1,0:T(8,128)(2,1)S(1)}, u32[]{:S(2)}, u32[]{:S(2)}) collective-permute-start(bf16[128,512]{1,0:T(8,128)(2,1)} %get-tuple-element.31), channel_id=1, source_target_pairs={{127,0},{120,1},{121,2},{122,3},{123,4},{124,5},{125,6},{126,7},{7... | collective-permute-start | bytes 393224 | tf_op jit(solution)/shard_map/ppermute | solution.py:270
  53.7 14.0 %collective-permute-start.9 = (bf16[128,512]{1,0:T(8,128)(2,1)}, bf16[128,512]{1,0:T(8,128)(2,1)S(1)}, u32[]{:S(2)}, u32[]{:S(2)}) collective-permute-start(bf16[128,512]{1,0:T(8,128)(2,1)} %get-tuple-element.32), channel_id=1, source_target_pairs={{120,0},{121,1},{122,2},{123,3},{124,4},{125,5},{126,6},{127,7},{0... | collective-permute-start | bytes 393224 | tf_op jit(solution)/shard_map/ppermute | solution.py:270
  56.8 12.3 %collective-permute-start.10 = (bf16[128,512]{1,0:T(8,128)(2,1)}, bf16[128,512]{1,0:T(8,128)(2,1)S(1)}, u32[]{:S(2)}, u32[]{:S(2)}) collective-permute-start(bf16[128,512]{1,0:T(8,128)(2,1)} %get-tuple-element.33), channel_id=1, source_target_pairs={{121,0},{122,1},{123,2},{124,3},{125,4},{126,5},{127,6},{120,7},{1... | collective-permute-start | bytes 393224 | tf_op jit(solution)/shard_map/ppermute | solution.py:270
  57.8 12.5 %collective-permute-start.11 = (bf16[128,512]{1,0:T(8,128)(2,1)}, bf16[128,512]{1,0:T(8,128)(2,1)S(1)}, u32[]{:S(2)}, u32[]{:S(2)}) collective-permute-start(bf16[128,512]{1,0:T(8,128)(2,1)} %get-tuple-element.34), channel_id=1, source_target_pairs={{7,0},{0,1},{1,2},{2,3},{3,4},{4,5},{5,6},{6,7},{15,8},{8,9},{9,10... | collective-permute-start | bytes 393224 | tf_op jit(solution)/shard_map/ppermute | solution.py:270
  57.8 12.5 %collective-permute-start.12 = (bf16[128,512]{1,0:T(8,128)(2,1)}, bf16[128,512]{1,0:T(8,128)(2,1)S(1)}, u32[]{:S(2)}, u32[]{:S(2)}) collective-permute-start(bf16[128,512]{1,0:T(8,128)(2,1)} %get-tuple-element.35), channel_id=1, source_target_pairs={{1,0},{2,1},{3,2},{4,3},{5,4},{6,5},{7,6},{0,7},{9,8},{10,9},{11,1... | collective-permute-start | bytes 393224 | tf_op jit(solution)/shard_map/ppermute | solution.py:270
  64.3 12.8 %copy-start = (bf16[128,512]{1,0:T(8,128)(2,1)}, bf16[128,512]{1,0:T(8,128)(2,1)S(1)}, u32[]{:S(2)}) copy-start(bf16[128,512]{1,0:T(8,128)(2,1)S(1)} %collective-permute-done.8.refs_1_) | copy-start | bytes 393220
  64.3 6.0 %collective-permute-start.13 = (bf16[128,512]{1,0:T(8,128)(2,1)}, bf16[128,512]{1,0:T(8,128)(2,1)S(1)}, u32[]{:S(2)}, u32[]{:S(2)}) collective-permute-start(bf16[128,512]{1,0:T(8,128)(2,1)} %get-tuple-element.36), channel_id=1, source_target_pairs={{15,0},{8,1},{9,2},{10,3},{11,4},{12,5},{13,6},{14,7},{23,8},{16,9... | collective-permute-start | bytes 393224 | tf_op jit(solution)/shard_map/ppermute | solution.py:270
  67.7 9.4 %copy-start.1 = (bf16[128,512]{1,0:T(8,128)(2,1)}, bf16[128,512]{1,0:T(8,128)(2,1)S(1)}, u32[]{:S(2)}) copy-start(bf16[128,512]{1,0:T(8,128)(2,1)S(1)} %collective-permute-done.9.refs_2_) | copy-start | bytes 393220
  67.7 6.2 %collective-permute-start.14 = (bf16[128,512]{1,0:T(8,128)(2,1)}, bf16[128,512]{1,0:T(8,128)(2,1)S(1)}, u32[]{:S(2)}, u32[]{:S(2)}) collective-permute-start(bf16[128,512]{1,0:T(8,128)(2,1)} %get-tuple-element.37), channel_id=1, source_target_pairs={{8,0},{9,1},{10,2},{11,3},{12,4},{13,5},{14,6},{15,7},{16,8},{17,9... | collective-permute-start | bytes 393224 | tf_op jit(solution)/shard_map/ppermute | solution.py:270
  69.1 8.1 %copy-start.2 = (bf16[128,512]{1,0:T(8,128)(2,1)}, bf16[128,512]{1,0:T(8,128)(2,1)S(1)}, u32[]{:S(2)}) copy-start(bf16[128,512]{1,0:T(8,128)(2,1)S(1)} %collective-permute-done.10.refs_3_) | copy-start | bytes 393220
  69.1 8.1 %collective-permute-start.15 = (bf16[128,512]{1,0:T(8,128)(2,1)}, bf16[128,512]{1,0:T(8,128)(2,1)S(1)}, u32[]{:S(2)}, u32[]{:S(2)}) collective-permute-start(bf16[128,512]{1,0:T(8,128)(2,1)} %get-tuple-element.38), channel_id=1, source_target_pairs={{9,0},{10,1},{11,2},{12,3},{13,4},{14,5},{15,6},{8,7},{17,8},{18,9... | collective-permute-start | bytes 393224 | tf_op jit(solution)/shard_map/ppermute | solution.py:270
  70.3 6.9 %copy-start.3 = (bf16[128,512]{1,0:T(8,128)(2,1)}, bf16[128,512]{1,0:T(8,128)(2,1)S(1)}, u32[]{:S(2)}) copy-start(bf16[128,512]{1,0:T(8,128)(2,1)S(1)} %collective-permute-done.11.refs_4_) | copy-start | bytes 393220
  70.3 6.9 %copy-start.4 = (bf16[128,512]{1,0:T(8,128)(2,1)}, bf16[128,512]{1,0:T(8,128)(2,1)S(1)}, u32[]{:S(2)}) copy-start(bf16[128,512]{1,0:T(8,128)(2,1)S(1)} %collective-permute-done.12.refs_5_) | copy-start | bytes 393220
  70.3 6.9 %copy-start.5 = (bf16[128,512]{1,0:T(8,128)(2,1)}, bf16[128,512]{1,0:T(8,128)(2,1)S(1)}, u32[]{:S(2)}) copy-start(bf16[128,512]{1,0:T(8,128)(2,1)S(1)} %collective-permute-done.13.refs_6_) | copy-start | bytes 393220
  73.9 3.3 %copy-start.6 = (bf16[128,512]{1,0:T(8,128)(2,1)}, bf16[128,512]{1,0:T(8,128)(2,1)S(1)}, u32[]{:S(2)}) copy-start(bf16[128,512]{1,0:T(8,128)(2,1)S(1)} %collective-permute-done.14.refs_7_) | copy-start | bytes 393220
  77.1 0.7 copy-start.7

commit v5 on v4

--- a/solution.py
+++ b/solution.py
@@ -12,8 +12,8 @@
 SELF_CAP = 4096
 WIN = 128
 BRICKS_PER_STEP = 64
-UNROLL = 8
-WIN_UNROLL = 4
+UNROLL = 16
+WIN_UNROLL = 8
 
 step_table = ((-1, -1), (-1, 0), (-1, 1), (0, -1), (0, 1), (1, -1), (1, 0), (1, 1))
 
@@ -95,11 +95,12 @@
     base = 0
     for src in sources:
         count = src.shape[0] // WIN
-
-        def gather_body(u, carry, src=src, base=base):
+        unroll = min(WIN_UNROLL, count)
+
+        def gather_body(u, carry, src=src, base=base, unroll=unroll):
             results = []
-            for t in range(WIN_UNROLL):
-                j = u * WIN_UNROLL + t
+            for t in range(unroll):
+                j = u * unroll + t
                 pick, rows = pick_of(base + j)
                 entries = src[pl.ds(pl.multiple_of(j * WIN, WIN), WIN), :]
                 results.append((rows, jnp.dot(pick, entries, preferred_element_type=jnp.float32)))
@@ -107,7 +108,7 @@
                 acc[rows, :] += value
             return carry
 
-        lax.fori_loop(0, count // WIN_UNROLL, gather_body, 0)
+        lax.fori_loop(0, count // unroll, gather_body, 0)
         base += count
 
     coarse[...] = jnp.maximum(acc[...] + bias_ref[...], 0.0).astype(jnp.bfloat16)
@@ -115,16 +116,17 @@
     base = 0
     for out in outs:
         count = out.shape[1] // WIN
-
-        def scatter_body(u, carry, out=out, base=base):
-            for t in range(WIN_UNROLL):
-                j = u * WIN_UNROLL + t
+        unroll = min(WIN_UNROLL, count)
+
+        def scatter_body(u, carry, out=out, base=base, unroll=unroll):
+            for t in range(unroll):
+                j = u * unroll + t
                 pick, rows = pick_of(base + j)
                 chosen = lax.dot_general(coarse[rows, :], pick, TN, preferred_element_type=jnp.float32)
                 out[:, pl.ds(pl.multiple_of(j * WIN, WIN), WIN)] = chosen.astype(jnp.bfloat16)
             return carry
 
-        lax.fori_loop(0, count // WIN_UNROLL, scatter_body, 0)
+        lax.fori_loop(0, count // unroll, scatter_body, 0)
         base += count
 
 

time: 96.7 us -> 86.4 us (0.89); the launches traced: 95.3 us -> 86.3 us
  Pallas kernels: 49.5 us -> 39.8 us
  waiting for transfers between devices: 20.9 us -> 22.7 us
  starting transfers between devices: 19.4 us -> 18.3 us
    pallas_call x2, Pallas kernels: 24 us -> 19.7 us  [down_call(): pl.pallas_call(functools.partial(down_kernel, first_window), out_shape=sh...]
    pallas_call x1, Pallas kernels: 17.5 us -> 13.3 us  [local(): up(brick_window, block_offset, xt, entry_rows, w_up_t, answers[0], *retur...]
    pallas_call x1, Pallas kernels: 7.99 us -> 6.77 us  [local(): coarse(cell_window, cells, b_down.reshape(1, out_width), parts[0], *arrived)]
    ppermute x8, waiting for transfers between devices: 5.86 us -> 7.06 us  [local(): lax.ppermute(parts[1 + g], ('outer', 'inner'), group_route(g, 1))]
    ppermute x8, starting transfers between devices: 11 us -> 9.85 us  [local(): lax.ppermute(parts[1 + g], ('outer', 'inner'), group_route(g, 1))]
  transfers between devices with their start and end apart: 16 -> 16, of which waited for: 7 -> 9; matrix products, arithmetic and copies ran while one was open for 1% -> 1% of each run, Pallas kernels for 13% -> 10%
where the time goes in v5:
time: 86.4 us; the launch traced here: 86.3 us
  Pallas kernels  39.8 us (46%)
  waiting for transfers between devices  22.7 us (26%)
  starting transfers between devices  18.3 us (21%)
  local copies, waits for them, and re-layouts  3.02 us (3%)
  other arithmetic  2.2 us (3%)
    pallas_call x2, Pallas kernels, down_call(): pl.pallas_call(functools.partial(down_kernel, first_window), out_shape=sh...  19.7 us
    ppermute x8, waiting for transfers between devices, local(): lax.ppermute(answers[1 + g], ('outer', 'inner'), group_route(g, -1))  15.7 us
    pallas_call x1, Pallas kernels, local(): up(brick_window, block_offset, xt, entry_rows, w_up_t, answers[0], *retur...  13.3 us
    ppermute x8, starting transfers between devices, local(): lax.ppermute(parts[1 + g], ('outer', 'inner'), group_route(g, 1))  9.85 us
    ppermute x8, starting transfers between devices, local(): lax.ppermute(answers[1 + g], ('outer', 'inner'), group_route(g, -1))  8.46 us
    ppermute x8, waiting for transfers between devices, local(): lax.ppermute(parts[1 + g], ('outer', 'inner'), group_route(g, 1))  7.06 us
    pallas_call x1, Pallas kernels, local(): coarse(cell_window, cells, b_down.reshape(1, out_width), parts[0], *arrived)  6.77 us
  transfers between devices with their start and end apart: 16, of which 9 were waited for; matrix products, arithmetic and copies ran while one was open for 1% of the time, Pallas kernels for 10%

profile of v5, /device:TPU:24, one launch (start us, length us, event | category | flops | bytes accessed | tf_op | source)
XLA Modules:
  0.0 86.3 jit_solution(4909002563506127545)
XLA Ops:
  0.0 1.0 %slice_reduce_fusion = s32[256]{0:T(256)S(1)} fusion(s32[256,128]{1,0:T(8,128)} %bitcast.9), kind=kLoop, calls=%fused_computation | loop fusion | bytes 2048 | tf_op jit(solution)/shard_map/slice | solution.py:195
  1.0 0.6 and_select_fusion.1.win_ref
  1.6 0.1 squeeze.6
  1.7 0.1 convert_reduce_fusion.count_ref
  1.9 0.2 reduce_window_sum.18
  2.1 0.2 reduce_window_sum.17
  2.3 0.1 fusion.2
  2.4 0.1 select_reduce_fusion
  2.6 0.7 reshape.114.order_ref
  3.2 0.0 copy-done.17
  3.2 11.2 %shard_map.74 = (bf16[512,128]{1,0:T(8,128)(2,1)}, bf16[512,128]{1,0:T(8,128)(2,1)}, bf16[512,128]{1,0:T(8,128)(2,1)}, bf16[512,128]{1,0:T(8,128)(2,1)}, bf16[51...) custom-call(s32[4]{0:T(128)} %copy-done.17, ...), custom_call_target="tpu_custom_call" | custom-call | flops 536870912 | bytes 5373952 | tf_op jit(solution)/shard_map/pallas_call | solution.py:220
  14.4 3.9 %collective-permute-start = (bf16[512,128]{1,0:T(8,128)(2,1)}, bf16[512,128]{1,0:T(8,128)(2,1)S(1)}, u32[]{:S(2)}, u32[]{:S(2)}) collective-permute-start(bf16[512,128]{1,0:T(8,128)(2,1)} %get-tuple-element.22), channel_id=1, source_target_pairs={{0,127},{1,120},{2,121},{3,122},{4,123},{5,124},{6,125},{7,126},{8... | collective-permute-start | bytes 393224 | tf_op jit(solution)/shard_map/ppermute | solution.py:246
  18.3 1.5 %collective-permute-start.1 = (bf16[512,128]{1,0:T(8,128)(2,1)}, bf16[512,128]{1,0:T(8,128)(2,1)S(1)}, u32[]{:S(2)}, u32[]{:S(2)}) collective-permute-start(bf16[512,128]{1,0:T(8,128)(2,1)} %get-tuple-element.23), channel_id=1, source_target_pairs={{0,120},{1,121},{2,122},{3,123},{4,124},{5,125},{6,126},{7,127},{8... | collective-permute-start | bytes 393224 | tf_op jit(solution)/shard_map/ppermute | solution.py:246
  19.8 1.0 %collective-permute-start.2 = (bf16[512,128]{1,0:T(8,128)(2,1)}, bf16[512,128]{1,0:T(8,128)(2,1)S(1)}, u32[]{:S(2)}, u32[]{:S(2)}) collective-permute-start(bf16[512,128]{1,0:T(8,128)(2,1)} %get-tuple-element.24), channel_id=1, source_target_pairs={{0,121},{1,122},{2,123},{3,124},{4,125},{5,126},{6,127},{7,120},{8... | collective-permute-start | bytes 393224 | tf_op jit(solution)/shard_map/ppermute | solution.py:246
  20.8 2.0 %collective-permute-start.3 = (bf16[512,128]{1,0:T(8,128)(2,1)}, bf16[512,128]{1,0:T(8,128)(2,1)S(1)}, u32[]{:S(2)}, u32[]{:S(2)}) collective-permute-start(bf16[512,128]{1,0:T(8,128)(2,1)} %get-tuple-element.25), channel_id=1, source_target_pairs={{0,7},{1,0},{2,1},{3,2},{4,3},{5,4},{6,5},{7,6},{8,15},{9,8},{10,9... | collective-permute-start | bytes 393224 | tf_op jit(solution)/shard_map/ppermute | solution.py:246
  22.8 0.0 collective-permute-start.4
  22.8 0.0 copy-done.8
  22.8 0.1 reduce_min.9
  22.9 0.0 collective-permute-done.refs_1_
  22.9 0.0 copy-start.9
  22.9 1.4 %collective-permute-start.5 = (bf16[512,128]{1,0:T(8,128)(2,1)}, bf16[512,128]{1,0:T(8,128)(2,1)S(1)}, u32[]{:S(2)}, u32[]{:S(2)}) collective-permute-start(bf16[512,128]{1,0:T(8,128)(2,1)} %get-tuple-element.27), channel_id=1, source_target_pairs={{0,15},{1,8},{2,9},{3,10},{4,11},{5,12},{6,13},{7,14},{8,23},{9,16... | collective-permute-start | bytes 393224 | tf_op jit(solution)/shard_map/ppermute | solution.py:246
  24.4 1.0 %collective-permute-done.1.refs_2_ = bf16[512,128]{1,0:T(8,128)(2,1)S(1)} collective-permute-done((bf16[512,128]{1,0:T(8,128)(2,1)}, bf16[512,128]{1,0:T(8,128)(2,1)S(1)}, u32[]{:S(2)}, u32[]{:S(2)}) %collective-permute-start.1) | collective-permute-done | bytes 131104 | tf_op jit(solution)/shard_map/ppermute | solution.py:246
  25.4 0.0 collective-permute-start.6
  25.4 2.6 %collective-permute-done.2.refs_3_ = bf16[512,128]{1,0:T(8,128)(2,1)S(1)} collective-permute-done((bf16[512,128]{1,0:T(8,128)(2,1)}, bf16[512,128]{1,0:T(8,128)(2,1)S(1)}, u32[]{:S(2)}, u32[]{:S(2)}) %collective-permute-start.2) | collective-permute-done | bytes 131104 | tf_op jit(solution)/shard_map/ppermute | solution.py:246
  28.0 0.0 collective-permute-start.7
  28.0 0.6 and_select_fusion.cw_ref
  28.7 8.6 %shard_map.73.refs_0_ = bf16[4096,128]{1,0:T(8,128)(2,1)} custom-call(s32[4]{0:T(128)} %copy-done.17, s32[256]{0:T(256)} %reshape.114.order_ref, s32[256]{0:T(256)} %and_select_fusion.1.win_ref, s32[256]{0:T(256)} %off_ref.5, bf16[64,32768]{1,0:T(8,128)(2,1)} %bitcast.7, s32[256,128]{1,0:T(8,128)} %bitcast.11, bf16[8,64,128]{2,1,0:T(8,128)(2,1)} %w_ref.3), custom_call_target="tpu_custom_call" | custom-call | flops 536870912 | bytes 5373952 | tf_op jit(solution)/shard_map/pallas_call | solution.py:220
  37.2 0.0 collective-permute-done.3.refs_4_
  37.2 0.0 collective-permute-done.4.refs_5_
  37.2 0.0 copy-start.13
  37.3 0.0 collective-permute-done.5.refs_6_
  37.3 0.0 copy-start.14
  37.3 1.3 %collective-permute-done.6.refs_7_ = bf16[512,128]{1,0:T(8,128)(2,1)S(1)} collective-permute-done((bf16[512,128]{1,0:T(8,128)(2,1)}, bf16[512,128]{1,0:T(8,128)(2,1)S(1)}, u32[]{:S(2)}, u32[]{:S(2)}) %collective-permute-start.6) | collective-permute-done | bytes 131104 | tf_op jit(solution)/shard_map/ppermute | solution.py:246
  38.6 2.1 %collective-permute-done.7.refs_8_ = bf16[512,128]{1,0:T(8,128)(2,1)S(1)} collective-permute-done((bf16[512,128]{1,0:T(8,128)(2,1)}, bf16[512,128]{1,0:T(8,128)(2,1)S(1)}, u32[]{:S(2)}, u32[]{:S(2)}) %collective-permute-start.7) | collective-permute-done | bytes 131104 | tf_op jit(solution)/shard_map/ppermute | solution.py:246
  40.7 0.0 copy-done.9
  40.7 0.0 copy-done.10
  40.7 0.0 copy-done.11
  40.7 0.0 copy-done.12
  40.7 0.0 copy-done.13
  40.7 0.0 copy-done.14
  40.8 0.0 copy-done.15
  40.8 0.6 copy-done.16
  41.4 6.8 %shard_map.75 = (bf16[128,4096]{1,0:T(8,128)(2,1)}, bf16[128,512]{1,0:T(8,128)(2,1)}, bf16[128,512]{1,0:T(8,128)(2,1)}, bf16[128,512]{1,0:T(8,128)(2,1)}, bf16[1...) custom-call(s32[64]{0:T(128)} %and_select_fusion.cw_ref, ...), custom_call_target="tpu_custom_call" | custom-call | flops 536870912 | bytes 4194304 | tf_op jit(solution)/shard_map/pallas_call | solution.py:269
  48.1 0.0 collective-permute-start.8
  48.1 1.4 %collective-permute-start.9 = (bf16[128,512]{1,0:T(8,128)(2,1)}, bf16[128,512]{1,0:T(8,128)(2,1)S(1)}, u32[]{:S(2)}, u32[]{:S(2)}) collective-permute-start(bf16[128,512]{1,0:T(8,128)(2,1)} %get-tuple-element.32), channel_id=1, source_target_pairs={{120,0},{121,1},{122,2},{123,3},{124,4},{125,5},{126,6},{127,7},{0... | collective-permute-start | bytes 393224 | tf_op jit(solution)/shard_map/ppermute | solution.py:272
  49.5 1.0 %collective-permute-start.10 = (bf16[128,512]{1,0:T(8,128)(2,1)}, bf16[128,512]{1,0:T(8,128)(2,1)S(1)}, u32[]{:S(2)}, u32[]{:S(2)}) collective-permute-start(bf16[128,512]{1,0:T(8,128)(2,1)} %get-tuple-element.33), channel_id=1, source_target_pairs={{121,0},{122,1},{123,2},{124,3},{125,4},{126,5},{127,6},{120,7},{1... | collective-permute-start | bytes 393224 | tf_op jit(solution)/shard_map/ppermute | solution.py:272
  50.5 0.0 collective-permute-start.11
  50.5 1.7 %collective-permute-start.12 = (bf16[128,512]{1,0:T(8,128)(2,1)}, bf16[128,512]{1,0:T(8,128)(2,1)S(1)}, u32[]{:S(2)}, u32[]{:S(2)}) collective-permute-start(bf16[128,512]{1,0:T(8,128)(2,1)} %get-tuple-element.35), channel_id=1, source_target_pairs={{1,0},{2,1},{3,2},{4,3},{5,4},{6,5},{7,6},{0,7},{9,8},{10,9},{11,1... | collective-permute-start | bytes 393224 | tf_op jit(solution)/shard_map/ppermute | solution.py:272
  52.2 6.5 %collective-permute-done.8.refs_1_ = bf16[128,512]{1,0:T(8,128)(2,1)S(1)} collective-permute-done((bf16[128,512]{1,0:T(8,128)(2,1)}, bf16[128,512]{1,0:T(8,128)(2,1)S(1)}, u32[]{:S(2)}, u32[]{:S(2)}) %collective-permute-start.8) | collective-permute-done | bytes 131104 | tf_op jit(solution)/shard_map/ppermute | solution.py:272
  58.7 0.6 collective-permute-start.13
  59.3 0.3 collective-permute-done.9.refs_2_
  59.7 2.8 %collective-permute-start.14 = (bf16[128,512]{1,0:T(8,128)(2,1)}, bf16[128,512]{1,0:T(8,128)(2,1)S(1)}, u32[]{:S(2)}, u32[]{:S(2)}) collective-permute-start(bf16[128,512]{1,0:T(8,128)(2,1)} %get-tuple-element.37), channel_id=1, source_target_pairs={{8,0},{9,1},{10,2},{11,3},{12,4},{13,5},{14,6},{15,7},{16,8},{17,9... | collective-permute-start | bytes 393224 | tf_op jit(solution)/shard_map/ppermute | solution.py:272
  62.4 2.1 %collective-permute-done.10.refs_3_ = bf16[128,512]{1,0:T(8,128)(2,1)S(1)} collective-permute-done((bf16[128,512]{1,0:T(8,128)(2,1)}, bf16[128,512]{1,0:T(8,128)(2,1)S(1)}, u32[]{:S(2)}, u32[]{:S(2)}) %collective-permute-start.10) | collective-permute-done | bytes 131104 | tf_op jit(solution)/shard_map/ppermute | solution.py:272
  64.6 1.0 %collective-permute-start.15 = (bf16[128,512]{1,0:T(8,128)(2,1)}, bf16[128,512]{1,0:T(8,128)(2,1)S(1)}, u32[]{:S(2)}, u32[]{:S(2)}) collective-permute-start(bf16[128,512]{1,0:T(8,128)(2,1)} %get-tuple-element.38), channel_id=1, source_target_pairs={{9,0},{10,1},{11,2},{12,3},{13,4},{14,5},{15,6},{8,7},{17,8},{18,9... | collective-permute-start | bytes 393224 | tf_op jit(solution)/shard_map/ppermute | solution.py:272
  65.6 0.0 collective-permute-done.11.refs_4_
  65.6 0.0 collective-permute-done.12.refs_5_
  65.6 0.0 copy-start.4
  65.6 0.0 collective-permute-done.13.refs_6_
  65.6 0.0 copy-start.5
  65.6 1.0 %collective-permute-done.14.refs_7_ = bf16[128,512]{1,0:T(8,128)(2,1)S(1)} collective-permute-done((bf16[128,512]{1,0:T(8,128)(2,1)}, bf16[128,512]{1,0:T(8,128)(2,1)S(1)}, u32[]{:S(2)}, u32[]{:S(2)}) %collective-permute-start.14) | collective-permute-done | bytes 131104 | tf_op jit(solution)/shard_map/ppermute | solution.py:272
  66.6 5.7 %collective-permute-done.15.refs_8_ = bf16[128,512]{1,0:T(8,128)(2,1)S(1)} collective-permute-done((bf16[128,512]{1,0:T(8,128)(2,1)}, bf16[128,512]{1,0:T(8,128)(2,1)S(1)}, u32[]{:S(2)}, u32[]{:S(2)}) %collective-permute-start.15) | collective-permute-done | bytes 131104 | tf_op jit(solution)/shard_map/ppermute | solution.py:272
  72.3 0.0 copy-done.2
  72.4 0.6 copy-done.7
  73.0 13.3 %shard_map.76 = bf16[64,32768]{1,0:T(8,128)(2,1)} custom-call(s32[256]{0:T(256)} %and_select_fusion.1.win_ref, s32[256]{0:T(256)} %off_ref.5, bf16[64,32768]{1,0:T(8,128)(2,1)} %bitcast.8, s32[256,128]{1,0:T(8,128)} %bitcast.12, bf16[8,64,128]{2,1,0:T(8,128)(2,1)} %bitcast.13, bf16[128,4096]{1,0:T(8,128)(2,1)} %get-tuple-element.30.refs_0_, ...), custom_call_target="tpu_custom_call" | custom-call | flops 1610612736 | bytes 10616832 | tf_op jit(solution)/shard_map/pallas_call | solution.py:300
  (21 shorter events, 0.1 us)
Async XLA Ops:
  0.0 22.8 %copy-start.8 = (s32[1,8192]{1,0:T(1,128)S(1)}, s32[1,8192]{1,0:T(1,128)}, u32[]{:S(2)}) copy-start(s32[1,8192]{1,0:T(1,128)} %param.10) | copy-start | bytes 98308
  1.8 1.4 %copy-start.17 = (s32[4]{0:T(128)}, s32[4]{0:T(128)S(1)}, u32[]{:S(2)}) copy-start(s32[4]{0:T(128)S(1)} %convert_reduce_fusion.count_ref) | copy-start | bytes 52
  14.4 8.5 %collective-permute-start = (bf16[512,128]{1,0:T(8,128)(2,1)}, bf16[512,128]{1,0:T(8,128)(2,1)S(1)}, u32[]{:S(2)}, u32[]{:S(2)}) collective-permute-start(bf16[512,128]{1,0:T(8,128)(2,1)} %get-tuple-element.22), channel_id=1, source_target_pairs={{0,127},{1,120},{2,121},{3,122},{4,123},{5,124},{6,125},{7,126},{8... | collective-permute-start | bytes 393224 | tf_op jit(solution)/shard_map/ppermute | solution.py:246
  18.3 7.1 %collective-permute-start.1 = (bf16[512,128]{1,0:T(8,128)(2,1)}, bf16[512,128]{1,0:T(8,128)(2,1)S(1)}, u32[]{:S(2)}, u32[]{:S(2)}) collective-permute-start(bf16[512,128]{1,0:T(8,128)(2,1)} %get-tuple-element.23), channel_id=1, source_target_pairs={{0,120},{1,121},{2,122},{3,123},{4,124},{5,125},{6,126},{7,127},{8... | collective-permute-start | bytes 393224 | tf_op jit(solution)/shard_map/ppermute | solution.py:246
  19.8 8.2 %collective-permute-start.2 = (bf16[512,128]{1,0:T(8,128)(2,1)}, bf16[512,128]{1,0:T(8,128)(2,1)S(1)}, u32[]{:S(2)}, u32[]{:S(2)}) collective-permute-start(bf16[512,128]{1,0:T(8,128)(2,1)} %get-tuple-element.24), channel_id=1, source_target_pairs={{0,121},{1,122},{2,123},{3,124},{4,125},{5,126},{6,127},{7,120},{8... | collective-permute-start | bytes 393224 | tf_op jit(solution)/shard_map/ppermute | solution.py:246
  20.8 16.5 %collective-permute-start.3 = (bf16[512,128]{1,0:T(8,128)(2,1)}, bf16[512,128]{1,0:T(8,128)(2,1)S(1)}, u32[]{:S(2)}, u32[]{:S(2)}) collective-permute-start(bf16[512,128]{1,0:T(8,128)(2,1)} %get-tuple-element.25), channel_id=1, source_target_pairs={{0,7},{1,0},{2,1},{3,2},{4,3},{5,4},{6,5},{7,6},{8,15},{9,8},{10,9... | collective-permute-start | bytes 393224 | tf_op jit(solution)/shard_map/ppermute | solution.py:246
  22.8 14.4 %collective-permute-start.4 = (bf16[512,128]{1,0:T(8,128)(2,1)}, bf16[512,128]{1,0:T(8,128)(2,1)S(1)}, u32[]{:S(2)}, u32[]{:S(2)}) collective-permute-start(bf16[512,128]{1,0:T(8,128)(2,1)} %get-tuple-element.26), channel_id=1, source_target_pairs={{0,1},{1,2},{2,3},{3,4},{4,5},{5,6},{6,7},{7,0},{8,9},{9,10},{10,1... | collective-permute-start | bytes 393224 | tf_op jit(solution)/shard_map/ppermute | solution.py:246
  22.9 17.8 %copy-start.9 = (bf16[512,128]{1,0:T(8,128)(2,1)}, bf16[512,128]{1,0:T(8,128)(2,1)S(1)}, u32[]{:S(2)}) copy-start(bf16[512,128]{1,0:T(8,128)(2,1)S(1)} %collective-permute-done.refs_1_) | copy-start | bytes 393220
  22.9 14.3 %collective-permute-start.5 = (bf16[512,128]{1,0:T(8,128)(2,1)}, bf16[512,128]{1,0:T(8,128)(2,1)S(1)}, u32[]{:S(2)}, u32[]{:S(2)}) collective-permute-start(bf16[512,128]{1,0:T(8,128)(2,1)} %get-tuple-element.27), channel_id=1, source_target_pairs={{0,15},{1,8},{2,9},{3,10},{4,11},{5,12},{6,13},{7,14},{8,23},{9,16... | collective-permute-start | bytes 393224 | tf_op jit(solution)/shard_map/ppermute | solution.py:246
  25.4 15.3 %copy-start.10 = (bf16[512,128]{1,0:T(8,128)(2,1)}, bf16[512,128]{1,0:T(8,128)(2,1)S(1)}, u32[]{:S(2)}) copy-start(bf16[512,128]{1,0:T(8,128)(2,1)S(1)} %collective-permute-done.1.refs_2_) | copy-start | bytes 393220
  25.4 13.2 %collective-permute-start.6 = (bf16[512,128]{1,0:T(8,128)(2,1)}, bf16[512,128]{1,0:T(8,128)(2,1)S(1)}, u32[]{:S(2)}, u32[]{:S(2)}) collective-permute-start(bf16[512,128]{1,0:T(8,128)(2,1)} %get-tuple-element.28), channel_id=1, source_target_pairs={{0,8},{1,9},{2,10},{3,11},{4,12},{5,13},{6,14},{7,15},{8,16},{9,17... | collective-permute-start | bytes 393224 | tf_op jit(solution)/shard_map/ppermute | solution.py:246
  28.0 12.7 %copy-start.11 = (bf16[512,128]{1,0:T(8,128)(2,1)}, bf16[512,128]{1,0:T(8,128)(2,1)S(1)}, u32[]{:S(2)}) copy-start(bf16[512,128]{1,0:T(8,128)(2,1)S(1)} %collective-permute-done.2.refs_3_) | copy-start | bytes 393220
  28.0 12.7 %collective-permute-start.7 = (bf16[512,128]{1,0:T(8,128)(2,1)}, bf16[512,128]{1,0:T(8,128)(2,1)S(1)}, u32[]{:S(2)}, u32[]{:S(2)}) collective-permute-start(bf16[512,128]{1,0:T(8,128)(2,1)} %get-tuple-element.29), channel_id=1, source_target_pairs={{0,9},{1,10},{2,11},{3,12},{4,13},{5,14},{6,15},{7,8},{8,17},{9,18... | collective-permute-start | bytes 393224 | tf_op jit(solution)/shard_map/ppermute | solution.py:246
  37.2 3.5 %copy-start.12 = (bf16[512,128]{1,0:T(8,128)(2,1)}, bf16[512,128]{1,0:T(8,128)(2,1)S(1)}, u32[]{:S(2)}) copy-start(bf16[512,128]{1,0:T(8,128)(2,1)S(1)} %collective-permute-done.3.refs_4_) | copy-start | bytes 393220
  37.2 3.5 %copy-start.13 = (bf16[512,128]{1,0:T(8,128)(2,1)}, bf16[512,128]{1,0:T(8,128)(2,1)S(1)}, u32[]{:S(2)}) copy-start(bf16[512,128]{1,0:T(8,128)(2,1)S(1)} %collective-permute-done.4.refs_5_) | copy-start | bytes 393220
  37.3 3.5 %copy-start.14 = (bf16[512,128]{1,0:T(8,128)(2,1)}, bf16[512,128]{1,0:T(8,128)(2,1)S(1)}, u32[]{:S(2)}) copy-start(bf16[512,128]{1,0:T(8,128)(2,1)S(1)} %collective-permute-done.5.refs_6_) | copy-start | bytes 393220
  38.6 2.1 %copy-start.15 = (bf16[512,128]{1,0:T(8,128)(2,1)}, bf16[512,128]{1,0:T(8,128)(2,1)S(1)}, u32[]{:S(2)}) copy-start(bf16[512,128]{1,0:T(8,128)(2,1)S(1)} %collective-permute-done.6.refs_7_) | copy-start | bytes 393220
  40.7 0.6 copy-start.16
  48.1 10.6 %collective-permute-start.8 = (bf16[128,512]{1,0:T(8,128)(2,1)}, bf16[128,512]{1,0:T(8,128)(2,1)S(1)}, u32[]{:S(2)}, u32[]{:S(2)}) collective-permute-start(bf16[128,512]{1,0:T(8,128)(2,1)} %get-tuple-element.31), channel_id=1, source_target_pairs={{127,0},{120,1},{121,2},{122,3},{123,4},{124,5},{125,6},{126,7},{7... | collective-permute-start | bytes 393224 | tf_op jit(solution)/shard_map/ppermute | solution.py:272
  48.1 11.5 %collective-permute-start.9 = (bf16[128,512]{1,0:T(8,128)(2,1)}, bf16[128,512]{1,0:T(8,128)(2,1)S(1)}, u32[]{:S(2)}, u32[]{:S(2)}) collective-permute-start(bf16[128,512]{1,0:T(8,128)(2,1)} %get-tuple-element.32), channel_id=1, source_target_pairs={{120,0},{121,1},{122,2},{123,3},{124,4},{125,5},{126,6},{127,7},{0... | collective-permute-start | bytes 393224 | tf_op jit(solution)/shard_map/ppermute | solution.py:272
  49.5 15.1 %collective-permute-start.10 = (bf16[128,512]{1,0:T(8,128)(2,1)}, bf16[128,512]{1,0:T(8,128)(2,1)S(1)}, u32[]{:S(2)}, u32[]{:S(2)}) collective-permute-start(bf16[128,512]{1,0:T(8,128)(2,1)} %get-tuple-element.33), channel_id=1, source_target_pairs={{121,0},{122,1},{123,2},{124,3},{125,4},{126,5},{127,6},{120,7},{1... | collective-permute-start | bytes 393224 | tf_op jit(solution)/shard_map/ppermute | solution.py:272
  50.5 15.1 %collective-permute-start.11 = (bf16[128,512]{1,0:T(8,128)(2,1)}, bf16[128,512]{1,0:T(8,128)(2,1)S(1)}, u32[]{:S(2)}, u32[]{:S(2)}) collective-permute-start(bf16[128,512]{1,0:T(8,128)(2,1)} %get-tuple-element.34), channel_id=1, source_target_pairs={{7,0},{0,1},{1,2},{2,3},{3,4},{4,5},{5,6},{6,7},{15,8},{8,9},{9,10... | collective-permute-start | bytes 393224 | tf_op jit(solution)/shard_map/ppermute | solution.py:272
  50.5 15.1 %collective-permute-start.12 = (bf16[128,512]{1,0:T(8,128)(2,1)}, bf16[128,512]{1,0:T(8,128)(2,1)S(1)}, u32[]{:S(2)}, u32[]{:S(2)}) collective-permute-start(bf16[128,512]{1,0:T(8,128)(2,1)} %get-tuple-element.35), channel_id=1, source_target_pairs={{1,0},{2,1},{3,2},{4,3},{5,4},{6,5},{7,6},{0,7},{9,8},{10,9},{11,1... | collective-permute-start | bytes 393224 | tf_op jit(solution)/shard_map/ppermute | solution.py:272
  58.7 13.6 %copy-start = (bf16[128,512]{1,0:T(8,128)(2,1)}, bf16[128,512]{1,0:T(8,128)(2,1)S(1)}, u32[]{:S(2)}) copy-start(bf16[128,512]{1,0:T(8,128)(2,1)S(1)} %collective-permute-done.8.refs_1_) | copy-start | bytes 393220
  58.7 6.9 %collective-permute-start.13 = (bf16[128,512]{1,0:T(8,128)(2,1)}, bf16[128,512]{1,0:T(8,128)(2,1)S(1)}, u32[]{:S(2)}, u32[]{:S(2)}) collective-permute-start(bf16[128,512]{1,0:T(8,128)(2,1)} %get-tuple-element.36), channel_id=1, source_target_pairs={{15,0},{8,1},{9,2},{10,3},{11,4},{12,5},{13,6},{14,7},{23,8},{16,9... | collective-permute-start | bytes 393224 | tf_op jit(solution)/shard_map/ppermute | solution.py:272
  59.7 12.6 %copy-start.1 = (bf16[128,512]{1,0:T(8,128)(2,1)}, bf16[128,512]{1,0:T(8,128)(2,1)S(1)}, u32[]{:S(2)}) copy-start(bf16[128,512]{1,0:T(8,128)(2,1)S(1)} %collective-permute-done.9.refs_2_) | copy-start | bytes 393220
  59.7 7.0 %collective-permute-start.14 = (bf16[128,512]{1,0:T(8,128)(2,1)}, bf16[128,512]{1,0:T(8,128)(2,1)S(1)}, u32[]{:S(2)}, u32[]{:S(2)}) collective-permute-start(bf16[128,512]{1,0:T(8,128)(2,1)} %get-tuple-element.37), channel_id=1, source_target_pairs={{8,0},{9,1},{10,2},{11,3},{12,4},{13,5},{14,6},{15,7},{16,8},{17,9... | collective-permute-start | bytes 393224 | tf_op jit(solution)/shard_map/ppermute | solution.py:272
  64.6 7.7 %copy-start.2 = (bf16[128,512]{1,0:T(8,128)(2,1)}, bf16[128,512]{1,0:T(8,128)(2,1)S(1)}, u32[]{:S(2)}) copy-start(bf16[128,512]{1,0:T(8,128)(2,1)S(1)} %collective-permute-done.10.refs_3_) | copy-start | bytes 393220
  64.6 7.7 %collective-permute-start.15 = (bf16[128,512]{1,0:T(8,128)(2,1)}, bf16[128,512]{1,0:T(8,128)(2,1)S(1)}, u32[]{:S(2)}, u32[]{:S(2)}) collective-permute-start(bf16[128,512]{1,0:T(8,128)(2,1)} %get-tuple-element.38), channel_id=1, source_target_pairs={{9,0},{10,1},{11,2},{12,3},{13,4},{14,5},{15,6},{8,7},{17,8},{18,9... | collective-permute-start | bytes 393224 | tf_op jit(solution)/shard_map/ppermute | solution.py:272
  65.6 6.8 %copy-start.3 = (bf16[128,512]{1,0:T(8,128)(2,1)}, bf16[128,512]{1,0:T(8,128)(2,1)S(1)}, u32[]{:S(2)}) copy-start(bf16[128,512]{1,0:T(8,128)(2,1)S(1)} %collective-permute-done.11.refs_4_) | copy-start | bytes 393220
  65.6 6.8 %copy-start.4 = (bf16[128,512]{1,0:T(8,128)(2,1)}, bf16[128,512]{1,0:T(8,128)(2,1)S(1)}, u32[]{:S(2)}) copy-start(bf16[128,512]{1,0:T(8,128)(2,1)S(1)} %collective-permute-done.12.refs_5_) | copy-start | bytes 393220
  65.6 6.8 %copy-start.5 = (bf16[128,512]{1,0:T(8,128)(2,1)}, bf16[128,512]{1,0:T(8,128)(2,1)S(1)}, u32[]{:S(2)}) copy-start(bf16[128,512]{1,0:T(8,128)(2,1)S(1)} %collective-permute-done.13.refs_6_) | copy-start | bytes 393220
  66.6 5.7 %copy-start.6 = (bf16[128,512]{1,0:T(8,128)(2,1)}, bf16[128,512]{1,0:T(8,128)(2,1)S(1)}, u32[]{:S(2)}) copy-start(bf16[128,512]{1,0:T(8,128)(2,1)S(1)} %collective-permute-done.14.refs_7_) | copy-start | bytes 393220
  72.3 0.7 copy-start.7
